TPU v7x, 128 devices: a whole 4x4x4 slice. The times are simulated.
128 devices in a mesh: req: 8 (over z, core), exp: 16 (over x, y).
Axes of the slice: x: 4, y: 4, z: 4, core: 2. Of those that a mesh axis runs over, the one named last changes fastest.
Arguments:
- tokens: bfloat16 [32768, 1536], P(('req', 'exp')), may hold values from -6 to 6
- attn_gain: float32 [1536], replicated, may hold values from 0.1 to 1.9
- w_query: bfloat16 [1536, 1536], P('req'), may hold values from -0.15625 to 0.15625
- key_projection: bfloat16 [1536, 256], P('req'), may hold values from -0.15625 to 0.15625
- value_projection: bfloat16 [1536, 256], P('req'), may hold values from -0.15625 to 0.15625
- w_out: bfloat16 [1536, 1536], P(None, 'req'), may hold values from -0.15625 to 0.15625
- moe_gain: float32 [1536], replicated, may hold values from 0.1 to 1.9
- w_gate: bfloat16 [32, 1536, 768], P('exp'), may hold values from -0.15625 to 0.15625
- w_up: bfloat16 [32, 1536, 768], P('exp'), may hold values from -0.15625 to 0.15625
- w_down: bfloat16 [32, 768, 1536], P('exp'), may hold values from -0.21875 to 0.21875
- routes: int32 [32768, 4], P(('req', 'exp')), may hold values from 0 to 31, all different within a row; in each aligned block of 128 rows (0 to 127, 128 to 255, ...) at most 24 rows name the same one
- gate_weights: float32 [32768, 4], P(('req', 'exp')), may hold values from 0.1 to 1
- kv_cache: bfloat16 [512, 1024, 512], P(('req', 'exp')), may hold values from -360 to 360, as said below
- lengths: int32 [512], P(('req', 'exp')), may hold values from 128 to 1024, as said below
- parents: int32 [512, 64], P(('req', 'exp')), may hold values from 0 to 62, as said below
- accepted: int32 [512], P(('req', 'exp')), may hold values from 0 to 63
Outputs:
- layer_out: bfloat16 [32768, 1536], P(('req', 'exp'))
- new_entries: bfloat16 [512, 64, 512], P(('req', 'exp'))
Inputs may be any that keep to these rules, and one draw needn't show every extreme that they name: `routes`: each row names 4 different experts; among the rows of one aligned block of 128 rows no expert is named more than 24 times, and in some block one expert exactly 24 times. `kv_cache`: cache entries are finite; slots at or after a request's length hold arbitrary values. `lengths`: some request has exactly 1024 live slots. parents[r, 0] = 0 marks the root; for i >= 1, parents[r, i] < i.
All inputs are finite; a program needn't handle non-finite values.
Results may differ from a plain program's by a relative error of at most 0.013.
The roundings to bfloat16 on the way count: a program that leaves them out, or rounds other values in their place, can miss the bound.
Values may be sent and summed in bfloat16 or wider, within the bound.
No kernel may reach another device: no remote copies, remote signals or barrier semaphores. Data moves between devices by JAX's collectives and lax.ppermute only.
A program may use at most 128 MiB of HBM per device.

v0:
```python
import math

import jax
import jax.numpy as jnp
from jax import lax
from jax.sharding import PartitionSpec as P

QUERY_HEADS = 12
KEY_VALUE_HEADS = 2
HEAD_SIZE = 128
EXPERTS = 32
TOP = 4
DRAFT_TOKENS = 64
CAP = 24


eps_norm = 1e-06
rope_base = 1000000.0


def rms_scale(token_rows, gain_vec):
    widened = token_rows.astype(jnp.float32)
    inverse = lax.rsqrt(jnp.mean(widened * widened, axis=-1, keepdims=True) + eps_norm)
    return (widened * inverse * gain_vec).astype(jnp.bfloat16)


def rotate(values, positions):
    row_count = values.shape[0]
    head_count = values.shape[1] // HEAD_SIZE
    half_size = HEAD_SIZE // 2
    reshaped_rows = values.reshape(row_count, head_count, HEAD_SIZE)
    frequency = rope_base ** (-jnp.arange(half_size, dtype=jnp.float32) / half_size)
    angles = positions.astype(jnp.float32)[:, None] * frequency[None, :]
    cosine = jnp.cos(angles)[:, None, :]
    sine_part = jnp.sin(angles)[:, None, :]
    leading = reshaped_rows[..., :half_size]
    second = reshaped_rows[..., half_size:]
    turned = jnp.concatenate(
        [leading * cosine - second * sine_part, second * cosine + leading * sine_part], axis=-1
    )
    return turned.reshape(row_count, head_count * HEAD_SIZE)


def ancestry(parents):
    node_count = parents.shape[-1]
    node_index = jnp.arange(node_count, dtype=jnp.int32)
    parent_step = (parents[..., :, None] == node_index[None, None, :]).astype(jnp.float32)
    closure = jnp.maximum(parent_step, jnp.eye(node_count, dtype=jnp.float32)[None])
    for squaring in range(max(1, (node_count - 1).bit_length())):
        closure = jnp.minimum(jnp.einsum("rij,rjk->rik", closure, closure), 1.0)
    tree_depth = jnp.sum(closure, axis=-1).astype(jnp.int32) - 1
    return (closure, tree_depth)


def attend(query_rows, tree_key_value, cached_row_block, length, closure):
    tree_drafts = query_rows.shape[0]
    queries_per_group = QUERY_HEADS // KEY_VALUE_HEADS
    key_value_width = KEY_VALUE_HEADS * HEAD_SIZE
    reshaped_rows = query_rows.reshape(tree_drafts, KEY_VALUE_HEADS, queries_per_group, HEAD_SIZE)
    cached_key_rows = cached_row_block[:, :key_value_width].reshape(-1, KEY_VALUE_HEADS, HEAD_SIZE)
    cached_value_rows = cached_row_block[:, key_value_width:].reshape(
        -1, KEY_VALUE_HEADS, HEAD_SIZE
    )
    tree_key_rows = tree_key_value[:, :key_value_width].reshape(-1, KEY_VALUE_HEADS, HEAD_SIZE)
    tree_value_rows = tree_key_value[:, key_value_width:].reshape(-1, KEY_VALUE_HEADS, HEAD_SIZE)
    scale = 1.0 / math.sqrt(HEAD_SIZE)
    cache_scores = (
        jnp.einsum(
            "igsd,jgd->gsij", reshaped_rows, cached_key_rows, preferred_element_type=jnp.float32
        )
        * scale
    )
    draft_scores = (
        jnp.einsum(
            "igsd,jgd->gsij", reshaped_rows, tree_key_rows, preferred_element_type=jnp.float32
        )
        * scale
    )
    live_cache = (jnp.arange(cached_row_block.shape[0]) < length)[None, None, None, :]
    live_draft = (closure > 0.5)[None, None, :, :]
    cache_scores = jnp.where(live_cache, cache_scores, -1e30)
    draft_scores = jnp.where(live_draft, draft_scores, -1e30)
    highest = jnp.maximum(jnp.max(cache_scores, axis=-1), jnp.max(draft_scores, axis=-1))[..., None]
    cache_weight = jnp.exp(cache_scores - highest)
    draft_weight = jnp.exp(draft_scores - highest)
    running = jnp.sum(cache_weight, axis=-1, keepdims=True) + jnp.sum(
        draft_weight, axis=-1, keepdims=True
    )
    cache_probs = (cache_weight / running).astype(jnp.bfloat16)
    draft_probs = (draft_weight / running).astype(jnp.bfloat16)
    context = jnp.einsum(
        "gsij,jgd->igsd", cache_probs, cached_value_rows, preferred_element_type=jnp.float32
    )
    context = context + jnp.einsum(
        "gsij,jgd->igsd", draft_probs, tree_value_rows, preferred_element_type=jnp.float32
    )
    return context.reshape(tree_drafts, QUERY_HEADS * HEAD_SIZE).astype(jnp.bfloat16)


def compact(kv_rows, closure, tree_depth, accepted):
    path_mask = jnp.take_along_axis(closure, accepted[:, None, None], axis=1)[:, 0, :]
    level = jnp.arange(kv_rows.shape[1], dtype=jnp.int32)
    select = (
        path_mask[:, None, :] * (tree_depth[:, None, :] == level[None, :, None]).astype(jnp.float32)
    ).astype(jnp.bfloat16)
    return jnp.einsum("rtj,rjw->rtw", select, kv_rows, preferred_element_type=jnp.float32).astype(
        jnp.bfloat16
    )


def pack_slots(token_rows, routes, capacity):
    flat_expert = routes.reshape(-1)
    onehot = (flat_expert[:, None] == jnp.arange(EXPERTS, dtype=jnp.int32)[None, :]).astype(
        jnp.int32
    )
    earlier = jnp.cumsum(onehot, axis=0) - onehot
    slot_number = jnp.sum(earlier * onehot, axis=1)
    owner = jnp.arange(flat_expert.shape[0], dtype=jnp.int32) // TOP
    slot_index = flat_expert * capacity + slot_number
    layer_width = token_rows.shape[1]
    buffer = (
        jnp.zeros((EXPERTS * capacity, layer_width), token_rows.dtype)
        .at[slot_index]
        .set(token_rows[owner])
    )
    return (buffer, slot_index)


def expert_products(received, w_gate, w_up, w_down):
    gate_part = jnp.einsum("pekd,edf->pekf", received, w_gate, preferred_element_type=jnp.float32)
    up_part = jnp.einsum("pekd,edf->pekf", received, w_up, preferred_element_type=jnp.float32)
    hidden = (jnp.maximum(gate_part, 0.0) * up_part).astype(jnp.bfloat16)
    return jnp.einsum("pekf,efd->pekd", hidden, w_down, preferred_element_type=jnp.float32).astype(
        jnp.bfloat16
    )


def combine_picks(returned_rows, slot_index, gate_weights):
    layer_width = returned_rows.shape[-1]
    picked = returned_rows.reshape(-1, layer_width)[slot_index].astype(jnp.float32)
    weighted = picked * gate_weights.reshape(-1)[:, None]
    return jnp.sum(weighted.reshape(-1, TOP, layer_width), axis=1)


def routed_whole(moe_in, routes, gate_weights, w_gate, w_up, w_down):
    capacity = 2 * CAP
    buffer, slot_index = pack_slots(moe_in, routes, capacity)
    peer_count = lax.axis_size("exp")
    reshaped_rows = buffer.reshape(peer_count, w_gate.shape[0], capacity, moe_in.shape[1])
    produced = expert_products(
        lax.all_to_all(reshaped_rows, "exp", split_axis=0, concat_axis=0, tiled=True),
        w_gate,
        w_up,
        w_down,
    )
    returned_rows = lax.all_to_all(produced, "exp", split_axis=0, concat_axis=0, tiled=True)
    return combine_picks(returned_rows, slot_index, gate_weights)


def local(
    tokens,
    attn_gain,
    w_query,
    key_projection,
    value_projection,
    w_out,
    moe_gain,
    w_gate,
    w_up,
    w_down,
    routes,
    gate_weights,
    kv_cache,
    lengths,
    parents,
    accepted,
):
    rows_here = tokens.shape[0]
    local_reqs = kv_cache.shape[0]
    normed = rms_scale(tokens, attn_gain)
    closure, tree_depth = ancestry(parents)
    positions = (lengths[:, None] + tree_depth).reshape(-1)
    query_sum = jnp.dot(
        normed,
        lax.all_gather(w_query, "req", axis=0, tiled=True),
        preferred_element_type=jnp.float32,
    )
    key_sum = jnp.dot(
        normed,
        lax.all_gather(key_projection, "req", axis=0, tiled=True),
        preferred_element_type=jnp.float32,
    )
    value_sum = jnp.dot(
        normed,
        lax.all_gather(value_projection, "req", axis=0, tiled=True),
        preferred_element_type=jnp.float32,
    )
    query_rows = rotate(query_sum, positions).astype(jnp.bfloat16)
    tree_key_value = jnp.concatenate([rotate(key_sum, positions), value_sum], axis=1).astype(
        jnp.bfloat16
    )
    query_req = query_rows.reshape(local_reqs, DRAFT_TOKENS, query_rows.shape[1])
    key_value_request = tree_key_value.reshape(local_reqs, DRAFT_TOKENS, tree_key_value.shape[1])
    context = jax.vmap(attend)(query_req, key_value_request, kv_cache, lengths, closure).reshape(
        rows_here, -1
    )
    attn_out = jnp.dot(
        context,
        lax.all_gather(w_out, "req", axis=1, tiled=True),
        preferred_element_type=jnp.float32,
    )
    residual = (tokens.astype(jnp.float32) + attn_out).astype(jnp.bfloat16)
    moe_in = rms_scale(residual, moe_gain)
    mixed = routed_whole(moe_in, routes, gate_weights, w_gate, w_up, w_down)
    layer_out = (residual.astype(jnp.float32) + mixed).astype(jnp.bfloat16)
    new_entries = compact(key_value_request, closure, tree_depth, accepted)
    return (layer_out, new_entries)


def solution(mesh):
    return jax.shard_map(
        local,
        mesh=mesh,
        in_specs=(
            P(("req", "exp"), None),
            P(),
            P("req", None),
            P("req", None),
            P("req", None),
            P(None, "req"),
            P(),
            P("exp", None, None),
            P("exp", None, None),
            P("exp", None, None),
            P(("req", "exp"), None),
            P(("req", "exp"), None),
            P(("req", "exp"), None, None),
            P(("req", "exp")),
            P(("req", "exp"), None),
            P(("req", "exp")),
        ),
        out_specs=(P(("req", "exp"), None), P(("req", "exp"), None, None)),
        check_vma=False,
    )
```

profile of v0, /device:TPU:0, one launch (start us, length us, event | category | flops | bytes accessed | tf_op | source)
XLA Modules:
  0.0 302.0 jit_solution(12283053572318838056)
XLA Ops:
  14.7 15.8 %all_gather.13 = bf16[1536,256]{1,0:T(8,128)(2,1)S(1)} all-gather(bf16[192,256]{1,0:T(8,128)(2,1)S(1)} %copy-done.16), channel_id=1, replica_groups=mesh['req'=8,'exp'=16] {'req'}, dimensions={0}, use_global_device_ids=true | all-gather | bytes 884736 | tf_op jit(solution)/shard_map/all_gather | solution.py:190
  32.1 4.6 %fusion.76 = (bf16[4,1024,256]{2,1,0:T(8,128)(2,1)}, bf16[4,1024,256]{2,1,0:T(8,128)(2,1)}) fusion(bf16[4,1024,512]{2,1,0:T(8,128)(2,1)} %param.28), kind=kLoop, calls=%fused_computation.124 | loop fusion | bytes 8388608 | tf_op jit(solution)/shard_map/vmap()/slice | solution.py:61
  36.7 3.0 %copy.155 = bf16[4,1024,256]{1,2,0:T(8,128)(2,1)S(1)} copy(bf16[4,1024,256]{2,1,0:T(8,128)(2,1)} %get-tuple-element.3) | data formatting | bytes 4194304
  39.8 15.2 %all_gather.14 = bf16[1536,256]{1,0:T(8,128)(2,1)S(1)} all-gather(bf16[192,256]{1,0:T(8,128)(2,1)S(1)} %copy-done.17), channel_id=1, replica_groups=mesh['req'=8,'exp'=16] {'req'}, dimensions={0}, use_global_device_ids=true | all-gather | bytes 884736 | tf_op jit(solution)/shard_map/all_gather | solution.py:195
  56.2 4.1 %copy.158 = bf16[4,1024,256]{1,2,0:T(8,128)(2,1)} copy(bf16[4,1024,256]{2,1,0:T(8,128)(2,1)} %get-tuple-element.2) | data formatting | bytes 4194304
  60.4 9.0 %reduce-window.6 = s32[32,8,128]{2,1,0:T(8,128)S(1)} reduce-window(s32[32,8,128]{2,1,0:T(8,128)S(1)} %fusion.50, s32[]{:T(128)} %constant.64.clone.1), window={size=1x1x128 pad=0_0x0_0x127_0}, to_apply=%region_6.7 | reduce-window | flops 4161536 | bytes 262148 | tf_op jit(solution)/shard_map/reduce-window
  70.6 4.7 %fusion.74 = f32[256,1536]{0,1:T(8,128)S(1)} fusion(bf16[1536,1536]{1,0:T(8,128)(2,1)} %all-gather.3.cloned.1.call-done, bf16[256,1536]{1,0:T(8,128)(2,1)} %param.16, f32[1536]{0:T(1024)S(1)} %copy-done.23, f32[256]{0:T(256)S(1)} %add_rsqrt_fusion.1), kind=kOutput, calls=%fused_computation.123 | convolution fusion | flops 1209532416 | bytes 7085056 | tf_op jit(solution)/shard_map/dot_general | solution.py:183
  76.5 1.5 copy.110
  78.9 2.1 bitcast_reduce_fusion
  81.4 3.1 %fusion.1 = f32[4,2,6,64]{3,2,1,0:T(8,128)S(1)} fusion(f32[4,2,64,6,1024]{4,2,3,1,0:T(8,128)S(1)} %get-tuple-element.17, f32[4,2,6,64]{3,2,1,0:T(8,128)S(1)} %max.24, pred[4,1024]{1,0:T(4,128)(4,1)S(1)} %iota_compare_fusion.7), kind=kLoop, calls=%fused_computation.9 | loop fusion | flops 12579840 | bytes 12611584 | tf_op jit(solution)/shard_map/vmap()/reduce_sum | solution.py:86
  86.1 4.5 %fusion.32 = bf16[4,64,2,6,128]{4,1,3,2,0:T(8,128)(2,1)S(1)} fusion(f32[4,2,128,6,64]{2,4,3,1,0:T(8,128)S(1)} %fusion.34, bf16[4,1024,2,128,1]{1,3,4,2,0:T(8,128)(2,1)S(1)} %bitcast.108, f32[4,2,64,6,1024]{4,2,3,1,0:T(8,128)S(1)} %get-tuple-element.17, f32[4,2,6,64]{3,2,1,0:T(8,128)S(1)} %add.116, f32[4,2,6,64]{3,2,1,0:T(8,128)S(1)} %max.24, ...), kind=kOutput, calls=%fused_computation.36 | convolution fusion | flops 821821440 | bytes 17068032 | tf_op jit(solution)/shard_map/vmap(gsij,jgd->igsd)/dot_general | solution.py:91
  92.0 3.8 %multiply_reduce_fusion.1 = (f32[256]{0:T(256)S(1)}, f32[256,1536]{1,0:T(8,128)S(1)}) fusion(bf16[256,1536]{1,0:T(8,128)(2,1)S(1)} %convert_element_type.118, bf16[1536,1536]{0,1:T(8,128)(2,1)} %all-gather.5.cloned.1.call-done, bf16[256,1536]{1,0:T(8,128)(2,1)S(1)} %copy-done.5), kind=kOutput, calls=%fused_computation.40 | convolution fusion | flops 1210318592 | bytes 7865344 | tf_op jit(solution)/shard_map/dot_general | solution.py:207
  97.3 19.0 %scatter_custom_fusion = bf16[1536,1536]{1,0:T(8,128)(2,1)} fusion(s32[1024]{0:T(1024)S(1)} %bitcast.117, bf16[256,1536]{1,0:T(8,128)(2,1)S(1)} %multiply_convert_fusion.1, s32[1024]{0:T(1024)S(1)} %broadcast_clamp_fusion.1, bf16[]{:T(256)} %constant.62.clone.1), kind=kCustom, calls=%fused_computation.22 | custom fusion | bytes 4718594 | tf_op jit(solution)/shard_map/scatter | solution.py:124
  116.3 64.2 %all_to_all.10 = bf16[16,2,48,1536]{3,2,1,0:T(8,128)(2,1)S(1)} all-to-all(bf16[16,2,48,1536]{3,2,1,0:T(8,128)(2,1)} %bitcast.104), channel_id=1, replica_groups=mesh['req'=8,'exp'=16] {'exp'}, dimensions={0} | all-to-all | bytes 9437184 | tf_op jit(solution)/shard_map/all_to_all | solution.py:151
  180.5 2.2 copy-done.2
  182.7 5.4 %fusion.5 = f32[2,16,48,768]{3,2,1,0:T(8,128)} fusion(bf16[2,1536,768]{2,1,0:T(8,128)(2,1)S(1)} %bitcast.121, bf16[16,2,48,1536]{3,2,1,0:T(8,128)(2,1)S(1)} %all_to_all.10), kind=kOutput, calls=%fused_computation.14 | convolution fusion | flops 3623878656 | bytes 14155776 | tf_op jit(solution)/shard_map/pekd,edf->pekf/dot_general | solution.py:131
  188.1 14.4 %convert_bitcast_fusion = bf16[16,2,48,1536]{3,2,0,1:T(8,128)(2,1)} fusion(bf16[2,768,1536]{2,1,0:T(8,128)(2,1)} %param.25, f32[2,16,48,768]{3,2,1,0:T(8,128)} %fusion.5, bf16[2,1536,768]{2,1,0:T(8,128)(2,1)} %param.23, bf16[16,2,48,1536]{3,2,1,0:T(8,128)(2,1)} %copy-done.2), kind=kOutput, calls=%fused_computation.18 | convolution fusion | flops 7253655552 | bytes 23592960 | tf_op jit(solution)/shard_map/pekf,efd->pekd/dot_general | solution.py:133
  202.5 4.9 %copy.133 = bf16[16,2,48,1536]{3,2,1,0:T(8,128)(2,1)} copy(bf16[16,2,48,1536]{3,2,0,1:T(8,128)(2,1)} %convert_bitcast_fusion) | data formatting | bytes 9437184 | tf_op jit(solution)/shard_map/convert_element_type | solution.py:133
  207.4 4.9 %all-to-all-start.1 = ((bf16[16,2,48,1536]{3,2,1,0:T(8,128)(2,1)}), bf16[16,2,48,1536]{3,2,1,0:T(8,128)(2,1)}, u32[]{:S(2)}, u32[]{:S(2)}) async-start(bf16[16,2,48,1536]{3,2,1,0:T(8,128)(2,1)} %copy.133), calls=%async_computation.1 | async-start | bytes 9437184 | tf_op jit(solution)/shard_map/all_to_all | solution.py:156
  212.8 1.5 gather_fusion.1
  215.2 57.6 %all-to-all-done.1 = bf16[16,2,48,1536]{3,2,1,0:T(8,128)(2,1)} async-done(((bf16[16,2,48,1536]{3,2,1,0:T(8,128)(2,1)}), bf16[16,2,48,1536]{3,2,1,0:T(8,128)(2,1)}, u32[]{:S(2)}, u32[]{:S(2)}) %all-to-all-start.1) | async-done | bytes 4718624 | tf_op jit(solution)/shard_map/all_to_all | solution.py:156
  272.9 9.6 %gather_fusion = bf16[1024,1536]{1,0:T(8,128)(2,1)S(1)} fusion(bf16[1536,1536]{1,0:T(8,128)(2,1)} %bitcast.28, s32[1024]{0:T(1024)S(1)} %broadcast_clamp_fusion), kind=kCustom, calls=%fused_computation.1 | custom fusion | bytes 6295552 | tf_op jit(solution)/shard_map/gather | solution.py:140
  282.5 3.8 %reshape.310 = f32[256,4,1536]{2,1,0:T(4,128)} reshape(bf16[1024,1536]{1,0:T(8,128)(2,1)S(1)} %gather_fusion) | data formatting | bytes 9437184 | tf_op jit(solution)/shard_map/convert_element_type | solution.py:140
  286.3 7.5 %multiply_reduce_fusion = f32[256,1536]{1,0:T(8,128)S(1)} fusion(f32[256,4,1536]{2,1,0:T(4,128)} %reshape.310, f32[256,4]{1,0:T(8,128)S(1)} %copy.134), kind=kLoop, calls=%fused_computation.10 | loop fusion | flops 2752512 | bytes 7868416 | tf_op jit(solution)/shard_map/reduce_sum | solution.py:142
  (123 shorter events, 20.5 us)
Async XLA Ops:
  7.2 7.3 %copy-start.4 = (bf16[256,1536]{1,0:T(8,128)(2,1)S(1)}, bf16[256,1536]{1,0:T(8,128)(2,1)}, u32[]{:S(2)}) copy-start(bf16[256,1536]{1,0:T(8,128)(2,1)} %param.16) | copy-start | bytes 2359300
  7.2 7.5 %copy-start.16 = (bf16[192,256]{1,0:T(8,128)(2,1)S(1)}, bf16[192,256]{1,0:T(8,128)(2,1)}, u32[]{:S(2)}) copy-start(bf16[192,256]{1,0:T(8,128)(2,1)} %param.19) | copy-start | bytes 294916
  7.2 23.3 %copy-start.22 = (f32[1536]{0:T(1024)S(1)}, f32[1536]{0:T(1024)}, u32[]{:S(2)}) copy-start(f32[1536]{0:T(1024)} %param.17) | copy-start | bytes 18436
  7.2 63.4 %all-gather.3.cloned.1.call-start = ((), (), s32[]{:S(2)}) async-start(), calls=%async_computation.2 | async-start | bytes 5308416 | tf_op jit(solution)/shard_map/all_gather | solution.py:185
  7.9 84.1 %all-gather.5.cloned.1.call-start = ((), (), s32[]{:S(2)}) async-start(), calls=%async_computation.3 | async-start | bytes 5308416 | tf_op jit(solution)/shard_map/all_gather | solution.py:209
  12.9 23.8 %copy-start.6 = (f32[256,64]{0,1:T(8,128)}, f32[256,64]{0,1:T(8,128)S(1)}, u32[]{:S(2)}) copy-start(f32[256,64]{0,1:T(8,128)S(1)} %get-tuple-element.12) | copy-start | bytes 196612
  12.9 23.8 %copy-start.8 = (f32[256,64]{0,1:T(8,128)}, f32[256,64]{0,1:T(8,128)S(1)}, u32[]{:S(2)}) copy-start(f32[256,64]{0,1:T(8,128)S(1)} %get-tuple-element.13) | copy-start | bytes 196612
  36.7 3.0 %copy-start.17 = (bf16[192,256]{1,0:T(8,128)(2,1)S(1)}, bf16[192,256]{1,0:T(8,128)(2,1)}, u32[]{:S(2)}) copy-start(bf16[192,256]{1,0:T(8,128)(2,1)} %param.20) | copy-start | bytes 294916
  56.1 4.2 %copy-start.14 = (bf16[256,256]{1,0:T(8,128)(2,1)}, bf16[256,256]{1,0:T(8,128)(2,1)S(1)}, u32[]{:S(2)}) copy-start(bf16[256,256]{1,0:T(8,128)(2,1)S(1)} %convolution_convert_fusion.1) | copy-start | bytes 393220
  56.1 13.6 %copy-start.18 = (s32[256,4]{0,1:T(4,128)S(1)}, s32[256,4]{0,1:T(4,128)}, u32[]{:S(2)}) copy-start(s32[256,4]{0,1:T(4,128)} %param.26) | copy-start | bytes 12292
  56.1 13.9 %copy-start.10 = (f32[256,64]{1,0:T(8,128)S(1)}, f32[256,64]{1,0:T(8,128)}, u32[]{:S(2)}) copy-start(f32[256,64]{1,0:T(8,128)} %copy.116) | copy-start | bytes 196612
  56.2 13.9 %copy-start.11 = (f32[256,64]{1,0:T(8,128)S(1)}, f32[256,64]{1,0:T(8,128)}, u32[]{:S(2)}) copy-start(f32[256,64]{1,0:T(8,128)} %copy.118) | copy-start | bytes 196612
  56.2 14.2 %copy-start.21 = (s32[4]{0:T(128)S(1)}, s32[4]{0:T(128)}, u32[]{:S(2)}) copy-start(s32[4]{0:T(128)} %param.29) | copy-start | bytes 52
  56.2 14.3 %copy-start.23 = (f32[1536]{0:T(1024)S(1)}, f32[1536]{0:T(1024)}, u32[]{:S(2)}) copy-start(f32[1536]{0:T(1024)} %param.17) | copy-start | bytes 18436
  70.5 4.8 %copy-start.7 = (f32[256,64]{0,1:T(8,128)S(1)}, f32[256,64]{0,1:T(8,128)}, u32[]{:S(2)}) copy-start(f32[256,64]{0,1:T(8,128)} %copy-done.6) | copy-start | bytes 196612
  70.5 4.8 %copy-start.9 = (f32[256,64]{0,1:T(8,128)S(1)}, f32[256,64]{0,1:T(8,128)}, u32[]{:S(2)}) copy-start(f32[256,64]{0,1:T(8,128)} %copy-done.8) | copy-start | bytes 196612
  92.0 5.0 %copy-start.19 = (f32[1536]{0:T(1024)S(1)}, f32[1536]{0:T(1024)}, u32[]{:S(2)}) copy-start(f32[1536]{0:T(1024)} %param.22) | copy-start | bytes 18436
  97.2 85.4 %slice-start = ((s8[4718592]{0:T(1024)(128)(4,1)}), s8[524288]{0:T(1024)(128)(4,1)S(1)}, s32[]{:S(2)}) async-start(s8[4718592]{0:T(1024)(128)(4,1)} %bitcast.120), calls=%async_computation.4 | async-start | bytes 1048576
  116.3 66.4 %slice-start.1 = ((s8[4718592]{0:T(1024)(128)(4,1)}), s8[4194304]{0:T(1024)(128)(4,1)S(1)}, s32[]{:S(2)}) async-start(s8[4718592]{0:T(1024)(128)(4,1)} %bitcast.120), calls=%async_computation.5 | async-start | bytes 8388608
  207.4 5.1 %copy-start.20 = (f32[256,4]{0,1:T(4,128)S(1)}, f32[256,4]{0,1:T(4,128)}, u32[]{:S(2)}) copy-start(f32[256,4]{0,1:T(4,128)} %param.27) | copy-start | bytes 12292
  207.4 5.3 %copy-start.24 = (s32[4]{0:T(128)S(1)}, s32[4]{0:T(128)}, u32[]{:S(2)}) copy-start(s32[4]{0:T(128)} %param.31) | copy-start | bytes 52
  207.4 7.0 %copy-start.15 = (bf16[256,256]{1,0:T(8,128)(2,1)S(1)}, bf16[256,256]{1,0:T(8,128)(2,1)}, u32[]{:S(2)}) copy-start(bf16[256,256]{1,0:T(8,128)(2,1)} %copy-done.14) | copy-start | bytes 393220
  207.4 65.5 %all-to-all-start.1 = ((bf16[16,2,48,1536]{3,2,1,0:T(8,128)(2,1)}), bf16[16,2,48,1536]{3,2,1,0:T(8,128)(2,1)}, u32[]{:S(2)}, u32[]{:S(2)}) async-start(bf16[16,2,48,1536]{3,2,1,0:T(8,128)(2,1)} %copy.133), calls=%async_computation.1 | async-start | bytes 9437184 | tf_op jit(solution)/shard_map/all_to_all | solution.py:156
  286.3 7.5 %copy-start.1 = (f32[256,1536]{1,0:T(8,128)S(1)}, f32[256,1536]{1,0:T(8,128)}, u32[]{:S(2)}) copy-start(f32[256,1536]{1,0:T(8,128)} %copy-done) | copy-start | bytes 4718596
  (6 other events, 10.0 us)
Sparse Core Ops, SparseCore 0:
  9.7 39.4 all-gather.2
  50.8 34.0 all-gather.4
where the time goes:
time: 306 us; the launch traced here: 302 us
  blocking collectives  95.2 us (31%)
  local copies, waits for them, and re-layouts  62.7 us (20%)
  waiting for transfers between devices  59.1 us (19%)
  matrix products  40.7 us (13%)
  other arithmetic  24.4 us (8%)
  between operations  14.9 us (5%)
  starting transfers between devices  5.01 us (2%)
    all_to_all x1, blocking collectives, routed_whole(): lax.all_to_all(reshaped_rows, 'exp', split_axis=0, concat_axis=0, tiled=T...  64.2 us
    all_to_all x1, waiting for transfers between devices, routed_whole(): lax.all_to_all(produced, 'exp', split_axis=0, concat_axis=0, tiled=True)  57.6 us
    scatter x1, local copies, waits for them, and re-layouts, pack_slots(): buffer = jnp.zeros((EXPERTS * capacity, layer_width), token_rows.dtype).a...  19 us
    all_gather x1, blocking collectives, local(): lax.all_gather(key_projection, 'req', axis=0, tiled=True)  15.8 us
    all_gather x1, blocking collectives, local(): lax.all_gather(value_projection, 'req', axis=0, tiled=True)  15.2 us
    dot_general x1, matrix products, expert_products(): jnp.einsum('pekf,efd->pekd', hidden, w_down, preferred_element_type=jnp.f...  14.4 us
    unnamed x61, local copies, waits for them, and re-layouts  12.9 us
    gather x1, local copies, waits for them, and re-layouts, combine_picks(): returned_rows.reshape(-1, layer_width)[slot_index].astype(jnp.float32)  9.6 us
  transfers between devices with their start and end apart: 3, of which 1 were waited for; matrix products, arithmetic and copies ran while one was open for 18% of the time, Pallas kernels for 0%

commit v1 on v0

--- a/solution.py
+++ b/solution.py
@@ -108,22 +108,24 @@
     )
 
 
-def pack_slots(token_rows, routes, capacity):
-    flat_expert = routes.reshape(-1)
-    onehot = (flat_expert[:, None] == jnp.arange(EXPERTS, dtype=jnp.int32)[None, :]).astype(
-        jnp.int32
-    )
-    earlier = jnp.cumsum(onehot, axis=0) - onehot
-    slot_number = jnp.sum(earlier * onehot, axis=1)
-    owner = jnp.arange(flat_expert.shape[0], dtype=jnp.int32) // TOP
-    slot_index = flat_expert * capacity + slot_number
-    layer_width = token_rows.shape[1]
-    buffer = (
-        jnp.zeros((EXPERTS * capacity, layer_width), token_rows.dtype)
-        .at[slot_index]
-        .set(token_rows[owner])
-    )
-    return (buffer, slot_index)
+def slot_tables(routes, capacity):
+    rows = routes.shape[0]
+    expert_ids = jnp.arange(EXPERTS, dtype=jnp.int32)
+    picks = routes[:, :, None] == expert_ids[None, None, :]
+    chosen = jnp.sum(picks.astype(jnp.int32), axis=1).astype(jnp.bfloat16)
+    row_ids = jnp.arange(rows, dtype=jnp.int32)
+    before = (row_ids[None, :] < row_ids[:, None]).astype(jnp.bfloat16)
+    earlier = jnp.dot(before, chosen, preferred_element_type=jnp.float32).astype(jnp.int32)
+    slot_number = jnp.sum(jnp.where(picks, earlier[:, None, :], 0), axis=2)
+    slot_index = routes * capacity + slot_number
+    slot_ids = jnp.arange(EXPERTS * capacity, dtype=jnp.int32)
+    hit = slot_index[:, :, None] == slot_ids[None, None, :]
+    return hit
+
+
+def pack_slots(token_rows, hit):
+    place = jnp.sum(hit.astype(jnp.bfloat16), axis=1)
+    return jnp.einsum("ts,td->sd", place, token_rows, preferred_element_type=jnp.bfloat16)
 
 
 def expert_products(received, w_gate, w_up, w_down):
@@ -135,16 +137,20 @@
     )
 
 
-def combine_picks(returned_rows, slot_index, gate_weights):
+def combine_picks(returned_rows, hit, gate_weights):
     layer_width = returned_rows.shape[-1]
-    picked = returned_rows.reshape(-1, layer_width)[slot_index].astype(jnp.float32)
-    weighted = picked * gate_weights.reshape(-1)[:, None]
-    return jnp.sum(weighted.reshape(-1, TOP, layer_width), axis=1)
+    flat_rows = returned_rows.reshape(-1, layer_width)
+    weight = jnp.sum(jnp.where(hit, gate_weights[:, :, None], 0.0), axis=1)
+    weight_hi = weight.astype(jnp.bfloat16)
+    weight_lo = (weight - weight_hi.astype(jnp.float32)).astype(jnp.bfloat16)
+    mixed = jnp.dot(weight_hi, flat_rows, preferred_element_type=jnp.float32)
+    return mixed + jnp.dot(weight_lo, flat_rows, preferred_element_type=jnp.float32)
 
 
 def routed_whole(moe_in, routes, gate_weights, w_gate, w_up, w_down):
     capacity = 2 * CAP
-    buffer, slot_index = pack_slots(moe_in, routes, capacity)
+    hit = slot_tables(routes, capacity)
+    buffer = pack_slots(moe_in, hit)
     peer_count = lax.axis_size("exp")
     reshaped_rows = buffer.reshape(peer_count, w_gate.shape[0], capacity, moe_in.shape[1])
     produced = expert_products(
@@ -154,7 +160,7 @@
         w_down,
     )
     returned_rows = lax.all_to_all(produced, "exp", split_axis=0, concat_axis=0, tiled=True)
-    return combine_picks(returned_rows, slot_index, gate_weights)
+    return combine_picks(returned_rows, hit, gate_weights)
 
 
 def local(

time: 306 us -> 265 us (0.87); the launches traced: 302 us -> 264 us
  local copies, waits for them, and re-layouts: 62.7 us -> 30.7 us
  other arithmetic: 24.4 us -> 9.41 us
  matrix products: 40.7 us -> 51.6 us
    scatter x1 -> x0, local copies, waits for them, and re-layouts: 19 us -> none  [pack_slots(): buffer = jnp.zeros((EXPERTS * capacity, layer_width), token_rows.dtype).a...]
    dot_general x0 -> x4, matrix products: none -> 10 us  [the longest x1 4.67 us: combine_picks(): jnp.dot(weight_lo, flat_rows, preferred_element_type=jnp.float32)]
    gather x1 -> x0, local copies, waits for them, and re-layouts: 9.6 us -> none  [combine_picks(): returned_rows.reshape(-1, layer_width)[slot_index].astype(jnp.float32)]
    another operation x5 -> x2, other arithmetic: 9.44 us -> 1.27 us
    reduce_sum x2 -> x4, other arithmetic: 7.55 us -> 2 us  [the longest x1 1.03 us: combine_picks(): weight = jnp.sum(jnp.where(hit, gate_weights[:, :, None], 0.0), axis=1)]
    convert_element_type x1 -> x0, local copies, waits for them, and re-layouts: 3.84 us -> none  [combine_picks(): returned_rows.reshape(-1, layer_width)[slot_index].astype(jnp.float32)]
    unnamed x61 -> x41, local copies, waits for them, and re-layouts: 12.9 us -> 10.7 us
  transfers between devices with their start and end apart: 3 -> 3, of which waited for: 1 -> 1; matrix products, arithmetic and copies ran while one was open for 18% -> 19% of each run, Pallas kernels for 0% -> 0%
where the time goes in v1:
time: 265 us; the launch traced here: 264 us
  blocking collectives  95 us (36%)
  waiting for transfers between devices  58.2 us (22%)
  matrix products  51.6 us (19%)
  local copies, waits for them, and re-layouts  30.7 us (12%)
  between operations  14.5 us (5%)
  other arithmetic  9.41 us (4%)
  starting transfers between devices  4.79 us (2%)
    all_to_all x1, blocking collectives, routed_whole(): lax.all_to_all(reshaped_rows, 'exp', split_axis=0, concat_axis=0, tiled=T...  64 us
    all_to_all x1, waiting for transfers between devices, routed_whole(): lax.all_to_all(produced, 'exp', split_axis=0, concat_axis=0, tiled=True)  56.8 us
    all_gather x1, blocking collectives, local(): lax.all_gather(key_projection, 'req', axis=0, tiled=True)  15.6 us
    all_gather x1, blocking collectives, local(): lax.all_gather(value_projection, 'req', axis=0, tiled=True)  15.4 us
    dot_general x1, matrix products, expert_products(): jnp.einsum('pekf,efd->pekd', hidden, w_down, preferred_element_type=jnp.f...  14.4 us
    unnamed x41, local copies, waits for them, and re-layouts  10.7 us
    dot_general x1, matrix products, expert_products(): jnp.einsum('pekd,edf->pekf', received, w_up, preferred_element_type=jnp.f...  5.4 us
  transfers between devices with their start and end apart: 3, of which 1 were waited for; matrix products, arithmetic and copies ran while one was open for 19% of the time, Pallas kernels for 0%

profile of v1, /device:TPU:0, one launch (start us, length us, event | category | flops | bytes accessed | tf_op | source)
XLA Modules:
  0.0 264.1 jit_solution(11095050774544696425)
XLA Ops:
  13.6 15.6 %all_gather.13 = bf16[1536,256]{1,0:T(8,128)(2,1)S(1)} all-gather(bf16[192,256]{1,0:T(8,128)(2,1)S(1)} %copy-done.8), channel_id=1, replica_groups=mesh['req'=8,'exp'=16] {'req'}, dimensions={0}, use_global_device_ids=true | all-gather | bytes 884736 | tf_op jit(solution)/shard_map/all_gather | solution.py:196
  30.8 4.5 %fusion.82 = (bf16[4,1024,256]{2,1,0:T(8,128)(2,1)}, bf16[4,1024,256]{2,1,0:T(8,128)(2,1)}) fusion(bf16[4,1024,512]{2,1,0:T(8,128)(2,1)} %param.28), kind=kLoop, calls=%fused_computation.121 | loop fusion | bytes 8388608 | tf_op jit(solution)/shard_map/vmap()/slice | solution.py:61
  35.4 3.0 %copy.148 = bf16[4,1024,256]{1,2,0:T(8,128)(2,1)S(1)} copy(bf16[4,1024,256]{2,1,0:T(8,128)(2,1)} %get-tuple-element.3) | data formatting | bytes 4194304
  38.4 15.4 %all_gather.14 = bf16[1536,256]{1,0:T(8,128)(2,1)S(1)} all-gather(bf16[192,256]{1,0:T(8,128)(2,1)} %param.20), channel_id=1, replica_groups=mesh['req'=8,'exp'=16] {'req'}, dimensions={0}, use_global_device_ids=true | all-gather | bytes 884736 | tf_op jit(solution)/shard_map/all_gather | solution.py:201
  53.8 1.8 convolution_convert_fusion.1
  55.6 1.6 reshape.210
  57.2 4.0 %copy.151 = bf16[4,1024,256]{1,2,0:T(8,128)(2,1)} copy(bf16[4,1024,256]{2,1,0:T(8,128)(2,1)} %get-tuple-element.2) | data formatting | bytes 4194304
  64.8 4.7 %fusion.80 = f32[256,1536]{0,1:T(8,128)S(1)} fusion(bf16[1536,1536]{1,0:T(8,128)(2,1)} %all-gather.3.cloned.1.call-done, bf16[256,1536]{1,0:T(8,128)(2,1)} %param.16, f32[1536]{0:T(1024)} %param.17, f32[256]{0:T(256)} %copy-done.13), kind=kOutput, calls=%fused_computation.120 | convolution fusion | flops 1209532416 | bytes 7085056 | tf_op jit(solution)/shard_map/dot_general | solution.py:189
  70.7 1.6 copy.107
  73.1 2.1 bitcast_reduce_fusion
  75.6 3.1 %fusion.1 = f32[4,2,6,64]{3,2,1,0:T(8,128)S(1)} fusion(f32[4,2,64,6,1024]{4,2,3,1,0:T(8,128)S(1)} %get-tuple-element.17, f32[4,2,6,64]{3,2,1,0:T(8,128)S(1)} %max.24, pred[4,1024]{1,0:T(4,128)(4,1)S(1)} %iota_compare_fusion.9), kind=kLoop, calls=%fused_computation.6 | loop fusion | flops 12579840 | bytes 12611584 | tf_op jit(solution)/shard_map/vmap()/reduce_sum | solution.py:86
  80.3 4.2 %fusion.33 = bf16[4,64,2,6,128]{4,1,3,2,0:T(8,128)(2,1)S(1)} fusion(f32[4,2,128,6,64]{2,4,3,1,0:T(8,128)S(1)} %fusion.40, bf16[4,1024,2,128,1]{1,3,4,2,0:T(8,128)(2,1)S(1)} %bitcast.97, f32[4,2,64,6,1024]{4,2,3,1,0:T(8,128)S(1)} %get-tuple-element.17, f32[4,2,6,64]{3,2,1,0:T(8,128)S(1)} %add.80, f32[4,2,6,64]{3,2,1,0:T(8,128)S(1)} %max.24, ...), kind=kOutput, calls=%fused_computation.36 | convolution fusion | flops 821821440 | bytes 17068032 | tf_op jit(solution)/shard_map/vmap(gsij,jgd->igsd)/dot_general | solution.py:91
  85.0 1.7 convert_element_type.128
  86.8 4.4 %multiply_reduce_fusion = (f32[256]{0:T(256)S(1)}, f32[256,1536]{1,0:T(8,128)S(1)}) fusion(bf16[256,1536]{1,0:T(8,128)(2,1)} %convert_element_type.128, bf16[1536,1536]{0,1:T(8,128)(2,1)} %all-gather.5.cloned.1.call-done, bf16[256,1536]{1,0:T(8,128)(2,1)} %param.16), kind=kOutput, calls=%fused_computation.40 | convolution fusion | flops 1210318592 | bytes 7865344 | tf_op jit(solution)/shard_map/dot_general | solution.py:213
  91.2 1.5 fusion.36
  92.7 64.0 %all_to_all.10 = bf16[16,2,48,1536]{3,2,1,0:T(8,128)(2,1)S(1)} all-to-all(bf16[16,2,48,1536]{3,2,1,0:T(8,128)(2,1)S(1)} %fusion.36), channel_id=1, replica_groups=mesh['req'=8,'exp'=16] {'exp'}, dimensions={0} | all-to-all | bytes 9437184 | tf_op jit(solution)/shard_map/all_to_all | solution.py:157
  156.7 2.2 copy-done
  158.9 5.4 %fusion.6 = f32[2,16,48,768]{3,2,1,0:T(8,128)} fusion(bf16[2,1536,768]{2,1,0:T(8,128)(2,1)S(1)} %bitcast.104, bf16[16,2,48,1536]{3,2,1,0:T(8,128)(2,1)S(1)} %all_to_all.10), kind=kOutput, calls=%fused_computation.13 | convolution fusion | flops 3623878656 | bytes 14155776 | tf_op jit(solution)/shard_map/pekd,edf->pekf/dot_general | solution.py:133
  164.3 14.4 %convert_bitcast_fusion = bf16[16,2,48,1536]{3,2,0,1:T(8,128)(2,1)} fusion(bf16[2,768,1536]{2,1,0:T(8,128)(2,1)} %param.25, f32[2,16,48,768]{3,2,1,0:T(8,128)} %fusion.6, bf16[2,1536,768]{2,1,0:T(8,128)(2,1)} %param.23, bf16[16,2,48,1536]{3,2,1,0:T(8,128)(2,1)} %copy-done), kind=kOutput, calls=%fused_computation.17 | convolution fusion | flops 7253655552 | bytes 23592960 | tf_op jit(solution)/shard_map/pekf,efd->pekd/dot_general | solution.py:135
  178.7 4.9 %copy.126 = bf16[16,2,48,1536]{3,2,1,0:T(8,128)(2,1)} copy(bf16[16,2,48,1536]{3,2,0,1:T(8,128)(2,1)} %convert_bitcast_fusion) | data formatting | bytes 9437184 | tf_op jit(solution)/shard_map/convert_element_type | solution.py:135
  183.6 4.7 %all-to-all-start.1 = ((bf16[16,2,48,1536]{3,2,1,0:T(8,128)(2,1)}), bf16[16,2,48,1536]{3,2,1,0:T(8,128)(2,1)}, u32[]{:S(2)}, u32[]{:S(2)}) async-start(bf16[16,2,48,1536]{3,2,1,0:T(8,128)(2,1)} %copy.126), calls=%async_computation.1 | async-start | bytes 9437184 | tf_op jit(solution)/shard_map/all_to_all | solution.py:162
  192.1 56.8 %all-to-all-done.1 = bf16[16,2,48,1536]{3,2,1,0:T(8,128)(2,1)} async-done(((bf16[16,2,48,1536]{3,2,1,0:T(8,128)(2,1)}), bf16[16,2,48,1536]{3,2,1,0:T(8,128)(2,1)}, u32[]{:S(2)}, u32[]{:S(2)}) %all-to-all-start.1) | async-done | bytes 4718624 | tf_op jit(solution)/shard_map/all_to_all | solution.py:162
  248.9 3.7 %fusion.45 = f32[256,1536]{1,0:T(8,128)S(1)} fusion(bf16[1536,1536]{1,0:T(8,128)(2,1)} %bitcast.26, f32[256,1536]{1,0:T(8,128)S(1)} %select_reduce_fusion), kind=kOutput, calls=%fused_computation.65 | convolution fusion | flops 1208352768 | bytes 7864320 | tf_op jit(solution)/shard_map/dot_general | solution.py:146
  252.6 4.7 %fusion.16 = bf16[256,1536]{1,0:T(8,128)(2,1)} fusion(f32[256,1536]{1,0:T(8,128)S(1)} %get-tuple-element.21, f32[256,1536]{1,0:T(8,128)S(1)} %fusion.45, bf16[1536,1536]{1,0:T(8,128)(2,1)} %bitcast.26, f32[256,1536]{1,0:T(8,128)S(1)} %select_reduce_fusion), kind=kOutput, calls=%fused_computation.25 | convolution fusion | flops 1210712064 | bytes 10223616 | tf_op jit(solution)/shard_map/dot_general | solution.py:147
  (89 shorter events, 19.8 us)
Async XLA Ops:
  7.2 6.2 %copy-start.3 = (bf16[256,1536]{1,0:T(8,128)(2,1)S(1)}, bf16[256,1536]{1,0:T(8,128)(2,1)}, u32[]{:S(2)}) copy-start(bf16[256,1536]{1,0:T(8,128)(2,1)} %param.16) | copy-start | bytes 2359300
  7.2 6.5 %copy-start.8 = (bf16[192,256]{1,0:T(8,128)(2,1)S(1)}, bf16[192,256]{1,0:T(8,128)(2,1)}, u32[]{:S(2)}) copy-start(bf16[192,256]{1,0:T(8,128)(2,1)} %param.19) | copy-start | bytes 294916
  7.2 22.0 %copy-start.14 = (f32[1536]{0:T(1024)S(1)}, f32[1536]{0:T(1024)}, u32[]{:S(2)}) copy-start(f32[1536]{0:T(1024)} %param.17) | copy-start | bytes 18436
  7.2 57.6 %all-gather.3.cloned.1.call-start = ((), (), s32[]{:S(2)}) async-start(), calls=%async_computation.2 | async-start | bytes 5308416 | tf_op jit(solution)/shard_map/all_gather | solution.py:191
  7.9 78.8 %all-gather.5.cloned.1.call-start = ((), (), s32[]{:S(2)}) async-start(), calls=%async_computation.3 | async-start | bytes 5308416 | tf_op jit(solution)/shard_map/all_gather | solution.py:215
  10.6 19.2 %copy-start.4 = (f32[4,64,64]{2,1,0:T(8,128)}, f32[4,64,64]{2,1,0:T(8,128)S(1)}, u32[]{:S(2)}) copy-start(f32[4,64,64]{2,1,0:T(8,128)S(1)} %get-tuple-element.15) | copy-start | bytes 196612
  13.6 40.2 %copy-start.13 = (f32[256]{0:T(256)}, f32[256]{0:T(256)S(1)}, u32[]{:S(2)}) copy-start(f32[256]{0:T(256)S(1)} %add_rsqrt_fusion.1) | copy-start | bytes 3076
  53.8 7.4 %copy-start.9 = (s32[256,4]{0,1:T(4,128)S(1)}, s32[256,4]{0,1:T(4,128)}, u32[]{:S(2)}) copy-start(s32[256,4]{0,1:T(4,128)} %param.26) | copy-start | bytes 12292
  57.2 7.5 %copy-start.12 = (s32[4]{0:T(128)S(1)}, s32[4]{0:T(128)}, u32[]{:S(2)}) copy-start(s32[4]{0:T(128)} %param.29) | copy-start | bytes 52
  69.5 2.8 %copy-start.5 = (pred[4,64,64]{1,2,0:T(8,128)(4,1)S(1)}, pred[4,64,64]{1,2,0:T(8,128)(4,1)}, u32[]{:S(2)}) copy-start(pred[4,64,64]{1,2,0:T(8,128)(4,1)} %copy.111) | copy-start | bytes 49156
  75.6 3.2 %copy-start.7 = (bf16[4,64,2,128]{3,2,1,0:T(2,128)(2,1)S(1)}, bf16[4,64,2,128]{3,2,1,0:T(2,128)(2,1)}, u32[]{:S(2)}) copy-start(bf16[4,64,2,128]{3,2,1,0:T(2,128)(2,1)} %reshape.210) | copy-start | bytes 393220
  78.7 1.6 copy-start.2
  86.8 4.4 %copy-start.1 = (bf16[1536,256]{1,0:T(8,128)(2,1)S(1)}, bf16[1536,256]{1,0:T(8,128)(2,1)}, u32[]{:S(2)}) copy-start(bf16[1536,256]{1,0:T(8,128)(2,1)} %copy.123) | copy-start | bytes 2359300
  86.8 4.4 %copy-start.10 = (f32[1536]{0:T(1024)S(1)}, f32[1536]{0:T(1024)}, u32[]{:S(2)}) copy-start(f32[1536]{0:T(1024)} %param.22) | copy-start | bytes 18436
  91.2 67.7 %slice-start = ((s8[4718592]{0:T(1024)(128)(4,1)}), s8[4194304]{0:T(1024)(128)(4,1)S(1)}, s32[]{:S(2)}) async-start(s8[4718592]{0:T(1024)(128)(4,1)} %bitcast.103), calls=%async_computation.4 | async-start | bytes 8388608
  92.7 66.2 %slice-start.1 = ((s8[4718592]{0:T(1024)(128)(4,1)}), s8[524288]{0:T(1024)(128)(4,1)S(1)}, s32[]{:S(2)}) async-start(s8[4718592]{0:T(1024)(128)(4,1)} %bitcast.103), calls=%async_computation.5 | async-start | bytes 1048576
  156.7 2.2 copy-start
  183.6 5.0 %copy-start.15 = (s32[4]{0:T(128)S(1)}, s32[4]{0:T(128)}, u32[]{:S(2)}) copy-start(s32[4]{0:T(128)} %param.31) | copy-start | bytes 52
  183.6 6.6 %copy-start.6 = (bf16[256,256]{1,0:T(8,128)(2,1)S(1)}, bf16[256,256]{1,0:T(8,128)(2,1)}, u32[]{:S(2)}) copy-start(bf16[256,256]{1,0:T(8,128)(2,1)} %convolution_convert_fusion.1) | copy-start | bytes 393220
  183.6 7.5 %copy-start.11 = (f32[256,4]{0,1:T(4,128)S(1)}, f32[256,4]{0,1:T(4,128)}, u32[]{:S(2)}) copy-start(f32[256,4]{0,1:T(4,128)} %param.27) | copy-start | bytes 12292
  183.6 65.3 %all-to-all-start.1 = ((bf16[16,2,48,1536]{3,2,1,0:T(8,128)(2,1)}), bf16[16,2,48,1536]{3,2,1,0:T(8,128)(2,1)}, u32[]{:S(2)}, u32[]{:S(2)}) async-start(bf16[16,2,48,1536]{3,2,1,0:T(8,128)(2,1)} %copy.126), calls=%async_computation.1 | async-start | bytes 9437184 | tf_op jit(solution)/shard_map/all_to_all | solution.py:162
Sparse Core Ops, SparseCore 0:
  9.7 38.5 all-gather.2
  50.0 34.2 all-gather.4

commit v2 on v1

--- a/solution.py
+++ b/solution.py
@@ -12,6 +12,7 @@
 TOP = 4
 DRAFT_TOKENS = 64
 CAP = 24
+BLOCK_ROWS = 128
 
 
 eps_norm = 1e-06
@@ -148,7 +149,7 @@
 
 
 def routed_whole(moe_in, routes, gate_weights, w_gate, w_up, w_down):
-    capacity = 2 * CAP
+    capacity = CAP * (moe_in.shape[0] // BLOCK_ROWS)
     hit = slot_tables(routes, capacity)
     buffer = pack_slots(moe_in, hit)
     peer_count = lax.axis_size("exp")
@@ -207,18 +208,22 @@
     )
     query_req = query_rows.reshape(local_reqs, DRAFT_TOKENS, query_rows.shape[1])
     key_value_request = tree_key_value.reshape(local_reqs, DRAFT_TOKENS, tree_key_value.shape[1])
-    context = jax.vmap(attend)(query_req, key_value_request, kv_cache, lengths, closure).reshape(
-        rows_here, -1
-    )
-    attn_out = jnp.dot(
-        context,
-        lax.all_gather(w_out, "req", axis=1, tiled=True),
-        preferred_element_type=jnp.float32,
-    )
-    residual = (tokens.astype(jnp.float32) + attn_out).astype(jnp.bfloat16)
-    moe_in = rms_scale(residual, moe_gain)
-    mixed = routed_whole(moe_in, routes, gate_weights, w_gate, w_up, w_down)
-    layer_out = (residual.astype(jnp.float32) + mixed).astype(jnp.bfloat16)
+    w_out_full = lax.all_gather(w_out, "req", axis=1, tiled=True)
+    chunk_count = rows_here // BLOCK_ROWS
+    reqs_per_chunk = local_reqs // chunk_count
+    outs = []
+    for chunk in range(chunk_count):
+        rq = slice(chunk * reqs_per_chunk, (chunk + 1) * reqs_per_chunk)
+        rw = slice(chunk * BLOCK_ROWS, (chunk + 1) * BLOCK_ROWS)
+        context = jax.vmap(attend)(
+            query_req[rq], key_value_request[rq], kv_cache[rq], lengths[rq], closure[rq]
+        ).reshape(BLOCK_ROWS, -1)
+        attn_out = jnp.dot(context, w_out_full, preferred_element_type=jnp.float32)
+        residual = (tokens[rw].astype(jnp.float32) + attn_out).astype(jnp.bfloat16)
+        moe_in = rms_scale(residual, moe_gain)
+        mixed = routed_whole(moe_in, routes[rw], gate_weights[rw], w_gate, w_up, w_down)
+        outs.append((residual.astype(jnp.float32) + mixed).astype(jnp.bfloat16))
+    layer_out = jnp.concatenate(outs, axis=0)
     new_entries = compact(key_value_request, closure, tree_depth, accepted)
     return (layer_out, new_entries)
 

time: 265 us -> 255 us (0.962)
  blocking collectives: 95 us -> 31.5 us
  matrix products: 51.6 us -> 71.7 us
  waiting for transfers between devices: 58.2 us -> 77.1 us
  starting transfers between devices: 4.79 us -> 21 us
    all_to_all x1 -> x0, blocking collectives: 64 us -> none  [routed_whole(): lax.all_to_all(reshaped_rows, 'exp', split_axis=0, concat_axis=0, tiled=T...]
    all_to_all x0 -> x2, waiting for transfers between devices: none -> 30.1 us  [routed_whole(): lax.all_to_all(reshaped_rows, 'exp', split_axis=0, concat_axis=0, tiled=T...]
    all_to_all x1 -> x2, waiting for transfers between devices: 56.8 us -> 33.9 us  [routed_whole(): lax.all_to_all(produced, 'exp', split_axis=0, concat_axis=0, tiled=True)]
    all_to_all x0 -> x2, starting transfers between devices: none -> 12.2 us  [routed_whole(): lax.all_to_all(reshaped_rows, 'exp', split_axis=0, concat_axis=0, tiled=T...]
    all_gather x1, waiting for transfers between devices: 0.01 us -> 11.7 us  [local(): w_out_full = lax.all_gather(w_out, 'req', axis=1, tiled=True)]
    dot_general x1 -> x2, matrix products: 5.4 us -> 13 us  [expert_products(): jnp.einsum('pekd,edf->pekf', received, w_up, preferred_element_type=jnp.f...]
    dot_general x1 -> x2, matrix products: 14.4 us -> 20.8 us  [expert_products(): jnp.einsum('pekf,efd->pekd', hidden, w_down, preferred_element_type=jnp.f...]
    all_to_all x1 -> x2, starting transfers between devices: 4.71 us -> 8.69 us  [routed_whole(): lax.all_to_all(produced, 'exp', split_axis=0, concat_axis=0, tiled=True)]
  transfers between devices with their start and end apart: 3 -> 6, of which waited for: 1 -> 5; matrix products, arithmetic and copies ran while one was open for 19% -> 38% of each run, Pallas kernels for 0% -> 0%
where the time goes in v2:
time: 255 us; the launch traced here: 254 us
  waiting for transfers between devices  77.1 us (30%)
  matrix products  71.7 us (28%)
  blocking collectives  31.5 us (12%)
  local copies, waits for them, and re-layouts  29.4 us (12%)
  starting transfers between devices  21 us (8%)
  between operations  14.8 us (6%)
  other arithmetic  8.51 us (3%)
    all_to_all x2, waiting for transfers between devices, routed_whole(): lax.all_to_all(produced, 'exp', split_axis=0, concat_axis=0, tiled=True)  33.9 us
    all_to_all x2, waiting for transfers between devices, routed_whole(): lax.all_to_all(reshaped_rows, 'exp', split_axis=0, concat_axis=0, tiled=T...  30.1 us
    dot_general x2, matrix products, expert_products(): jnp.einsum('pekf,efd->pekd', hidden, w_down, preferred_element_type=jnp.f...  20.8 us
    all_gather x1, blocking collectives, local(): lax.all_gather(value_projection, 'req', axis=0, tiled=True)  16.2 us
    all_gather x1, blocking collectives, local(): lax.all_gather(key_projection, 'req', axis=0, tiled=True)  15.3 us
    dot_general x2, matrix products, expert_products(): jnp.einsum('pekd,edf->pekf', received, w_up, preferred_element_type=jnp.f...  13 us
    all_to_all x2, starting transfers between devices, routed_whole(): lax.all_to_all(reshaped_rows, 'exp', split_axis=0, concat_axis=0, tiled=T...  12.2 us
    all_gather x1, waiting for transfers between devices, local(): w_out_full = lax.all_gather(w_out, 'req', axis=1, tiled=True)  11.7 us
  transfers between devices with their start and end apart: 6, of which 5 were waited for; matrix products, arithmetic and copies ran while one was open for 38% of the time, Pallas kernels for 0%

profile of v2, /device:TPU:0, one launch (start us, length us, event | category | flops | bytes accessed | tf_op | source)
XLA Modules:
  0.0 253.9 jit_solution(3814630672263138442)
XLA Ops:
  12.6 15.3 %all_gather.13 = bf16[1536,256]{1,0:T(8,128)(2,1)S(1)} all-gather(bf16[192,256]{1,0:T(8,128)(2,1)S(1)} %copy-done.14), channel_id=1, replica_groups=mesh['req'=8,'exp'=16] {'req'}, dimensions={0}, use_global_device_ids=true | all-gather | bytes 884736 | tf_op jit(solution)/shard_map/all_gather | solution.py:197
  28.7 16.2 %all_gather.14 = bf16[1536,256]{1,0:T(8,128)(2,1)S(1)} all-gather(bf16[192,256]{1,0:T(8,128)(2,1)S(1)} %copy-done.15), channel_id=1, replica_groups=mesh['req'=8,'exp'=16] {'req'}, dimensions={0}, use_global_device_ids=true | all-gather | bytes 884736 | tf_op jit(solution)/shard_map/all_gather | solution.py:202
  46.7 3.9 %fusion.158 = (bf16[2,1024,256]{2,1,0:T(8,128)(2,1)}, bf16[2,1024,256]{2,1,0:T(8,128)(2,1)}, bf16[2,1024,256]{2,1,0:T(8,128)(2,1)S(1)}, bf16[2,1024,256]{2,1,0:T(8,128)(2,1)}) fusion(bf16[4,1024,512]{2,1,0:T(8,128)(2,1)} %param.28), kind=kLoop, calls=%fused_computation.204 | loop fusion | bytes 8388608 | tf_op jit(solution)/shard_map/vmap()/slice | solution.py:61
  58.0 2.3 copy.226
  62.7 4.3 %fusion.156 = f32[256,1536]{0,1:T(8,128)S(1)} fusion(bf16[1536,1536]{1,0:T(8,128)(2,1)} %all-gather.3.cloned.1.call-done, bf16[256,1536]{1,0:T(8,128)(2,1)S(1)} %copy-done.3, f32[1536]{0:T(1024)S(1)} %copy-done.33, f32[256]{0:T(256)S(1)} %copy-done.31), kind=kOutput, calls=%fused_computation.203 | convolution fusion | flops 1209532416 | bytes 7085056 | tf_op jit(solution)/shard_map/dot_general | solution.py:190
  74.4 11.7 %all-gather.5.cloned.1.call-done = bf16[1536,1536]{0,1:T(8,128)(2,1)} async-done(((bf16[1536,192]{0,1:T(8,128)(2,1)}), bf16[1536,1536]{0,1:T(8,128)(2,1)}) %all-gather.5.cloned.1.call-update) | async-done | bytes 4718608 | tf_op jit(solution)/shard_map/all_gather | solution.py:211
  86.1 4.1 %multiply_reduce_fusion.1 = (f32[128]{0:T(128)S(1)}, f32[128,1536]{1,0:T(8,128)S(1)}) fusion(bf16[128,1536]{1,0:T(8,128)(2,1)S(1)} %convert_element_type.192, bf16[1536,1536]{0,1:T(8,128)(2,1)} %all-gather.5.cloned.1.call-done, bf16[256,1536]{1,0:T(8,128)(2,1)S(1)} %copy-done.4), kind=kOutput, calls=%fused_computation.98 | convolution fusion | flops 605159296 | bytes 6291968 | tf_op jit(solution)/shard_map/dot_general | solution.py:221
  90.3 2.3 fusion.90
  92.6 6.8 %all-to-all-start = ((bf16[16,2,24,1536]{3,2,1,0:T(8,128)(2,1)}), bf16[16,2,24,1536]{3,2,1,0:T(8,128)(2,1)}, u32[]{:S(2)}, u32[]{:S(2)}) async-start(bf16[16,2,24,1536]{3,2,1,0:T(8,128)(2,1)} %fusion.90), calls=%async_computation | async-start | bytes 4718592 | tf_op jit(solution)/shard_map/all_to_all | solution.py:158
  107.8 4.1 %multiply_reduce_fusion = (f32[128]{0:T(128)S(1)}, f32[128,1536]{1,0:T(8,128)S(1)}) fusion(bf16[128,1536]{1,0:T(8,128)(2,1)S(1)} %convert_element_type.212, bf16[1536,1536]{0,1:T(8,128)(2,1)} %all-gather.5.cloned.1.call-done, bf16[256,1536]{1,0:T(8,128)(2,1)S(1)} %copy-done.4), kind=kOutput, calls=%fused_computation.94 | convolution fusion | flops 605159296 | bytes 6291968 | tf_op jit(solution)/shard_map/dot_general | solution.py:221
  112.8 2.3 fusion.93
  115.0 18.0 %all-to-all-done = bf16[16,2,24,1536]{3,2,1,0:T(8,128)(2,1)} async-done(((bf16[16,2,24,1536]{3,2,1,0:T(8,128)(2,1)}), bf16[16,2,24,1536]{3,2,1,0:T(8,128)(2,1)}, u32[]{:S(2)}, u32[]{:S(2)}) %all-to-all-start) | async-done | bytes 2359328 | tf_op jit(solution)/shard_map/all_to_all | solution.py:158
  133.1 5.3 %all-to-all-start.2 = ((bf16[16,2,24,1536]{3,2,1,0:T(8,128)(2,1)}), bf16[16,2,24,1536]{3,2,1,0:T(8,128)(2,1)S(1)}, u32[]{:S(2)}, u32[]{:S(2)}) async-start(bf16[16,2,24,1536]{3,2,1,0:T(8,128)(2,1)} %fusion.93), calls=%async_computation.2 | async-start | bytes 4718592 | tf_op jit(solution)/shard_map/all_to_all | solution.py:158
  138.4 6.5 %fusion.10 = f32[2,16,24,768]{3,2,1,0:T(8,128)} fusion(bf16[2,1536,768]{2,1,0:T(8,128)(2,1)} %param.24, bf16[16,2,24,1536]{3,2,1,0:T(8,128)(2,1)} %all-to-all-done), kind=kOutput, calls=%fused_computation.19 | convolution fusion | flops 1811939328 | bytes 9437184 | tf_op jit(solution)/shard_map/pekd,edf->pekf/dot_general | solution.py:134
  144.9 10.4 %fusion.27 = bf16[16,2,24,1536]{3,2,0,1:T(8,128)(2,1)} fusion(bf16[2,768,1536]{2,1,0:T(8,128)(2,1)} %param.25, f32[2,16,24,768]{3,2,1,0:T(8,128)} %fusion.10, bf16[2,1536,768]{2,1,0:T(8,128)(2,1)} %param.23, bf16[16,2,24,1536]{3,2,1,0:T(8,128)(2,1)} %all-to-all-done), kind=kOutput, calls=%fused_computation.30 | convolution fusion | flops 3626827776 | bytes 16515072 | tf_op jit(solution)/shard_map/pekf,efd->pekd/dot_general | solution.py:136
  155.3 3.4 %copy.170 = bf16[16,2,24,1536]{3,2,1,0:T(8,128)(2,1)} copy(bf16[16,2,24,1536]{3,2,0,1:T(8,128)(2,1)} %fusion.27) | data formatting | bytes 4718592 | tf_op jit(solution)/shard_map/convert_element_type | solution.py:136
  158.7 12.0 %all-to-all-done.2 = bf16[16,2,24,1536]{3,2,1,0:T(8,128)(2,1)S(1)} async-done(((bf16[16,2,24,1536]{3,2,1,0:T(8,128)(2,1)}), bf16[16,2,24,1536]{3,2,1,0:T(8,128)(2,1)S(1)}, u32[]{:S(2)}, u32[]{:S(2)}) %all-to-all-start.2) | async-done | bytes 2359328 | tf_op jit(solution)/shard_map/all_to_all | solution.py:158
  172.1 4.0 %all-to-all-start.1 = ((bf16[16,2,24,1536]{3,2,1,0:T(8,128)(2,1)}), bf16[16,2,24,1536]{3,2,1,0:T(8,128)(2,1)S(1)}, u32[]{:S(2)}, u32[]{:S(2)}) async-start(bf16[16,2,24,1536]{3,2,1,0:T(8,128)(2,1)} %copy.170), calls=%async_computation.1 | async-start | bytes 4718592 | tf_op jit(solution)/shard_map/all_to_all | solution.py:163
  176.2 6.5 %fusion.8 = f32[2,16,24,768]{3,2,1,0:T(8,128)} fusion(bf16[2,1536,768]{2,1,0:T(8,128)(2,1)} %param.24, bf16[16,2,24,1536]{3,2,1,0:T(8,128)(2,1)} %copy-done.5), kind=kOutput, calls=%fused_computation.17 | convolution fusion | flops 1811939328 | bytes 9437184 | tf_op jit(solution)/shard_map/pekd,edf->pekf/dot_general | solution.py:134
  182.7 10.4 %fusion.24 = bf16[16,2,24,1536]{3,2,0,1:T(8,128)(2,1)} fusion(bf16[2,768,1536]{2,1,0:T(8,128)(2,1)} %param.25, f32[2,16,24,768]{3,2,1,0:T(8,128)} %fusion.8, bf16[2,1536,768]{2,1,0:T(8,128)(2,1)} %param.23, bf16[16,2,24,1536]{3,2,1,0:T(8,128)(2,1)} %copy-done.5), kind=kOutput, calls=%fused_computation.29 | convolution fusion | flops 3626827776 | bytes 16515072 | tf_op jit(solution)/shard_map/pekf,efd->pekd/dot_general | solution.py:136
  193.1 3.4 %copy.186 = bf16[16,2,24,1536]{3,2,1,0:T(8,128)(2,1)} copy(bf16[16,2,24,1536]{3,2,0,1:T(8,128)(2,1)} %fusion.24) | data formatting | bytes 4718592 | tf_op jit(solution)/shard_map/convert_element_type | solution.py:136
  196.5 10.0 %all-to-all-done.1 = bf16[16,2,24,1536]{3,2,1,0:T(8,128)(2,1)S(1)} async-done(((bf16[16,2,24,1536]{3,2,1,0:T(8,128)(2,1)}), bf16[16,2,24,1536]{3,2,1,0:T(8,128)(2,1)S(1)}, u32[]{:S(2)}, u32[]{:S(2)}) %all-to-all-start.1) | async-done | bytes 2359328 | tf_op jit(solution)/shard_map/all_to_all | solution.py:163
  206.5 4.7 %all-to-all-start.3 = ((bf16[16,2,24,1536]{3,2,1,0:T(8,128)(2,1)}), bf16[16,2,24,1536]{3,2,1,0:T(8,128)(2,1)}, u32[]{:S(2)}, u32[]{:S(2)}) async-start(bf16[16,2,24,1536]{3,2,1,0:T(8,128)(2,1)} %copy.186), calls=%async_computation.3 | async-start | bytes 4718592 | tf_op jit(solution)/shard_map/all_to_all | solution.py:163
  217.8 23.9 %all-to-all-done.3 = bf16[16,2,24,1536]{3,2,1,0:T(8,128)(2,1)} async-done(((bf16[16,2,24,1536]{3,2,1,0:T(8,128)(2,1)}), bf16[16,2,24,1536]{3,2,1,0:T(8,128)(2,1)}, u32[]{:S(2)}, u32[]{:S(2)}) %all-to-all-start.3) | async-done | bytes 2359328 | tf_op jit(solution)/shard_map/all_to_all | solution.py:163
  (160 shorter events, 47.2 us)
Async XLA Ops:
  7.2 5.4 %copy-start.14 = (bf16[192,256]{1,0:T(8,128)(2,1)S(1)}, bf16[192,256]{1,0:T(8,128)(2,1)}, u32[]{:S(2)}) copy-start(bf16[192,256]{1,0:T(8,128)(2,1)} %param.19) | copy-start | bytes 294916
  7.2 20.7 %copy-start.32 = (f32[1536]{0:T(1024)S(1)}, f32[1536]{0:T(1024)}, u32[]{:S(2)}) copy-start(f32[1536]{0:T(1024)} %param.17) | copy-start | bytes 18436
  7.2 55.5 %all-gather.3.cloned.1.call-start = ((), (), s32[]{:S(2)}) async-start(), calls=%async_computation.4 | async-start | bytes 5308416 | tf_op jit(solution)/shard_map/all_gather | solution.py:192
  7.9 78.2 %all-gather.5.cloned.1.call-start = ((), (), s32[]{:S(2)}) async-start(), calls=%async_computation.5 | async-start | bytes 5308416 | tf_op jit(solution)/shard_map/all_gather | solution.py:211
  10.7 35.3 %copy-start.11 = (f32[4,64,64]{2,1,0:T(8,128)}, f32[4,64,64]{2,1,0:T(8,128)S(1)}, u32[]{:S(2)}) copy-start(f32[4,64,64]{2,1,0:T(8,128)S(1)} %get-tuple-element.33) | copy-start | bytes 196612
  12.0 16.6 %copy-start.15 = (bf16[192,256]{1,0:T(8,128)(2,1)S(1)}, bf16[192,256]{1,0:T(8,128)(2,1)}, u32[]{:S(2)}) copy-start(bf16[192,256]{1,0:T(8,128)(2,1)} %param.20) | copy-start | bytes 294916
  12.3 32.6 %copy-start.30 = (f32[256]{0:T(256)}, f32[256]{0:T(256)S(1)}, u32[]{:S(2)}) copy-start(f32[256]{0:T(256)S(1)} %add_rsqrt_fusion) | copy-start | bytes 3076
  54.5 5.8 %copy-start.24 = (s32[128,4]{0,1:T(4,128)}, s32[128,4]{0,1:T(4,128)S(1)}, u32[]{:S(2)}) copy-start(s32[128,4]{0,1:T(4,128)S(1)} %get-tuple-element.22) | copy-start | bytes 6148
  54.5 6.4 %copy-start.22 = (s32[128,4]{0,1:T(4,128)}, s32[128,4]{0,1:T(4,128)S(1)}, u32[]{:S(2)}) copy-start(s32[128,4]{0,1:T(4,128)S(1)} %get-tuple-element.23) | copy-start | bytes 6148
  56.4 5.6 %copy-start.27 = (s32[4]{0:T(128)S(1)}, s32[4]{0:T(128)}, u32[]{:S(2)}) copy-start(s32[4]{0:T(128)} %param.29) | copy-start | bytes 52
  56.4 6.4 %copy-start.3 = (bf16[256,1536]{1,0:T(8,128)(2,1)S(1)}, bf16[256,1536]{1,0:T(8,128)(2,1)}, u32[]{:S(2)}) copy-start(bf16[256,1536]{1,0:T(8,128)(2,1)} %param.16) | copy-start | bytes 2359300
  56.4 6.3 %copy-start.31 = (f32[256]{0:T(256)S(1)}, f32[256]{0:T(256)}, u32[]{:S(2)}) copy-start(f32[256]{0:T(256)} %copy-done.30) | copy-start | bytes 3076
  56.4 6.3 %copy-start.33 = (f32[1536]{0:T(1024)S(1)}, f32[1536]{0:T(1024)}, u32[]{:S(2)}) copy-start(f32[1536]{0:T(1024)} %param.17) | copy-start | bytes 18436
  73.3 12.8 %copy-start.4 = (bf16[256,1536]{1,0:T(8,128)(2,1)S(1)}, bf16[256,1536]{1,0:T(8,128)(2,1)}, u32[]{:S(2)}) copy-start(bf16[256,1536]{1,0:T(8,128)(2,1)} %param.16) | copy-start | bytes 2359300
  92.6 40.5 %all-to-all-start = ((bf16[16,2,24,1536]{3,2,1,0:T(8,128)(2,1)}), bf16[16,2,24,1536]{3,2,1,0:T(8,128)(2,1)}, u32[]{:S(2)}, u32[]{:S(2)}) async-start(bf16[16,2,24,1536]{3,2,1,0:T(8,128)(2,1)} %fusion.90), calls=%async_computation | async-start | bytes 4718592 | tf_op jit(solution)/shard_map/all_to_all | solution.py:158
  133.1 37.6 %all-to-all-start.2 = ((bf16[16,2,24,1536]{3,2,1,0:T(8,128)(2,1)}), bf16[16,2,24,1536]{3,2,1,0:T(8,128)(2,1)S(1)}, u32[]{:S(2)}, u32[]{:S(2)}) async-start(bf16[16,2,24,1536]{3,2,1,0:T(8,128)(2,1)} %fusion.93), calls=%async_computation.2 | async-start | bytes 4718592 | tf_op jit(solution)/shard_map/all_to_all | solution.py:158
  172.1 34.3 %all-to-all-start.1 = ((bf16[16,2,24,1536]{3,2,1,0:T(8,128)(2,1)}), bf16[16,2,24,1536]{3,2,1,0:T(8,128)(2,1)S(1)}, u32[]{:S(2)}, u32[]{:S(2)}) async-start(bf16[16,2,24,1536]{3,2,1,0:T(8,128)(2,1)} %copy.170), calls=%async_computation.1 | async-start | bytes 4718592 | tf_op jit(solution)/shard_map/all_to_all | solution.py:163
  196.5 14.6 %copy-start.34 = (s32[4]{0:T(128)S(1)}, s32[4]{0:T(128)}, u32[]{:S(2)}) copy-start(s32[4]{0:T(128)} %param.31) | copy-start | bytes 52
  196.5 17.1 %copy-start.28 = (f32[256,4]{0,1:T(4,128)S(1)}, f32[256,4]{0,1:T(4,128)}, u32[]{:S(2)}) copy-start(f32[256,4]{0,1:T(4,128)} %param.27) | copy-start | bytes 12292
  196.5 17.1 %copy-start.25 = (s32[128,4]{0,1:T(4,128)S(1)}, s32[128,4]{0,1:T(4,128)}, u32[]{:S(2)}) copy-start(s32[128,4]{0,1:T(4,128)} %copy-done.24) | copy-start | bytes 6148
  196.5 17.3 %copy-start.23 = (s32[128,4]{0,1:T(4,128)S(1)}, s32[128,4]{0,1:T(4,128)}, u32[]{:S(2)}) copy-start(s32[128,4]{0,1:T(4,128)} %copy-done.22) | copy-start | bytes 6148
  196.5 17.6 %copy-start.29 = (s32[4,64]{1,0:T(4,128)S(1)}, s32[4,64]{1,0:T(4,128)}, u32[]{:S(2)}) copy-start(s32[4,64]{1,0:T(4,128)} %get-tuple-element.26) | copy-start | bytes 3076
  206.5 35.2 %all-to-all-start.3 = ((bf16[16,2,24,1536]{3,2,1,0:T(8,128)(2,1)}), bf16[16,2,24,1536]{3,2,1,0:T(8,128)(2,1)}, u32[]{:S(2)}, u32[]{:S(2)}) async-start(bf16[16,2,24,1536]{3,2,1,0:T(8,128)(2,1)} %copy.186), calls=%async_computation.3 | async-start | bytes 4718592 | tf_op jit(solution)/shard_map/all_to_all | solution.py:163
  217.8 26.1 %copy-start.1 = (f32[128,1536]{1,0:T(8,128)S(1)}, f32[128,1536]{1,0:T(8,128)}, u32[]{:S(2)}) copy-start(f32[128,1536]{1,0:T(8,128)} %copy-done) | copy-start | bytes 2359300
  (17 other events, 47.4 us)
Sparse Core Ops, SparseCore 0:
  9.7 40.4 all-gather.2
  51.9 34.1 all-gather.4

commit v3 on v2

--- a/solution.py
+++ b/solution.py
@@ -210,15 +210,13 @@
     key_value_request = tree_key_value.reshape(local_reqs, DRAFT_TOKENS, tree_key_value.shape[1])
     w_out_full = lax.all_gather(w_out, "req", axis=1, tiled=True)
     chunk_count = rows_here // BLOCK_ROWS
-    reqs_per_chunk = local_reqs // chunk_count
+    context_all = jax.vmap(attend)(
+        query_req, key_value_request, kv_cache, lengths, closure
+    ).reshape(rows_here, -1)
     outs = []
     for chunk in range(chunk_count):
-        rq = slice(chunk * reqs_per_chunk, (chunk + 1) * reqs_per_chunk)
         rw = slice(chunk * BLOCK_ROWS, (chunk + 1) * BLOCK_ROWS)
-        context = jax.vmap(attend)(
-            query_req[rq], key_value_request[rq], kv_cache[rq], lengths[rq], closure[rq]
-        ).reshape(BLOCK_ROWS, -1)
-        attn_out = jnp.dot(context, w_out_full, preferred_element_type=jnp.float32)
+        attn_out = jnp.dot(context_all[rw], w_out_full, preferred_element_type=jnp.float32)
         residual = (tokens[rw].astype(jnp.float32) + attn_out).astype(jnp.bfloat16)
         moe_in = rms_scale(residual, moe_gain)
         mixed = routed_whole(moe_in, routes[rw], gate_weights[rw], w_gate, w_up, w_down)

time: 255 us -> 253 us (level)
  waiting for transfers between devices: 77.1 us -> 73.3 us
  other arithmetic: 8.51 us -> 11.4 us
    all_gather x1, waiting for transfers between devices: 11.7 us -> 1.27 us  [local(): w_out_full = lax.all_gather(w_out, 'req', axis=1, tiled=True)]
    all_to_all x2, waiting for transfers between devices: 30.1 us -> 37.3 us  [routed_whole(): lax.all_to_all(reshaped_rows, 'exp', split_axis=0, concat_axis=0, tiled=T...]
    unnamed x75 -> x45, local copies, waits for them, and re-layouts: 9.22 us -> 10.7 us
  transfers between devices with their start and end apart: 6 -> 6, of which waited for: 5 -> 5; matrix products, arithmetic and copies ran while one was open for 38% -> 39% of each run, Pallas kernels for 0% -> 0%
where the time goes in v3:
time: 253 us; the launch traced here: 252 us
  waiting for transfers between devices  73.3 us (29%)
  matrix products  70.1 us (28%)
  local copies, waits for them, and re-layouts  31 us (12%)
  blocking collectives  30.9 us (12%)
  starting transfers between devices  21 us (8%)
  between operations  14.6 us (6%)
  other arithmetic  11.4 us (5%)
    all_to_all x2, waiting for transfers between devices, routed_whole(): lax.all_to_all(reshaped_rows, 'exp', split_axis=0, concat_axis=0, tiled=T...  37.3 us
    all_to_all x2, waiting for transfers between devices, routed_whole(): lax.all_to_all(produced, 'exp', split_axis=0, concat_axis=0, tiled=True)  33.3 us
    dot_general x2, matrix products, expert_products(): jnp.einsum('pekf,efd->pekd', hidden, w_down, preferred_element_type=jnp.f...  20.8 us
    all_gather x1, blocking collectives, local(): lax.all_gather(value_projection, 'req', axis=0, tiled=True)  16 us
    all_gather x1, blocking collectives, local(): lax.all_gather(key_projection, 'req', axis=0, tiled=True)  14.8 us
    dot_general x2, matrix products, expert_products(): jnp.einsum('pekd,edf->pekf', received, w_up, preferred_element_type=jnp.f...  13 us
    all_to_all x2, starting transfers between devices, routed_whole(): lax.all_to_all(reshaped_rows, 'exp', split_axis=0, concat_axis=0, tiled=T...  12.2 us
    unnamed x45, local copies, waits for them, and re-layouts  10.7 us
  transfers between devices with their start and end apart: 6, of which 5 were waited for; matrix products, arithmetic and copies ran while one was open for 39% of the time, Pallas kernels for 0%

profile of v3, /device:TPU:0, one launch (start us, length us, event | category | flops | bytes accessed | tf_op | source)
XLA Modules:
  0.0 252.1 jit_solution(4924337701285337408)
XLA Ops:
  11.8 14.8 %all_gather.13 = bf16[1536,256]{1,0:T(8,128)(2,1)S(1)} all-gather(bf16[192,256]{1,0:T(8,128)(2,1)S(1)} %copy-done.12), channel_id=1, replica_groups=mesh['req'=8,'exp'=16] {'req'}, dimensions={0}, use_global_device_ids=true | all-gather | bytes 884736 | tf_op jit(solution)/shard_map/all_gather | solution.py:197
  32.4 3.0 %copy.177 = bf16[4,1024,256]{1,2,0:T(8,128)(2,1)S(1)} copy(bf16[4,1024,256]{2,1,0:T(8,128)(2,1)} %get-tuple-element.3) | data formatting | bytes 4194304
  35.4 16.0 %all_gather.14 = bf16[1536,256]{1,0:T(8,128)(2,1)S(1)} all-gather(bf16[192,256]{1,0:T(8,128)(2,1)} %param.20), channel_id=1, replica_groups=mesh['req'=8,'exp'=16] {'req'}, dimensions={0}, use_global_device_ids=true | all-gather | bytes 884736 | tf_op jit(solution)/shard_map/all_gather | solution.py:202
  54.1 4.0 %copy.180 = bf16[4,1024,256]{1,2,0:T(8,128)(2,1)} copy(bf16[4,1024,256]{2,1,0:T(8,128)(2,1)} %get-tuple-element.2) | data formatting | bytes 4194304
  63.1 4.4 %fusion.131 = f32[256,1536]{0,1:T(8,128)S(1)} fusion(bf16[1536,1536]{1,0:T(8,128)(2,1)} %all-gather.3.cloned.1.call-done, bf16[256,1536]{1,0:T(8,128)(2,1)S(1)} %copy-done.3, f32[1536]{0:T(1024)} %param.17, f32[256]{0:T(256)} %copy-done.16), kind=kOutput, calls=%fused_computation.163 | convolution fusion | flops 1209532416 | bytes 7085056 | tf_op jit(solution)/shard_map/dot_general | solution.py:190
  73.5 3.1 %fusion.1 = f32[4,2,6,64]{3,2,1,0:T(8,128)S(1)} fusion(f32[4,2,64,6,1024]{4,2,3,1,0:T(8,128)S(1)} %get-tuple-element.25, f32[4,2,6,64]{3,2,1,0:T(8,128)S(1)} %max.25, pred[4,1024]{1,0:T(4,128)(4,1)S(1)} %iota_compare_fusion.12), kind=kLoop, calls=%fused_computation.6 | loop fusion | flops 12579840 | bytes 12611584 | tf_op jit(solution)/shard_map/vmap()/reduce_sum | solution.py:87
  78.3 4.0 %fusion.42 = bf16[4,64,2,6,128]{4,1,3,2,0:T(8,128)(2,1)S(1)} fusion(f32[4,2,128,6,64]{2,4,3,1,0:T(8,128)S(1)} %fusion.76, bf16[4,1024,2,128,1]{1,3,4,2,0:T(8,128)(2,1)S(1)} %bitcast.137, f32[4,2,64,6,1024]{4,2,3,1,0:T(8,128)S(1)} %get-tuple-element.25, f32[4,2,6,64]{3,2,1,0:T(8,128)S(1)} %add.104, f32[4,2,6,64]{3,2,1,0:T(8,128)S(1)} %max.25, ...), kind=kOutput, calls=%fused_computation.48 | convolution fusion | flops 821821440 | bytes 17068032 | tf_op jit(solution)/shard_map/vmap(gsij,jgd->igsd)/dot_general | solution.py:92
  84.4 4.1 %multiply_reduce_fusion.1 = (f32[128]{0:T(128)S(1)}, f32[128,1536]{1,0:T(8,128)S(1)}) fusion(bf16[128,1536]{1,0:T(8,128)(2,1)S(1)} %slice.60, bf16[1536,1536]{0,1:T(8,128)(2,1)} %all-gather.5.cloned.1.call-done, bf16[256,1536]{1,0:T(8,128)(2,1)S(1)} %copy-done.4), kind=kOutput, calls=%fused_computation.80 | convolution fusion | flops 605159296 | bytes 6291968 | tf_op jit(solution)/shard_map/dot_general | solution.py:219
  88.5 2.3 fusion.81
  90.8 6.9 %all-to-all-start = ((bf16[16,2,24,1536]{3,2,1,0:T(8,128)(2,1)}), bf16[16,2,24,1536]{3,2,1,0:T(8,128)(2,1)}, u32[]{:S(2)}, u32[]{:S(2)}) async-start(bf16[16,2,24,1536]{3,2,1,0:T(8,128)(2,1)} %fusion.81), calls=%async_computation | async-start | bytes 4718592 | tf_op jit(solution)/shard_map/all_to_all | solution.py:158
  98.8 4.1 %multiply_reduce_fusion = (f32[128]{0:T(128)S(1)}, f32[128,1536]{1,0:T(8,128)S(1)}) fusion(bf16[128,1536]{1,0:T(8,128)(2,1)S(1)} %slice.65, bf16[1536,1536]{0,1:T(8,128)(2,1)} %all-gather.5.cloned.1.call-done, bf16[256,1536]{1,0:T(8,128)(2,1)S(1)} %copy-done.4), kind=kOutput, calls=%fused_computation.78 | convolution fusion | flops 605159296 | bytes 6291968 | tf_op jit(solution)/shard_map/dot_general | solution.py:219
  106.0 25.3 %all-to-all-done = bf16[16,2,24,1536]{3,2,1,0:T(8,128)(2,1)} async-done(((bf16[16,2,24,1536]{3,2,1,0:T(8,128)(2,1)}), bf16[16,2,24,1536]{3,2,1,0:T(8,128)(2,1)}, u32[]{:S(2)}, u32[]{:S(2)}) %all-to-all-start) | async-done | bytes 2359328 | tf_op jit(solution)/shard_map/all_to_all | solution.py:158
  131.3 5.3 %all-to-all-start.2 = ((bf16[16,2,24,1536]{3,2,1,0:T(8,128)(2,1)}), bf16[16,2,24,1536]{3,2,1,0:T(8,128)(2,1)S(1)}, u32[]{:S(2)}, u32[]{:S(2)}) async-start(bf16[16,2,24,1536]{3,2,1,0:T(8,128)(2,1)} %fusion.84), calls=%async_computation.2 | async-start | bytes 4718592 | tf_op jit(solution)/shard_map/all_to_all | solution.py:158
  136.7 6.5 %fusion.9 = f32[2,16,24,768]{3,2,1,0:T(8,128)} fusion(bf16[2,1536,768]{2,1,0:T(8,128)(2,1)} %param.24, bf16[16,2,24,1536]{3,2,1,0:T(8,128)(2,1)} %all-to-all-done), kind=kOutput, calls=%fused_computation.14 | convolution fusion | flops 1811939328 | bytes 9437184 | tf_op jit(solution)/shard_map/pekd,edf->pekf/dot_general | solution.py:134
  143.1 10.4 %fusion.24 = bf16[16,2,24,1536]{3,2,0,1:T(8,128)(2,1)} fusion(bf16[2,768,1536]{2,1,0:T(8,128)(2,1)} %param.25, f32[2,16,24,768]{3,2,1,0:T(8,128)} %fusion.9, bf16[2,1536,768]{2,1,0:T(8,128)(2,1)} %param.23, bf16[16,2,24,1536]{3,2,1,0:T(8,128)(2,1)} %all-to-all-done), kind=kOutput, calls=%fused_computation.23 | convolution fusion | flops 3626827776 | bytes 16515072 | tf_op jit(solution)/shard_map/pekf,efd->pekd/dot_general | solution.py:136
  153.6 3.4 %copy.149 = bf16[16,2,24,1536]{3,2,1,0:T(8,128)(2,1)} copy(bf16[16,2,24,1536]{3,2,0,1:T(8,128)(2,1)} %fusion.24) | data formatting | bytes 4718592 | tf_op jit(solution)/shard_map/convert_element_type | solution.py:136
  156.9 12.0 %all-to-all-done.2 = bf16[16,2,24,1536]{3,2,1,0:T(8,128)(2,1)S(1)} async-done(((bf16[16,2,24,1536]{3,2,1,0:T(8,128)(2,1)}), bf16[16,2,24,1536]{3,2,1,0:T(8,128)(2,1)S(1)}, u32[]{:S(2)}, u32[]{:S(2)}) %all-to-all-start.2) | async-done | bytes 2359328 | tf_op jit(solution)/shard_map/all_to_all | solution.py:158
  170.4 4.0 %all-to-all-start.1 = ((bf16[16,2,24,1536]{3,2,1,0:T(8,128)(2,1)}), bf16[16,2,24,1536]{3,2,1,0:T(8,128)(2,1)S(1)}, u32[]{:S(2)}, u32[]{:S(2)}) async-start(bf16[16,2,24,1536]{3,2,1,0:T(8,128)(2,1)} %copy.149), calls=%async_computation.1 | async-start | bytes 4718592 | tf_op jit(solution)/shard_map/all_to_all | solution.py:163
  174.4 6.5 %fusion.7 = f32[2,16,24,768]{3,2,1,0:T(8,128)} fusion(bf16[2,1536,768]{2,1,0:T(8,128)(2,1)} %param.24, bf16[16,2,24,1536]{3,2,1,0:T(8,128)(2,1)} %copy-done.5), kind=kOutput, calls=%fused_computation.12 | convolution fusion | flops 1811939328 | bytes 9437184 | tf_op jit(solution)/shard_map/pekd,edf->pekf/dot_general | solution.py:134
  180.9 10.4 %fusion.21 = bf16[16,2,24,1536]{3,2,0,1:T(8,128)(2,1)} fusion(bf16[2,768,1536]{2,1,0:T(8,128)(2,1)} %param.25, f32[2,16,24,768]{3,2,1,0:T(8,128)} %fusion.7, bf16[2,1536,768]{2,1,0:T(8,128)(2,1)} %param.23, bf16[16,2,24,1536]{3,2,1,0:T(8,128)(2,1)} %copy-done.5), kind=kOutput, calls=%fused_computation.22 | convolution fusion | flops 3626827776 | bytes 16515072 | tf_op jit(solution)/shard_map/pekf,efd->pekd/dot_general | solution.py:136
  191.3 3.4 %copy.154 = bf16[16,2,24,1536]{3,2,1,0:T(8,128)(2,1)} copy(bf16[16,2,24,1536]{3,2,0,1:T(8,128)(2,1)} %fusion.21) | data formatting | bytes 4718592 | tf_op jit(solution)/shard_map/convert_element_type | solution.py:136
  194.7 10.0 %all-to-all-done.1 = bf16[16,2,24,1536]{3,2,1,0:T(8,128)(2,1)S(1)} async-done(((bf16[16,2,24,1536]{3,2,1,0:T(8,128)(2,1)}), bf16[16,2,24,1536]{3,2,1,0:T(8,128)(2,1)S(1)}, u32[]{:S(2)}, u32[]{:S(2)}) %all-to-all-start.1) | async-done | bytes 2359328 | tf_op jit(solution)/shard_map/all_to_all | solution.py:163
  204.7 4.7 %all-to-all-start.3 = ((bf16[16,2,24,1536]{3,2,1,0:T(8,128)(2,1)}), bf16[16,2,24,1536]{3,2,1,0:T(8,128)(2,1)}, u32[]{:S(2)}, u32[]{:S(2)}) async-start(bf16[16,2,24,1536]{3,2,1,0:T(8,128)(2,1)} %copy.154), calls=%async_computation.3 | async-start | bytes 4718592 | tf_op jit(solution)/shard_map/all_to_all | solution.py:163
  216.6 23.3 %all-to-all-done.3 = bf16[16,2,24,1536]{3,2,1,0:T(8,128)(2,1)} async-done(((bf16[16,2,24,1536]{3,2,1,0:T(8,128)(2,1)}), bf16[16,2,24,1536]{3,2,1,0:T(8,128)(2,1)}, u32[]{:S(2)}, u32[]{:S(2)}) %all-to-all-start.3) | async-done | bytes 2359328 | tf_op jit(solution)/shard_map/all_to_all | solution.py:163
  (116 shorter events, 45.8 us)
Async XLA Ops:
  7.2 4.4 %copy-start.3 = (bf16[256,1536]{1,0:T(8,128)(2,1)S(1)}, bf16[256,1536]{1,0:T(8,128)(2,1)}, u32[]{:S(2)}) copy-start(bf16[256,1536]{1,0:T(8,128)(2,1)} %param.16) | copy-start | bytes 2359300
  7.2 4.6 %copy-start.12 = (bf16[192,256]{1,0:T(8,128)(2,1)S(1)}, bf16[192,256]{1,0:T(8,128)(2,1)}, u32[]{:S(2)}) copy-start(bf16[192,256]{1,0:T(8,128)(2,1)} %param.19) | copy-start | bytes 294916
  7.2 19.5 %copy-start.17 = (f32[1536]{0:T(1024)S(1)}, f32[1536]{0:T(1024)}, u32[]{:S(2)}) copy-start(f32[1536]{0:T(1024)} %param.17) | copy-start | bytes 18436
  7.2 55.9 %all-gather.3.cloned.1.call-start = ((), (), s32[]{:S(2)}) async-start(), calls=%async_computation.4 | async-start | bytes 5308416 | tf_op jit(solution)/shard_map/all_gather | solution.py:192
  7.9 76.5 %all-gather.5.cloned.1.call-start = ((), (), s32[]{:S(2)}) async-start(), calls=%async_computation.5 | async-start | bytes 5308416 | tf_op jit(solution)/shard_map/all_gather | solution.py:211
  10.6 16.6 %copy-start.9 = (f32[4,64,64]{2,1,0:T(8,128)}, f32[4,64,64]{2,1,0:T(8,128)S(1)}, u32[]{:S(2)}) copy-start(f32[4,64,64]{2,1,0:T(8,128)S(1)} %get-tuple-element.23) | copy-start | bytes 196612
  11.6 15.7 %copy-start.2 = (bf16[4,1024,512]{2,1,0:T(8,128)(2,1)S(1)}, bf16[4,1024,512]{2,1,0:T(8,128)(2,1)}, u32[]{:S(2)}) copy-start(bf16[4,1024,512]{2,1,0:T(8,128)(2,1)} %param.28) | copy-start | bytes 12582916
  11.8 39.6 %copy-start.16 = (f32[256]{0:T(256)}, f32[256]{0:T(256)S(1)}, u32[]{:S(2)}) copy-start(f32[256]{0:T(256)S(1)} %add_rsqrt_fusion) | copy-start | bytes 3076
  32.4 19.1 %copy-start.18 = (f32[1536]{0:T(1024)S(1)}, f32[1536]{0:T(1024)}, u32[]{:S(2)}) copy-start(f32[1536]{0:T(1024)} %param.17) | copy-start | bytes 18436
  52.5 5.6 %copy-start.14 = (s32[256,4]{0,1:T(4,128)S(1)}, s32[256,4]{0,1:T(4,128)}, u32[]{:S(2)}) copy-start(s32[256,4]{0,1:T(4,128)} %param.26) | copy-start | bytes 12292
  67.5 2.7 %copy-start.10 = (pred[4,64,64]{1,2,0:T(8,128)(4,1)S(1)}, pred[4,64,64]{1,2,0:T(8,128)(4,1)}, u32[]{:S(2)}) copy-start(pred[4,64,64]{1,2,0:T(8,128)(4,1)} %copy.134) | copy-start | bytes 49156
  73.5 3.1 %copy-start.11 = (bf16[4,64,2,128]{3,2,1,0:T(2,128)(2,1)S(1)}, bf16[4,64,2,128]{3,2,1,0:T(2,128)(2,1)}, u32[]{:S(2)}) copy-start(bf16[4,64,2,128]{3,2,1,0:T(2,128)(2,1)} %reshape.232) | copy-start | bytes 393220
  76.7 1.7 copy-start.6
  82.3 2.1 copy-start.4
  83.1 5.4 %copy-start.8 = (bf16[768,128]{1,0:T(8,128)(2,1)S(1)}, bf16[768,128]{1,0:T(8,128)(2,1)}, u32[]{:S(2)}) copy-start(bf16[768,128]{1,0:T(8,128)(2,1)} %copy.146) | copy-start | bytes 589828
  83.1 5.4 %copy-start.13 = (f32[1536]{0:T(1024)S(1)}, f32[1536]{0:T(1024)}, u32[]{:S(2)}) copy-start(f32[1536]{0:T(1024)} %param.22) | copy-start | bytes 18436
  90.8 40.5 %all-to-all-start = ((bf16[16,2,24,1536]{3,2,1,0:T(8,128)(2,1)}), bf16[16,2,24,1536]{3,2,1,0:T(8,128)(2,1)}, u32[]{:S(2)}, u32[]{:S(2)}) async-start(bf16[16,2,24,1536]{3,2,1,0:T(8,128)(2,1)} %fusion.81), calls=%async_computation | async-start | bytes 4718592 | tf_op jit(solution)/shard_map/all_to_all | solution.py:158
  131.3 37.6 %all-to-all-start.2 = ((bf16[16,2,24,1536]{3,2,1,0:T(8,128)(2,1)}), bf16[16,2,24,1536]{3,2,1,0:T(8,128)(2,1)S(1)}, u32[]{:S(2)}, u32[]{:S(2)}) async-start(bf16[16,2,24,1536]{3,2,1,0:T(8,128)(2,1)} %fusion.84), calls=%async_computation.2 | async-start | bytes 4718592 | tf_op jit(solution)/shard_map/all_to_all | solution.py:158
  170.4 34.3 %all-to-all-start.1 = ((bf16[16,2,24,1536]{3,2,1,0:T(8,128)(2,1)}), bf16[16,2,24,1536]{3,2,1,0:T(8,128)(2,1)S(1)}, u32[]{:S(2)}, u32[]{:S(2)}) async-start(bf16[16,2,24,1536]{3,2,1,0:T(8,128)(2,1)} %copy.149), calls=%async_computation.1 | async-start | bytes 4718592 | tf_op jit(solution)/shard_map/all_to_all | solution.py:163
  194.7 14.7 %copy-start.19 = (s32[4]{0:T(128)S(1)}, s32[4]{0:T(128)}, u32[]{:S(2)}) copy-start(s32[4]{0:T(128)} %param.31) | copy-start | bytes 52
  194.7 17.1 %copy-start.15 = (f32[256,4]{0,1:T(4,128)S(1)}, f32[256,4]{0,1:T(4,128)}, u32[]{:S(2)}) copy-start(f32[256,4]{0,1:T(4,128)} %param.27) | copy-start | bytes 12292
  204.7 35.2 %all-to-all-start.3 = ((bf16[16,2,24,1536]{3,2,1,0:T(8,128)(2,1)}), bf16[16,2,24,1536]{3,2,1,0:T(8,128)(2,1)}, u32[]{:S(2)}, u32[]{:S(2)}) async-start(bf16[16,2,24,1536]{3,2,1,0:T(8,128)(2,1)} %copy.154), calls=%async_computation.3 | async-start | bytes 4718592 | tf_op jit(solution)/shard_map/all_to_all | solution.py:163
  216.6 25.5 %copy-start.1 = (f32[128,1536]{1,0:T(8,128)S(1)}, f32[128,1536]{1,0:T(8,128)}, u32[]{:S(2)}) copy-start(f32[128,1536]{1,0:T(8,128)} %copy-done) | copy-start | bytes 2359300
  242.1 2.2 copy-start.7
  (2 other events, 2.3 us)
Sparse Core Ops, SparseCore 0:
  9.7 38.1 all-gather.2
  49.6 34.7 all-gather.4

commit v4 on v3

--- a/solution.py
+++ b/solution.py
@@ -109,23 +109,27 @@
     )
 
 
-def slot_tables(routes, capacity):
+def slot_tables(routes, gate_weights, capacity):
     rows = routes.shape[0]
     expert_ids = jnp.arange(EXPERTS, dtype=jnp.int32)
     picks = routes[:, :, None] == expert_ids[None, None, :]
     chosen = jnp.sum(picks.astype(jnp.int32), axis=1).astype(jnp.bfloat16)
     row_ids = jnp.arange(rows, dtype=jnp.int32)
-    before = (row_ids[None, :] < row_ids[:, None]).astype(jnp.bfloat16)
+    same_block = (row_ids[None, :] // BLOCK_ROWS) == (row_ids[:, None] // BLOCK_ROWS)
+    before = ((row_ids[None, :] < row_ids[:, None]) & same_block).astype(jnp.bfloat16)
     earlier = jnp.dot(before, chosen, preferred_element_type=jnp.float32).astype(jnp.int32)
     slot_number = jnp.sum(jnp.where(picks, earlier[:, None, :], 0), axis=2)
     slot_index = routes * capacity + slot_number
     slot_ids = jnp.arange(EXPERTS * capacity, dtype=jnp.int32)
     hit = slot_index[:, :, None] == slot_ids[None, None, :]
-    return hit
-
-
-def pack_slots(token_rows, hit):
     place = jnp.sum(hit.astype(jnp.bfloat16), axis=1)
+    weight = jnp.sum(jnp.where(hit, gate_weights[:, :, None], 0.0), axis=1)
+    weight_hi = weight.astype(jnp.bfloat16)
+    weight_lo = (weight - weight_hi.astype(jnp.float32)).astype(jnp.bfloat16)
+    return place, weight_hi, weight_lo
+
+
+def pack_slots(token_rows, place):
     return jnp.einsum("ts,td->sd", place, token_rows, preferred_element_type=jnp.bfloat16)
 
 
@@ -138,20 +142,18 @@
     )
 
 
-def combine_picks(returned_rows, hit, gate_weights):
+def combine_picks(returned_rows, weight_hi, weight_lo):
     layer_width = returned_rows.shape[-1]
+    rows = weight_hi.shape[0]
     flat_rows = returned_rows.reshape(-1, layer_width)
-    weight = jnp.sum(jnp.where(hit, gate_weights[:, :, None], 0.0), axis=1)
-    weight_hi = weight.astype(jnp.bfloat16)
-    weight_lo = (weight - weight_hi.astype(jnp.float32)).astype(jnp.bfloat16)
-    mixed = jnp.dot(weight_hi, flat_rows, preferred_element_type=jnp.float32)
-    return mixed + jnp.dot(weight_lo, flat_rows, preferred_element_type=jnp.float32)
-
-
-def routed_whole(moe_in, routes, gate_weights, w_gate, w_up, w_down):
-    capacity = CAP * (moe_in.shape[0] // BLOCK_ROWS)
-    hit = slot_tables(routes, capacity)
-    buffer = pack_slots(moe_in, hit)
+    both = jnp.concatenate([weight_hi, weight_lo], axis=0)
+    mixed = jnp.dot(both, flat_rows, preferred_element_type=jnp.float32)
+    return mixed[:rows] + mixed[rows:]
+
+
+def routed_whole(moe_in, place, weight_hi, weight_lo, w_gate, w_up, w_down):
+    capacity = place.shape[1] // EXPERTS
+    buffer = pack_slots(moe_in, place)
     peer_count = lax.axis_size("exp")
     reshaped_rows = buffer.reshape(peer_count, w_gate.shape[0], capacity, moe_in.shape[1])
     produced = expert_products(
@@ -161,7 +163,7 @@
         w_down,
     )
     returned_rows = lax.all_to_all(produced, "exp", split_axis=0, concat_axis=0, tiled=True)
-    return combine_picks(returned_rows, hit, gate_weights)
+    return combine_picks(returned_rows, weight_hi, weight_lo)
 
 
 def local(
@@ -213,13 +215,16 @@
     context_all = jax.vmap(attend)(
         query_req, key_value_request, kv_cache, lengths, closure
     ).reshape(rows_here, -1)
+    place, weight_hi, weight_lo = slot_tables(routes, gate_weights, CAP)
     outs = []
     for chunk in range(chunk_count):
         rw = slice(chunk * BLOCK_ROWS, (chunk + 1) * BLOCK_ROWS)
         attn_out = jnp.dot(context_all[rw], w_out_full, preferred_element_type=jnp.float32)
         residual = (tokens[rw].astype(jnp.float32) + attn_out).astype(jnp.bfloat16)
         moe_in = rms_scale(residual, moe_gain)
-        mixed = routed_whole(moe_in, routes[rw], gate_weights[rw], w_gate, w_up, w_down)
+        mixed = routed_whole(
+            moe_in, place[rw], weight_hi[rw], weight_lo[rw], w_gate, w_up, w_down
+        )
         outs.append((residual.astype(jnp.float32) + mixed).astype(jnp.bfloat16))
     layer_out = jnp.concatenate(outs, axis=0)
     new_entries = compact(key_value_request, closure, tree_depth, accepted)

time: 253 us -> 251 us (level)
  waiting for transfers between devices: 73.3 us -> 77 us
  matrix products: 70.1 us -> 67 us
    all_to_all x2, waiting for transfers between devices: 33.3 us -> 36.3 us  [routed_whole(): lax.all_to_all(produced, 'exp', split_axis=0, concat_axis=0, tiled=True)]
    dot_general x4 -> x2, matrix products: 6.12 us -> 3.2 us  [combine_picks(): mixed = jnp.dot(both, flat_rows, preferred_element_type=jnp.float32)]
    unnamed x45 -> x53, local copies, waits for them, and re-layouts: 10.7 us -> 10.8 us
  transfers between devices with their start and end apart: 6 -> 6, of which waited for: 5 -> 5; matrix products, arithmetic and copies ran while one was open for 39% -> 37% of each run, Pallas kernels for 0% -> 0%
where the time goes in v4:
time: 251 us; the launch traced here: 250 us
  waiting for transfers between devices  77 us (31%)
  matrix products  67 us (27%)
  blocking collectives  30.9 us (12%)
  local copies, waits for them, and re-layouts  30.2 us (12%)
  starting transfers between devices  21 us (8%)
  between operations  14.6 us (6%)
  other arithmetic  9.53 us (4%)
    all_to_all x2, waiting for transfers between devices, routed_whole(): lax.all_to_all(reshaped_rows, 'exp', split_axis=0, concat_axis=0, tiled=T...  37.7 us
    all_to_all x2, waiting for transfers between devices, routed_whole(): lax.all_to_all(produced, 'exp', split_axis=0, concat_axis=0, tiled=True)  36.3 us
    dot_general x2, matrix products, expert_products(): jnp.einsum('pekf,efd->pekd', hidden, w_down, preferred_element_type=jnp.f...  20.8 us
    all_gather x1, blocking collectives, local(): lax.all_gather(key_projection, 'req', axis=0, tiled=True)  15.6 us
    all_gather x1, blocking collectives, local(): lax.all_gather(value_projection, 'req', axis=0, tiled=True)  15.3 us
    dot_general x2, matrix products, expert_products(): jnp.einsum('pekd,edf->pekf', received, w_up, preferred_element_type=jnp.f...  13 us
    all_to_all x2, starting transfers between devices, routed_whole(): lax.all_to_all(reshaped_rows, 'exp', split_axis=0, concat_axis=0, tiled=T...  12.2 us
    unnamed x53, local copies, waits for them, and re-layouts  10.8 us
  transfers between devices with their start and end apart: 6, of which 5 were waited for; matrix products, arithmetic and copies ran while one was open for 37% of the time, Pallas kernels for 0%

profile of v4, /device:TPU:0, one launch (start us, length us, event | category | flops | bytes accessed | tf_op | source)
XLA Modules:
  0.0 250.2 jit_solution(5174756153162118243)
XLA Ops:
  13.0 15.6 %all_gather.13 = bf16[1536,256]{1,0:T(8,128)(2,1)S(1)} all-gather(bf16[192,256]{1,0:T(8,128)(2,1)S(1)} %copy-done.16), channel_id=1, replica_groups=mesh['req'=8,'exp'=16] {'req'}, dimensions={0}, use_global_device_ids=true | all-gather | bytes 884736 | tf_op jit(solution)/shard_map/all_gather | solution.py:199
  30.2 4.6 %fusion.137 = (bf16[4,1024,256]{2,1,0:T(8,128)(2,1)}, bf16[4,1024,256]{2,1,0:T(8,128)(2,1)}) fusion(bf16[4,1024,512]{2,1,0:T(8,128)(2,1)} %param.28), kind=kLoop, calls=%fused_computation.165 | loop fusion | bytes 8388608 | tf_op jit(solution)/shard_map/vmap()/slice | solution.py:62
  34.8 3.0 %copy.161 = bf16[4,1024,256]{1,2,0:T(8,128)(2,1)S(1)} copy(bf16[4,1024,256]{2,1,0:T(8,128)(2,1)} %get-tuple-element.5) | data formatting | bytes 4194304
  37.8 15.3 %all_gather.14 = bf16[1536,256]{1,0:T(8,128)(2,1)S(1)} all-gather(bf16[192,256]{1,0:T(8,128)(2,1)} %param.20), channel_id=1, replica_groups=mesh['req'=8,'exp'=16] {'req'}, dimensions={0}, use_global_device_ids=true | all-gather | bytes 884736 | tf_op jit(solution)/shard_map/all_gather | solution.py:204
  56.5 4.0 %copy.164 = bf16[4,1024,256]{1,2,0:T(8,128)(2,1)} copy(bf16[4,1024,256]{2,1,0:T(8,128)(2,1)} %get-tuple-element.4) | data formatting | bytes 4194304
  62.6 4.4 %fusion.135 = f32[256,1536]{0,1:T(8,128)S(1)} fusion(bf16[1536,1536]{1,0:T(8,128)(2,1)} %all-gather.3.cloned.1.call-done, bf16[256,1536]{1,0:T(8,128)(2,1)S(1)} %copy-done.2, f32[1536]{0:T(1024)} %param.17, f32[256]{0:T(256)} %copy-done.21), kind=kOutput, calls=%fused_computation.164 | convolution fusion | flops 1209532416 | bytes 7085056 | tf_op jit(solution)/shard_map/dot_general | solution.py:192
  73.1 3.1 %fusion.1 = f32[4,2,6,64]{3,2,1,0:T(8,128)S(1)} fusion(f32[4,2,64,6,1024]{4,2,3,1,0:T(8,128)S(1)} %get-tuple-element.25, f32[4,2,6,64]{3,2,1,0:T(8,128)S(1)} %max.25, pred[4,1024]{1,0:T(4,128)(4,1)S(1)} %iota_compare_fusion.8), kind=kLoop, calls=%fused_computation.6 | loop fusion | flops 12579840 | bytes 12611584 | tf_op jit(solution)/shard_map/vmap()/reduce_sum | solution.py:87
  77.8 3.9 %fusion.40 = bf16[4,64,2,6,128]{4,1,3,2,0:T(8,128)(2,1)S(1)} fusion(f32[4,2,128,6,64]{2,4,3,1,0:T(8,128)S(1)} %fusion.74, bf16[4,1024,2,128,1]{1,3,4,2,0:T(8,128)(2,1)S(1)} %bitcast.120, f32[4,2,64,6,1024]{4,2,3,1,0:T(8,128)S(1)} %get-tuple-element.25, f32[4,2,6,64]{3,2,1,0:T(8,128)S(1)} %add.113, f32[4,2,6,64]{3,2,1,0:T(8,128)S(1)} %max.25, ...), kind=kOutput, calls=%fused_computation.46 | convolution fusion | flops 821821440 | bytes 17068032 | tf_op jit(solution)/shard_map/vmap(gsij,jgd->igsd)/dot_general | solution.py:92
  84.3 4.1 %multiply_reduce_fusion.1 = (f32[128]{0:T(128)S(1)}, f32[128,1536]{1,0:T(8,128)S(1)}) fusion(bf16[128,1536]{1,0:T(8,128)(2,1)S(1)} %slice.78, bf16[1536,1536]{0,1:T(8,128)(2,1)} %all-gather.5.cloned.1.call-done, bf16[256,1536]{1,0:T(8,128)(2,1)S(1)} %copy-done.3), kind=kOutput, calls=%fused_computation.75 | convolution fusion | flops 605159296 | bytes 6291968 | tf_op jit(solution)/shard_map/dot_general | solution.py:222
  90.7 6.9 %all-to-all-start = ((bf16[16,2,24,1536]{3,2,1,0:T(8,128)(2,1)}), bf16[16,2,24,1536]{3,2,1,0:T(8,128)(2,1)}, u32[]{:S(2)}, u32[]{:S(2)}) async-start(bf16[16,2,24,1536]{3,2,1,0:T(8,128)(2,1)} %bitcast.14), calls=%async_computation | async-start | bytes 4718592 | tf_op jit(solution)/shard_map/all_to_all | solution.py:160
  98.3 4.1 %multiply_reduce_fusion = (f32[128]{0:T(128)S(1)}, f32[128,1536]{1,0:T(8,128)S(1)}) fusion(bf16[128,1536]{1,0:T(8,128)(2,1)S(1)} %slice.86, bf16[1536,1536]{0,1:T(8,128)(2,1)} %all-gather.5.cloned.1.call-done, bf16[256,1536]{1,0:T(8,128)(2,1)S(1)} %copy-done.3), kind=kOutput, calls=%fused_computation.73 | convolution fusion | flops 605159296 | bytes 6291968 | tf_op jit(solution)/shard_map/dot_general | solution.py:222
  105.5 25.7 %all-to-all-done = bf16[16,2,24,1536]{3,2,1,0:T(8,128)(2,1)} async-done(((bf16[16,2,24,1536]{3,2,1,0:T(8,128)(2,1)}), bf16[16,2,24,1536]{3,2,1,0:T(8,128)(2,1)}, u32[]{:S(2)}, u32[]{:S(2)}) %all-to-all-start) | async-done | bytes 2359328 | tf_op jit(solution)/shard_map/all_to_all | solution.py:160
  131.2 5.3 %all-to-all-start.2 = ((bf16[16,2,24,1536]{3,2,1,0:T(8,128)(2,1)}), bf16[16,2,24,1536]{3,2,1,0:T(8,128)(2,1)S(1)}, u32[]{:S(2)}, u32[]{:S(2)}) async-start(bf16[16,2,24,1536]{3,2,1,0:T(8,128)(2,1)} %bitcast.24), calls=%async_computation.2 | async-start | bytes 4718592 | tf_op jit(solution)/shard_map/all_to_all | solution.py:160
  136.6 6.5 %fusion.9 = f32[2,16,24,768]{3,2,1,0:T(8,128)} fusion(bf16[2,1536,768]{2,1,0:T(8,128)(2,1)} %param.24, bf16[16,2,24,1536]{3,2,1,0:T(8,128)(2,1)} %all-to-all-done), kind=kOutput, calls=%fused_computation.14 | convolution fusion | flops 1811939328 | bytes 9437184 | tf_op jit(solution)/shard_map/pekd,edf->pekf/dot_general | solution.py:138
  143.1 10.4 %fusion.25 = bf16[16,2,24,1536]{3,2,0,1:T(8,128)(2,1)} fusion(bf16[2,768,1536]{2,1,0:T(8,128)(2,1)} %param.25, f32[2,16,24,768]{3,2,1,0:T(8,128)} %fusion.9, bf16[2,1536,768]{2,1,0:T(8,128)(2,1)} %param.23, bf16[16,2,24,1536]{3,2,1,0:T(8,128)(2,1)} %all-to-all-done), kind=kOutput, calls=%fused_computation.26 | convolution fusion | flops 3626827776 | bytes 16515072 | tf_op jit(solution)/shard_map/pekf,efd->pekd/dot_general | solution.py:140
  153.5 3.4 %copy.136 = bf16[16,2,24,1536]{3,2,1,0:T(8,128)(2,1)} copy(bf16[16,2,24,1536]{3,2,0,1:T(8,128)(2,1)} %fusion.25) | data formatting | bytes 4718592 | tf_op jit(solution)/shard_map/convert_element_type | solution.py:140
  156.9 12.0 %all-to-all-done.2 = bf16[16,2,24,1536]{3,2,1,0:T(8,128)(2,1)S(1)} async-done(((bf16[16,2,24,1536]{3,2,1,0:T(8,128)(2,1)}), bf16[16,2,24,1536]{3,2,1,0:T(8,128)(2,1)S(1)}, u32[]{:S(2)}, u32[]{:S(2)}) %all-to-all-start.2) | async-done | bytes 2359328 | tf_op jit(solution)/shard_map/all_to_all | solution.py:160
  170.3 4.0 %all-to-all-start.1 = ((bf16[16,2,24,1536]{3,2,1,0:T(8,128)(2,1)}), bf16[16,2,24,1536]{3,2,1,0:T(8,128)(2,1)S(1)}, u32[]{:S(2)}, u32[]{:S(2)}) async-start(bf16[16,2,24,1536]{3,2,1,0:T(8,128)(2,1)} %copy.136), calls=%async_computation.1 | async-start | bytes 4718592 | tf_op jit(solution)/shard_map/all_to_all | solution.py:165
  176.1 6.5 %fusion.7 = f32[2,16,24,768]{3,2,1,0:T(8,128)} fusion(bf16[2,1536,768]{2,1,0:T(8,128)(2,1)} %param.24, bf16[16,2,24,1536]{3,2,1,0:T(8,128)(2,1)} %copy-done.4), kind=kOutput, calls=%fused_computation.12 | convolution fusion | flops 1811939328 | bytes 9437184 | tf_op jit(solution)/shard_map/pekd,edf->pekf/dot_general | solution.py:138
  182.6 10.4 %fusion.22 = bf16[16,2,24,1536]{3,2,0,1:T(8,128)(2,1)} fusion(bf16[2,768,1536]{2,1,0:T(8,128)(2,1)} %param.25, f32[2,16,24,768]{3,2,1,0:T(8,128)} %fusion.7, bf16[2,1536,768]{2,1,0:T(8,128)(2,1)} %param.23, bf16[16,2,24,1536]{3,2,1,0:T(8,128)(2,1)} %copy-done.4), kind=kOutput, calls=%fused_computation.25 | convolution fusion | flops 3626827776 | bytes 16515072 | tf_op jit(solution)/shard_map/pekf,efd->pekd/dot_general | solution.py:140
  193.0 3.4 %copy.140 = bf16[16,2,24,1536]{3,2,1,0:T(8,128)(2,1)} copy(bf16[16,2,24,1536]{3,2,0,1:T(8,128)(2,1)} %fusion.22) | data formatting | bytes 4718592 | tf_op jit(solution)/shard_map/convert_element_type | solution.py:140
  196.4 8.2 %all-to-all-done.1 = bf16[16,2,24,1536]{3,2,1,0:T(8,128)(2,1)S(1)} async-done(((bf16[16,2,24,1536]{3,2,1,0:T(8,128)(2,1)}), bf16[16,2,24,1536]{3,2,1,0:T(8,128)(2,1)S(1)}, u32[]{:S(2)}, u32[]{:S(2)}) %all-to-all-start.1) | async-done | bytes 2359328 | tf_op jit(solution)/shard_map/all_to_all | solution.py:165
  204.6 4.7 %all-to-all-start.3 = ((bf16[16,2,24,1536]{3,2,1,0:T(8,128)(2,1)}), bf16[16,2,24,1536]{3,2,1,0:T(8,128)(2,1)}, u32[]{:S(2)}, u32[]{:S(2)}) async-start(bf16[16,2,24,1536]{3,2,1,0:T(8,128)(2,1)} %copy.140), calls=%async_computation.3 | async-start | bytes 4718592 | tf_op jit(solution)/shard_map/all_to_all | solution.py:165
  211.7 28.1 %all-to-all-done.3 = bf16[16,2,24,1536]{3,2,1,0:T(8,128)(2,1)} async-done(((bf16[16,2,24,1536]{3,2,1,0:T(8,128)(2,1)}), bf16[16,2,24,1536]{3,2,1,0:T(8,128)(2,1)}, u32[]{:S(2)}, u32[]{:S(2)}) %all-to-all-start.3) | async-done | bytes 2359328 | tf_op jit(solution)/shard_map/all_to_all | solution.py:165
  (119 shorter events, 38.0 us)
Async XLA Ops:
  7.2 5.6 %copy-start.2 = (bf16[256,1536]{1,0:T(8,128)(2,1)S(1)}, bf16[256,1536]{1,0:T(8,128)(2,1)}, u32[]{:S(2)}) copy-start(bf16[256,1536]{1,0:T(8,128)(2,1)} %param.16) | copy-start | bytes 2359300
  7.2 5.8 %copy-start.16 = (bf16[192,256]{1,0:T(8,128)(2,1)S(1)}, bf16[192,256]{1,0:T(8,128)(2,1)}, u32[]{:S(2)}) copy-start(bf16[192,256]{1,0:T(8,128)(2,1)} %param.19) | copy-start | bytes 294916
  7.2 21.4 %copy-start.22 = (f32[1536]{0:T(1024)S(1)}, f32[1536]{0:T(1024)}, u32[]{:S(2)}) copy-start(f32[1536]{0:T(1024)} %param.17) | copy-start | bytes 18436
  7.2 55.4 %all-gather.3.cloned.1.call-start = ((), (), s32[]{:S(2)}) async-start(), calls=%async_computation.4 | async-start | bytes 5308416 | tf_op jit(solution)/shard_map/all_gather | solution.py:194
  7.9 76.4 %all-gather.5.cloned.1.call-start = ((), (), s32[]{:S(2)}) async-start(), calls=%async_computation.5 | async-start | bytes 5308416 | tf_op jit(solution)/shard_map/all_gather | solution.py:213
  11.9 17.3 %copy-start.8 = (f32[256,64]{0,1:T(8,128)}, f32[256,64]{0,1:T(8,128)S(1)}, u32[]{:S(2)}) copy-start(f32[256,64]{0,1:T(8,128)S(1)} %get-tuple-element.20) | copy-start | bytes 196612
  11.9 17.3 %copy-start.10 = (f32[256,64]{0,1:T(8,128)}, f32[256,64]{0,1:T(8,128)S(1)}, u32[]{:S(2)}) copy-start(f32[256,64]{0,1:T(8,128)S(1)} %get-tuple-element.21) | copy-start | bytes 196612
  13.0 40.1 %copy-start.21 = (f32[256]{0:T(256)}, f32[256]{0:T(256)S(1)}, u32[]{:S(2)}) copy-start(f32[256]{0:T(256)S(1)} %add_rsqrt_fusion) | copy-start | bytes 3076
  54.9 5.7 %copy-start.17 = (s32[256,4]{0,1:T(4,128)S(1)}, s32[256,4]{0,1:T(4,128)}, u32[]{:S(2)}) copy-start(s32[256,4]{0,1:T(4,128)} %param.26) | copy-start | bytes 12292
  56.5 6.0 %copy-start.20 = (s32[4]{0:T(128)S(1)}, s32[4]{0:T(128)}, u32[]{:S(2)}) copy-start(s32[4]{0:T(128)} %param.29) | copy-start | bytes 52
  61.7 8.0 %copy-start.6 = (bf16[256,2,128]{2,0,1:T(8,128)(2,1)}, bf16[256,2,128]{2,0,1:T(8,128)(2,1)S(1)}, u32[]{:S(2)}) copy-start(bf16[256,2,128]{2,0,1:T(8,128)(2,1)S(1)} %pad_maximum_fusion.2) | copy-start | bytes 393220
  62.6 4.4 %copy-start.9 = (f32[256,64]{0,1:T(8,128)S(1)}, f32[256,64]{0,1:T(8,128)}, u32[]{:S(2)}) copy-start(f32[256,64]{0,1:T(8,128)} %copy-done.8) | copy-start | bytes 196612
  62.6 4.5 %copy-start.11 = (f32[256,64]{0,1:T(8,128)S(1)}, f32[256,64]{0,1:T(8,128)}, u32[]{:S(2)}) copy-start(f32[256,64]{0,1:T(8,128)} %copy-done.10) | copy-start | bytes 196612
  73.1 3.1 %copy-start.15 = (bf16[4,64,2,128]{3,2,1,0:T(2,128)(2,1)S(1)}, bf16[4,64,2,128]{3,2,1,0:T(2,128)(2,1)}, u32[]{:S(2)}) copy-start(bf16[4,64,2,128]{3,2,1,0:T(2,128)(2,1)} %reshape.304) | copy-start | bytes 393220
  82.6 5.8 %copy-start.18 = (f32[1536]{0:T(1024)S(1)}, f32[1536]{0:T(1024)}, u32[]{:S(2)}) copy-start(f32[1536]{0:T(1024)} %param.22) | copy-start | bytes 18436
  90.7 40.5 %all-to-all-start = ((bf16[16,2,24,1536]{3,2,1,0:T(8,128)(2,1)}), bf16[16,2,24,1536]{3,2,1,0:T(8,128)(2,1)}, u32[]{:S(2)}, u32[]{:S(2)}) async-start(bf16[16,2,24,1536]{3,2,1,0:T(8,128)(2,1)} %bitcast.14), calls=%async_computation | async-start | bytes 4718592 | tf_op jit(solution)/shard_map/all_to_all | solution.py:160
  131.2 37.6 %all-to-all-start.2 = ((bf16[16,2,24,1536]{3,2,1,0:T(8,128)(2,1)}), bf16[16,2,24,1536]{3,2,1,0:T(8,128)(2,1)S(1)}, u32[]{:S(2)}, u32[]{:S(2)}) async-start(bf16[16,2,24,1536]{3,2,1,0:T(8,128)(2,1)} %bitcast.24), calls=%async_computation.2 | async-start | bytes 4718592 | tf_op jit(solution)/shard_map/all_to_all | solution.py:160
  156.9 17.4 %copy-start.7 = (bf16[256,2,128]{2,0,1:T(8,128)(2,1)S(1)}, bf16[256,2,128]{2,0,1:T(8,128)(2,1)}, u32[]{:S(2)}) copy-start(bf16[256,2,128]{2,0,1:T(8,128)(2,1)} %copy-done.6) | copy-start | bytes 393220
  156.9 17.7 %copy-start.23 = (s32[4]{0:T(128)S(1)}, s32[4]{0:T(128)}, u32[]{:S(2)}) copy-start(s32[4]{0:T(128)} %param.31) | copy-start | bytes 52
  170.3 34.3 %all-to-all-start.1 = ((bf16[16,2,24,1536]{3,2,1,0:T(8,128)(2,1)}), bf16[16,2,24,1536]{3,2,1,0:T(8,128)(2,1)S(1)}, u32[]{:S(2)}, u32[]{:S(2)}) async-start(bf16[16,2,24,1536]{3,2,1,0:T(8,128)(2,1)} %copy.136), calls=%async_computation.1 | async-start | bytes 4718592 | tf_op jit(solution)/shard_map/all_to_all | solution.py:165
  196.4 12.9 %copy-start.19 = (f32[256,4]{0,1:T(4,128)S(1)}, f32[256,4]{0,1:T(4,128)}, u32[]{:S(2)}) copy-start(f32[256,4]{0,1:T(4,128)} %param.27) | copy-start | bytes 12292
  196.4 13.3 %copy-start.14 = (bf16[256,256]{1,0:T(8,128)(2,1)S(1)}, bf16[256,256]{1,0:T(8,128)(2,1)}, u32[]{:S(2)}) copy-start(bf16[256,256]{1,0:T(8,128)(2,1)} %convolution_convert_fusion.1) | copy-start | bytes 393220
  204.6 35.2 %all-to-all-start.3 = ((bf16[16,2,24,1536]{3,2,1,0:T(8,128)(2,1)}), bf16[16,2,24,1536]{3,2,1,0:T(8,128)(2,1)}, u32[]{:S(2)}, u32[]{:S(2)}) async-start(bf16[16,2,24,1536]{3,2,1,0:T(8,128)(2,1)} %copy.140), calls=%async_computation.3 | async-start | bytes 4718592 | tf_op jit(solution)/shard_map/all_to_all | solution.py:165
  211.7 30.6 %copy-start.1 = (f32[128,1536]{1,0:T(8,128)S(1)}, f32[128,1536]{1,0:T(8,128)}, u32[]{:S(2)}) copy-start(f32[128,1536]{1,0:T(8,128)} %copy-done) | copy-start | bytes 2359300
  (6 other events, 9.7 us)
Sparse Core Ops, SparseCore 0:
  9.7 38.5 all-gather.2
  50.0 34.2 all-gather.4

commit v5 on v4

--- a/solution.py
+++ b/solution.py
@@ -164,6 +164,30 @@
     )
     returned_rows = lax.all_to_all(produced, "exp", split_axis=0, concat_axis=0, tiled=True)
     return combine_picks(returned_rows, weight_hi, weight_lo)
+
+
+def plane_shift(piece, shift, plane_count, core_count):
+    pairs = [
+        (p * core_count + c, ((p + shift) % plane_count) * core_count + c)
+        for p in range(plane_count)
+        for c in range(core_count)
+    ]
+    return lax.ppermute(piece, "req", pairs)
+
+
+def balanced_gather(shard, plane_count, core_count):
+    half = shard.shape[1] // 2
+    from_below = plane_shift(shard, 1, plane_count, core_count)
+    from_above = plane_shift(shard, plane_count - 1, plane_count, core_count)
+    far_low = plane_shift(from_below[:, :half], 1, plane_count, core_count)
+    far_high = plane_shift(from_above[:, half:], plane_count - 1, plane_count, core_count)
+    mine = jnp.concatenate([shard, from_below, far_low, far_high, from_above], axis=1)
+    swap = [
+        (p * core_count + c, p * core_count + (core_count - 1 - c))
+        for p in range(plane_count)
+        for c in range(core_count)
+    ]
+    return jnp.concatenate([mine, lax.ppermute(mine, "req", swap)], axis=1)
 
 
 def local(
@@ -210,7 +234,13 @@
     )
     query_req = query_rows.reshape(local_reqs, DRAFT_TOKENS, query_rows.shape[1])
     key_value_request = tree_key_value.reshape(local_reqs, DRAFT_TOKENS, tree_key_value.shape[1])
-    w_out_full = lax.all_gather(w_out, "req", axis=1, tiled=True)
+    core_count = 2
+    plane_count = lax.axis_size("req") // core_count
+    place_req = lax.axis_index("req")
+    plane_me, core_me = place_req // core_count, place_req % core_count
+    plane_order = (plane_me - jnp.arange(plane_count, dtype=jnp.int32)) % plane_count
+    out_cols = w_out.shape[1]
+    w_out_full = balanced_gather(w_out, plane_count, core_count)
     chunk_count = rows_here // BLOCK_ROWS
     context_all = jax.vmap(attend)(
         query_req, key_value_request, kv_cache, lengths, closure
@@ -219,7 +249,13 @@
     outs = []
     for chunk in range(chunk_count):
         rw = slice(chunk * BLOCK_ROWS, (chunk + 1) * BLOCK_ROWS)
-        attn_out = jnp.dot(context_all[rw], w_out_full, preferred_element_type=jnp.float32)
+        attn_rel = jnp.dot(
+            context_all[rw], w_out_full, preferred_element_type=jnp.float32
+        ).reshape(BLOCK_ROWS, core_count, plane_count, out_cols)
+        attn_rel = jnp.where(core_me == 0, attn_rel, attn_rel[:, ::-1])
+        attn_out = (
+            jnp.take(attn_rel, plane_order, axis=2).transpose(0, 2, 1, 3).reshape(BLOCK_ROWS, -1)
+        )
         residual = (tokens[rw].astype(jnp.float32) + attn_out).astype(jnp.bfloat16)
         moe_in = rms_scale(residual, moe_gain)
         mixed = routed_whole(

time: 251 us -> 288 us (1.15)
  local copies, waits for them, and re-layouts: 30.2 us -> 44.8 us
  starting transfers between devices: 21 us -> 29.4 us
  waiting for transfers between devices: 77 us -> 83.4 us
  other arithmetic: 9.53 us -> 14 us
  blocking collectives: 30.9 us -> 35.1 us
    unnamed x53 -> x75, local copies, waits for them, and re-layouts: 10.8 us -> 18.8 us
    ppermute x0 -> x5, starting transfers between devices: none -> 7.98 us  [the longest x4 7.98 us: plane_shift(): return lax.ppermute(piece, 'req', pairs)]
    all_gather x1, blocking collectives: 15.6 us -> 21.5 us  [local(): lax.all_gather(key_projection, 'req', axis=0, tiled=True)]
    all_to_all x2, waiting for transfers between devices: 37.7 us -> 43.3 us  [routed_whole(): lax.all_to_all(reshaped_rows, 'exp', split_axis=0, concat_axis=0, tiled=T...]
    concatenate x0 -> x2, local copies, waits for them, and re-layouts: none -> 4.4 us  [the longest x1 3.3 us: balanced_gather(): return jnp.concatenate([mine, lax.ppermute(mine, 'req', swap)], axis=1)]
    ppermute x0 -> x5, waiting for transfers between devices: none -> 3.68 us  [the longest x4 3.68 us: plane_shift(): return lax.ppermute(piece, 'req', pairs)]
  transfers between devices with their start and end apart: 6 -> 10, of which waited for: 5 -> 5; matrix products, arithmetic and copies ran while one was open for 37% -> 29% of each run, Pallas kernels for 0% -> 0%
where the time goes in v5:
time: 288 us; the launch traced here: 287 us
  waiting for transfers between devices  83.4 us (29%)
  matrix products  65.9 us (23%)
  local copies, waits for them, and re-layouts  44.8 us (16%)
  blocking collectives  35.1 us (12%)
  starting transfers between devices  29.4 us (10%)
  between operations  14.7 us (5%)
  other arithmetic  14 us (5%)
    all_to_all x2, waiting for transfers between devices, routed_whole(): lax.all_to_all(reshaped_rows, 'exp', split_axis=0, concat_axis=0, tiled=T...  43.3 us
    all_to_all x2, waiting for transfers between devices, routed_whole(): lax.all_to_all(produced, 'exp', split_axis=0, concat_axis=0, tiled=True)  35.7 us
    all_gather x1, blocking collectives, local(): lax.all_gather(key_projection, 'req', axis=0, tiled=True)  21.5 us
    dot_general x2, matrix products, expert_products(): jnp.einsum('pekf,efd->pekd', hidden, w_down, preferred_element_type=jnp.f...  20.8 us
    unnamed x75, local copies, waits for them, and re-layouts  18.8 us
    all_gather x1, blocking collectives, local(): lax.all_gather(value_projection, 'req', axis=0, tiled=True)  13.6 us
    dot_general x2, matrix products, expert_products(): jnp.einsum('pekd,edf->pekf', received, w_up, preferred_element_type=jnp.f...  13.1 us
    all_to_all x2, starting transfers between devices, routed_whole(): lax.all_to_all(reshaped_rows, 'exp', split_axis=0, concat_axis=0, tiled=T...  12.7 us
  transfers between devices with their start and end apart: 10, of which 5 were waited for; matrix products, arithmetic and copies ran while one was open for 29% of the time, Pallas kernels for 0%

profile of v5, /device:TPU:0, one launch (start us, length us, event | category | flops | bytes accessed | tf_op | source)
XLA Modules:
  0.0 287.2 jit_solution(17738152868474953358)
XLA Ops:
  18.1 21.5 %all_gather.10 = bf16[1536,256]{1,0:T(8,128)(2,1)S(1)} all-gather(bf16[192,256]{1,0:T(8,128)(2,1)S(1)} %copy-done.21), channel_id=1, replica_groups=mesh['req'=8,'exp'=16] {'req'}, dimensions={0}, use_global_device_ids=true | all-gather | bytes 884736 | tf_op jit(solution)/shard_map/all_gather | solution.py:223
  58.4 3.7 %collective-permute-done.3 = bf16[1536,96]{0,1:T(8,128)(2,1)S(1)} collective-permute-done((bf16[1536,96]{0,1:T(8,128)(2,1)S(1)}, bf16[1536,96]{0,1:T(8,128)(2,1)S(1)}, u32[]{:S(2)}, u32[]{:S(2)}) %collective-permute-start.3) | collective-permute-done | bytes 294944 | tf_op jit(solution)/shard_map/ppermute | solution.py:175
  64.1 13.6 %all_gather.11 = bf16[1536,256]{1,0:T(8,128)(2,1)S(1)} all-gather(bf16[192,256]{1,0:T(8,128)(2,1)S(1)} %copy-done.22), channel_id=1, replica_groups=mesh['req'=8,'exp'=16] {'req'}, dimensions={0}, use_global_device_ids=true | all-gather | bytes 884736 | tf_op jit(solution)/shard_map/all_gather | solution.py:228
  80.5 4.0 %copy.176 = bf16[4,1024,256]{1,2,0:T(8,128)(2,1)} copy(bf16[4,1024,256]{2,1,0:T(8,128)(2,1)} %get-tuple-element.9) | data formatting | bytes 4194304
  87.1 3.3 %constant_dynamic-update-slice_fusion.5 = bf16[1536,1536]{0,1:T(8,128)(2,1)} fusion(bf16[1536,1536]{0,1:T(8,128)(2,1)} %get-tuple-element.20, bf16[1536,768]{0,1:T(8,128)(2,1)} %collective-permute-done.4), kind=kLoop, calls=%fused_computation.150 | loop fusion | bytes 4718592 | tf_op jit(solution)/shard_map/concatenate | solution.py:190
  90.4 4.4 %fusion.142 = f32[256,1536]{0,1:T(8,128)S(1)} fusion(bf16[1536,1536]{1,0:T(8,128)(2,1)} %all-gather.2.cloned.1.call-done, bf16[256,1536]{1,0:T(8,128)(2,1)S(1)} %copy-done.1, f32[1536]{0:T(1024)} %param.19, f32[256]{0:T(256)S(1)} %copy-done.29), kind=kOutput, calls=%fused_computation.194 | convolution fusion | flops 1209532416 | bytes 7085056 | tf_op jit(solution)/shard_map/dot_general | solution.py:216
  100.9 3.1 %fusion.1 = f32[4,2,6,64]{3,2,1,0:T(8,128)S(1)} fusion(f32[4,2,64,6,1024]{4,2,3,1,0:T(8,128)S(1)} %get-tuple-element.44, f32[4,2,6,64]{3,2,1,0:T(8,128)S(1)} %max.25, pred[4,1024]{1,0:T(4,128)(4,1)S(1)} %iota_compare_fusion.8), kind=kLoop, calls=%fused_computation.8 | loop fusion | flops 12579840 | bytes 12611584 | tf_op jit(solution)/shard_map/vmap()/reduce_sum | solution.py:87
  105.6 4.2 %fusion.36 = bf16[4,64,2,6,128]{4,1,3,2,0:T(8,128)(2,1)S(1)} fusion(f32[4,2,128,6,64]{2,4,3,1,0:T(8,128)S(1)} %fusion.74, bf16[4,1024,2,128,1]{1,3,4,2,0:T(8,128)(2,1)S(1)} %bitcast.141, f32[4,2,64,6,1024]{4,2,3,1,0:T(8,128)S(1)} %get-tuple-element.44, f32[4,2,6,64]{3,2,1,0:T(8,128)S(1)} %add.128, f32[4,2,6,64]{3,2,1,0:T(8,128)S(1)} %max.25, ...), kind=kOutput, calls=%fused_computation.42 | convolution fusion | flops 821821440 | bytes 17068032 | tf_op jit(solution)/shard_map/vmap(gsij,jgd->igsd)/dot_general | solution.py:92
  111.3 3.7 %fusion.92 = f32[128,2,4,192]{0,3,2,1:T(8,128)S(1)} fusion(bf16[2,4,192,1536]{3,2,1,0:T(8,128)(2,1)} %bitcast.133, bf16[128,1536,1,1]{1,0,2,3:T(8,128)(2,1)S(1)} %reshape.361), kind=kOutput, calls=%fused_computation.101 | convolution fusion | flops 603979776 | bytes 5898240 | tf_op jit(solution)/shard_map/dot_general | solution.py:252
  115.0 3.7 %fusion.90 = f32[128,2,4,192]{0,3,2,1:T(8,128)S(1)} fusion(bf16[2,4,192,1536]{3,2,1,0:T(8,128)(2,1)} %bitcast.134, bf16[128,1536,1,1]{1,0,2,3:T(8,128)(2,1)S(1)} %reshape.365), kind=kOutput, calls=%fused_computation.99 | convolution fusion | flops 603979776 | bytes 5898240 | tf_op jit(solution)/shard_map/dot_general | solution.py:252
  125.8 7.1 %all-to-all-start = ((bf16[16,2,24,1536]{3,2,1,0:T(8,128)(2,1)}), bf16[16,2,24,1536]{3,2,1,0:T(8,128)(2,1)S(1)}, u32[]{:S(2)}, u32[]{:S(2)}) async-start(bf16[16,2,24,1536]{3,2,1,0:T(8,128)(2,1)} %bitcast.20), calls=%async_computation | async-start | bytes 4718592 | tf_op jit(solution)/shard_map/all_to_all | solution.py:160
  135.2 31.2 %all-to-all-done = bf16[16,2,24,1536]{3,2,1,0:T(8,128)(2,1)S(1)} async-done(((bf16[16,2,24,1536]{3,2,1,0:T(8,128)(2,1)}), bf16[16,2,24,1536]{3,2,1,0:T(8,128)(2,1)S(1)}, u32[]{:S(2)}, u32[]{:S(2)}) %all-to-all-start) | async-done | bytes 2359328 | tf_op jit(solution)/shard_map/all_to_all | solution.py:160
  167.8 5.6 %all-to-all-start.2 = ((bf16[16,2,24,1536]{3,2,1,0:T(8,128)(2,1)}), bf16[16,2,24,1536]{3,2,1,0:T(8,128)(2,1)S(1)}, u32[]{:S(2)}, u32[]{:S(2)}) async-start(bf16[16,2,24,1536]{3,2,1,0:T(8,128)(2,1)} %bitcast.35), calls=%async_computation.2 | async-start | bytes 4718592 | tf_op jit(solution)/shard_map/all_to_all | solution.py:160
  173.5 6.5 %fusion.9 = f32[2,16,24,768]{3,2,1,0:T(8,128)} fusion(bf16[2,1536,768]{2,1,0:T(8,128)(2,1)} %param.26, bf16[16,2,24,1536]{3,2,1,0:T(8,128)(2,1)} %copy-done.4), kind=kOutput, calls=%fused_computation.16 | convolution fusion | flops 1811939328 | bytes 9437184 | tf_op jit(solution)/shard_map/pekd,edf->pekf/dot_general | solution.py:138
  180.0 10.4 %fusion.25 = bf16[16,2,24,1536]{3,2,0,1:T(8,128)(2,1)} fusion(bf16[2,768,1536]{2,1,0:T(8,128)(2,1)} %param.27, f32[2,16,24,768]{3,2,1,0:T(8,128)} %fusion.9, bf16[2,1536,768]{2,1,0:T(8,128)(2,1)} %param.25, bf16[16,2,24,1536]{3,2,1,0:T(8,128)(2,1)} %copy-done.4), kind=kOutput, calls=%fused_computation.28 | convolution fusion | flops 3626827776 | bytes 16515072 | tf_op jit(solution)/shard_map/pekf,efd->pekd/dot_general | solution.py:140
  190.4 3.4 %copy.145 = bf16[16,2,24,1536]{3,2,1,0:T(8,128)(2,1)} copy(bf16[16,2,24,1536]{3,2,0,1:T(8,128)(2,1)} %fusion.25) | data formatting | bytes 4718592 | tf_op jit(solution)/shard_map/convert_element_type | solution.py:140
  193.8 12.1 %all-to-all-done.2 = bf16[16,2,24,1536]{3,2,1,0:T(8,128)(2,1)S(1)} async-done(((bf16[16,2,24,1536]{3,2,1,0:T(8,128)(2,1)}), bf16[16,2,24,1536]{3,2,1,0:T(8,128)(2,1)S(1)}, u32[]{:S(2)}, u32[]{:S(2)}) %all-to-all-start.2) | async-done | bytes 2359328 | tf_op jit(solution)/shard_map/all_to_all | solution.py:160
  207.3 4.0 %all-to-all-start.1 = ((bf16[16,2,24,1536]{3,2,1,0:T(8,128)(2,1)}), bf16[16,2,24,1536]{3,2,1,0:T(8,128)(2,1)S(1)}, u32[]{:S(2)}, u32[]{:S(2)}) async-start(bf16[16,2,24,1536]{3,2,1,0:T(8,128)(2,1)} %copy.145), calls=%async_computation.1 | async-start | bytes 4718592 | tf_op jit(solution)/shard_map/all_to_all | solution.py:165
  211.4 6.5 %fusion.7 = f32[2,16,24,768]{3,2,1,0:T(8,128)} fusion(bf16[2,1536,768]{2,1,0:T(8,128)(2,1)} %param.26, bf16[16,2,24,1536]{3,2,1,0:T(8,128)(2,1)} %copy-done.3), kind=kOutput, calls=%fused_computation.14 | convolution fusion | flops 1811939328 | bytes 9437184 | tf_op jit(solution)/shard_map/pekd,edf->pekf/dot_general | solution.py:138
  217.9 10.4 %fusion.22 = bf16[16,2,24,1536]{3,2,0,1:T(8,128)(2,1)} fusion(bf16[2,768,1536]{2,1,0:T(8,128)(2,1)} %param.27, f32[2,16,24,768]{3,2,1,0:T(8,128)} %fusion.7, bf16[2,1536,768]{2,1,0:T(8,128)(2,1)} %param.25, bf16[16,2,24,1536]{3,2,1,0:T(8,128)(2,1)} %copy-done.3), kind=kOutput, calls=%fused_computation.27 | convolution fusion | flops 3626827776 | bytes 16515072 | tf_op jit(solution)/shard_map/pekf,efd->pekd/dot_general | solution.py:140
  228.4 3.4 %copy.150 = bf16[16,2,24,1536]{3,2,1,0:T(8,128)(2,1)} copy(bf16[16,2,24,1536]{3,2,0,1:T(8,128)(2,1)} %fusion.22) | data formatting | bytes 4718592 | tf_op jit(solution)/shard_map/convert_element_type | solution.py:140
  231.8 9.9 %all-to-all-done.1 = bf16[16,2,24,1536]{3,2,1,0:T(8,128)(2,1)S(1)} async-done(((bf16[16,2,24,1536]{3,2,1,0:T(8,128)(2,1)}), bf16[16,2,24,1536]{3,2,1,0:T(8,128)(2,1)S(1)}, u32[]{:S(2)}, u32[]{:S(2)}) %all-to-all-start.1) | async-done | bytes 2359328 | tf_op jit(solution)/shard_map/all_to_all | solution.py:165
  241.7 4.6 %all-to-all-start.3 = ((bf16[16,2,24,1536]{3,2,1,0:T(8,128)(2,1)}), bf16[16,2,24,1536]{3,2,1,0:T(8,128)(2,1)}, u32[]{:S(2)}, u32[]{:S(2)}) async-start(bf16[16,2,24,1536]{3,2,1,0:T(8,128)(2,1)} %copy.150), calls=%async_computation.3 | async-start | bytes 4718592 | tf_op jit(solution)/shard_map/all_to_all | solution.py:165
  251.1 25.8 %all-to-all-done.3 = bf16[16,2,24,1536]{3,2,1,0:T(8,128)(2,1)} async-done(((bf16[16,2,24,1536]{3,2,1,0:T(8,128)(2,1)}), bf16[16,2,24,1536]{3,2,1,0:T(8,128)(2,1)}, u32[]{:S(2)}, u32[]{:S(2)}) %all-to-all-start.3) | async-done | bytes 2359328 | tf_op jit(solution)/shard_map/all_to_all | solution.py:165
  (162 shorter events, 66.2 us)
Async XLA Ops:
  7.2 9.8 %copy-start.11 = (bf16[1536,192]{0,1:T(8,128)(2,1)S(1)}, bf16[1536,192]{0,1:T(8,128)(2,1)}, u32[]{:S(2)}) copy-start(bf16[1536,192]{0,1:T(8,128)(2,1)} %param.23) | copy-start | bytes 1769476
  7.2 83.2 %all-gather.2.cloned.1.call-start = ((), (), s32[]{:S(2)}) async-start(), calls=%async_computation.4 | async-start | bytes 5308416 | tf_op jit(solution)/shard_map/all_gather | solution.py:218
  7.9 31.7 %copy-start.1 = (bf16[256,1536]{1,0:T(8,128)(2,1)S(1)}, bf16[256,1536]{1,0:T(8,128)(2,1)}, u32[]{:S(2)}) copy-start(bf16[256,1536]{1,0:T(8,128)(2,1)} %param.18) | copy-start | bytes 2359300
  7.9 31.7 %copy-start.31 = (f32[1536]{0:T(1024)S(1)}, f32[1536]{0:T(1024)}, u32[]{:S(2)}) copy-start(f32[1536]{0:T(1024)} %param.19) | copy-start | bytes 18436
  7.9 34.7 %collective-permute-start = (bf16[1536,192]{0,1:T(8,128)(2,1)}, bf16[1536,192]{0,1:T(8,128)(2,1)S(1)}, u32[]{:S(2)}, u32[]{:S(2)}) collective-permute-start(bf16[1536,192]{0,1:T(8,128)(2,1)} %param.23), channel_id=1, source_target_pairs={{0,32},{16,48},{32,64},{48,80},{64,96},{80,112},{96,0},{112,16},{1... | collective-permute-start | bytes 1769480 | tf_op jit(solution)/shard_map/ppermute | solution.py:175
  10.0 43.0 %collective-permute-start.2 = (bf16[1536,192]{0,1:T(8,128)(2,1)}, bf16[1536,192]{0,1:T(8,128)(2,1)S(1)}, u32[]{:S(2)}, u32[]{:S(2)}) collective-permute-start(bf16[1536,192]{0,1:T(8,128)(2,1)} %param.23), channel_id=1, source_target_pairs={{0,96},{16,112},{32,0},{48,16},{64,32},{80,48},{96,64},{112,80},{1... | collective-permute-start | bytes 1769480 | tf_op jit(solution)/shard_map/ppermute | solution.py:175
  14.1 26.1 %copy-start.17 = (f32[4,64,64]{2,1,0:T(8,128)}, f32[4,64,64]{2,1,0:T(8,128)S(1)}, u32[]{:S(2)}) copy-start(f32[4,64,64]{2,1,0:T(8,128)S(1)} %get-tuple-element.42) | copy-start | bytes 196612
  17.0 60.7 %copy-start.28 = (f32[256]{0:T(256)}, f32[256]{0:T(256)S(1)}, u32[]{:S(2)}) copy-start(f32[256]{0:T(256)S(1)} %add_rsqrt_fusion) | copy-start | bytes 3076
  17.0 23.2 %copy-start = (bf16[4,1024,512]{2,1,0:T(8,128)(2,1)S(1)}, bf16[4,1024,512]{2,1,0:T(8,128)(2,1)}, u32[]{:S(2)}) copy-start(bf16[4,1024,512]{2,1,0:T(8,128)(2,1)} %param.30) | copy-start | bytes 12582916
  42.6 7.4 %copy-start.6 = (bf16[1536,192]{0,1:T(8,128)(2,1)}, bf16[1536,192]{0,1:T(8,128)(2,1)S(1)}, u32[]{:S(2)}) copy-start(bf16[1536,192]{0,1:T(8,128)(2,1)S(1)} %collective-permute-done) | copy-start | bytes 1769476
  43.4 13.2 %collective-permute-start.1 = (bf16[1536,96]{0,1:T(8,128)(2,1)}, bf16[1536,96]{0,1:T(8,128)(2,1)}, u32[]{:S(2)}, u32[]{:S(2)}) collective-permute-start(bf16[1536,96]{0,1:T(8,128)(2,1)} %slice.111), channel_id=1, source_target_pairs={{0,32},{16,48},{32,64},{48,80},{64,96},{80,112},{96,0},{112,16},{1... | collective-permute-start | bytes 884744 | tf_op jit(solution)/shard_map/ppermute | solution.py:175
  53.1 9.0 %collective-permute-start.3 = (bf16[1536,96]{0,1:T(8,128)(2,1)S(1)}, bf16[1536,96]{0,1:T(8,128)(2,1)S(1)}, u32[]{:S(2)}, u32[]{:S(2)}) collective-permute-start(bf16[1536,96]{0,1:T(8,128)(2,1)S(1)} %slice.112), channel_id=1, source_target_pairs={{0,96},{16,112},{32,0},{48,16},{64,32},{80,48},{96,64},{112,80},{1... | collective-permute-start | bytes 884744 | tf_op jit(solution)/shard_map/ppermute | solution.py:175
  54.4 9.7 %copy-start.22 = (bf16[192,256]{1,0:T(8,128)(2,1)S(1)}, bf16[192,256]{1,0:T(8,128)(2,1)}, u32[]{:S(2)}) copy-start(bf16[192,256]{1,0:T(8,128)(2,1)} %param.22) | copy-start | bytes 294916
  64.1 23.0 %collective-permute-start.4 = (bf16[1536,768]{0,1:T(8,128)(2,1)}, bf16[1536,768]{0,1:T(8,128)(2,1)}, u32[]{:S(2)}, u32[]{:S(2)}) collective-permute-start(bf16[1536,768]{0,1:T(8,128)(2,1)} %get-tuple-element.19), channel_id=1, source_target_pairs={{0,16},{16,0},{32,48},{48,32},{64,80},{80,64},{96,112},{112,96},{1... | collective-permute-start | bytes 7077896 | tf_op jit(solution)/shard_map/ppermute | solution.py:190
  86.2 11.3 %copy-start.7 = (bf16[256,2,128]{2,0,1:T(8,128)(2,1)}, bf16[256,2,128]{2,0,1:T(8,128)(2,1)S(1)}, u32[]{:S(2)}) copy-start(bf16[256,2,128]{2,0,1:T(8,128)(2,1)S(1)} %pad_maximum_fusion.2) | copy-start | bytes 393220
  125.8 40.7 %all-to-all-start = ((bf16[16,2,24,1536]{3,2,1,0:T(8,128)(2,1)}), bf16[16,2,24,1536]{3,2,1,0:T(8,128)(2,1)S(1)}, u32[]{:S(2)}, u32[]{:S(2)}) async-start(bf16[16,2,24,1536]{3,2,1,0:T(8,128)(2,1)} %bitcast.20), calls=%async_computation | async-start | bytes 4718592 | tf_op jit(solution)/shard_map/all_to_all | solution.py:160
  167.8 38.0 %all-to-all-start.2 = ((bf16[16,2,24,1536]{3,2,1,0:T(8,128)(2,1)}), bf16[16,2,24,1536]{3,2,1,0:T(8,128)(2,1)S(1)}, u32[]{:S(2)}, u32[]{:S(2)}) async-start(bf16[16,2,24,1536]{3,2,1,0:T(8,128)(2,1)} %bitcast.35), calls=%async_computation.2 | async-start | bytes 4718592 | tf_op jit(solution)/shard_map/all_to_all | solution.py:160
  193.8 17.6 %copy-start.32 = (s32[4]{0:T(128)S(1)}, s32[4]{0:T(128)}, u32[]{:S(2)}) copy-start(s32[4]{0:T(128)} %param.33) | copy-start | bytes 52
  207.3 34.4 %all-to-all-start.1 = ((bf16[16,2,24,1536]{3,2,1,0:T(8,128)(2,1)}), bf16[16,2,24,1536]{3,2,1,0:T(8,128)(2,1)S(1)}, u32[]{:S(2)}, u32[]{:S(2)}) async-start(bf16[16,2,24,1536]{3,2,1,0:T(8,128)(2,1)} %copy.145), calls=%async_computation.1 | async-start | bytes 4718592 | tf_op jit(solution)/shard_map/all_to_all | solution.py:165
  231.8 14.5 %copy-start.8 = (bf16[256,2,128]{2,0,1:T(8,128)(2,1)S(1)}, bf16[256,2,128]{2,0,1:T(8,128)(2,1)}, u32[]{:S(2)}) copy-start(bf16[256,2,128]{2,0,1:T(8,128)(2,1)} %copy-done.7) | copy-start | bytes 393220
  231.8 16.2 %copy-start.25 = (f32[256,4]{0,1:T(4,128)S(1)}, f32[256,4]{0,1:T(4,128)}, u32[]{:S(2)}) copy-start(f32[256,4]{0,1:T(4,128)} %param.29) | copy-start | bytes 12292
  231.8 17.4 %copy-start.19 = (bf16[256,256]{1,0:T(8,128)(2,1)S(1)}, bf16[256,256]{1,0:T(8,128)(2,1)}, u32[]{:S(2)}) copy-start(bf16[256,256]{1,0:T(8,128)(2,1)} %convolution_convert_fusion.1) | copy-start | bytes 393220
  231.8 17.4 %copy-start.26 = (s32[4,64]{1,0:T(4,128)S(1)}, s32[4,64]{1,0:T(4,128)}, u32[]{:S(2)}) copy-start(s32[4,64]{1,0:T(4,128)} %get-tuple-element.35) | copy-start | bytes 3076
  241.7 35.2 %all-to-all-start.3 = ((bf16[16,2,24,1536]{3,2,1,0:T(8,128)(2,1)}), bf16[16,2,24,1536]{3,2,1,0:T(8,128)(2,1)}, u32[]{:S(2)}, u32[]{:S(2)}) async-start(bf16[16,2,24,1536]{3,2,1,0:T(8,128)(2,1)} %copy.150), calls=%async_computation.3 | async-start | bytes 4718592 | tf_op jit(solution)/shard_map/all_to_all | solution.py:165
  (19 other events, 68.0 us)
Sparse Core Ops, SparseCore 0:
  9.7 39.7 all-gather.1

commit v6 on v4

--- a/solution.py
+++ b/solution.py
@@ -189,28 +189,47 @@
     normed = rms_scale(tokens, attn_gain)
     closure, tree_depth = ancestry(parents)
     positions = (lengths[:, None] + tree_depth).reshape(-1)
-    query_sum = jnp.dot(
-        normed,
-        lax.all_gather(w_query, "req", axis=0, tiled=True),
-        preferred_element_type=jnp.float32,
-    )
-    key_sum = jnp.dot(
-        normed,
-        lax.all_gather(key_projection, "req", axis=0, tiled=True),
-        preferred_element_type=jnp.float32,
-    )
-    value_sum = jnp.dot(
-        normed,
-        lax.all_gather(value_projection, "req", axis=0, tiled=True),
-        preferred_element_type=jnp.float32,
-    )
+    kv_shard = jnp.concatenate([key_projection, value_projection], axis=1)
+    peer_count = lax.axis_size("exp")
+    place_exp = lax.axis_index("exp")
+    out_rows_each = w_out.shape[0] // peer_count
+    q_rows_each = w_query.shape[0] // peer_count
+    out_slice = lax.dynamic_slice_in_dim(w_out, place_exp * out_rows_each, out_rows_each, axis=0)
+    q_slice = lax.dynamic_slice_in_dim(w_query, place_exp * q_rows_each, q_rows_each, axis=0)
+    small = lax.all_gather(
+        jnp.concatenate([kv_shard.reshape(-1), q_slice.reshape(-1), out_slice.reshape(-1)]),
+        "req",
+        axis=0,
+    )
+    req_count = small.shape[0]
+    kv_end = kv_shard.size
+    q_end = kv_end + q_slice.size
+    kv_full = small[:, :kv_end].reshape(req_count * kv_shard.shape[0], kv_shard.shape[1])
+    q_rows = small[:, kv_end:q_end].reshape(req_count * q_rows_each, w_query.shape[1])
+    out_rows = (
+        small[:, q_end:]
+        .reshape(req_count, out_rows_each, w_out.shape[1])
+        .transpose(1, 0, 2)
+        .reshape(out_rows_each, -1)
+    )
+    q_full = lax.all_gather(q_rows, "exp", axis=0, tiled=True)
+    out_rows, q_full = lax.optimization_barrier((out_rows, q_full))
+    normed_perm = (
+        normed.reshape(rows_here, req_count, peer_count, q_rows_each)
+        .transpose(0, 2, 1, 3)
+        .reshape(rows_here, -1)
+    )
+    query_sum = jnp.dot(normed_perm, q_full, preferred_element_type=jnp.float32)
+    kv_sum = jnp.dot(normed, kv_full, preferred_element_type=jnp.float32)
+    key_sum = kv_sum[:, : key_projection.shape[1]]
+    value_sum = kv_sum[:, key_projection.shape[1] :]
     query_rows = rotate(query_sum, positions).astype(jnp.bfloat16)
     tree_key_value = jnp.concatenate([rotate(key_sum, positions), value_sum], axis=1).astype(
         jnp.bfloat16
     )
     query_req = query_rows.reshape(local_reqs, DRAFT_TOKENS, query_rows.shape[1])
     key_value_request = tree_key_value.reshape(local_reqs, DRAFT_TOKENS, tree_key_value.shape[1])
-    w_out_full = lax.all_gather(w_out, "req", axis=1, tiled=True)
+    w_out_full = lax.all_gather(out_rows, "exp", axis=0, tiled=True)
     chunk_count = rows_here // BLOCK_ROWS
     context_all = jax.vmap(attend)(
         query_req, key_value_request, kv_cache, lengths, closure

time: 251 us -> 316 us (1.26)
  waiting for transfers between devices: 77 us -> 146 us
  local copies, waits for them, and re-layouts: 30.2 us -> 61.3 us
  blocking collectives: 30.9 us -> 0 us
    all_gather x2 -> x3, waiting for transfers between devices: 1.69 us -> 74.7 us  [the longest x1 45.9 us: local(): q_full = lax.all_gather(q_rows, 'exp', axis=0, tiled=True)]
    all_gather x2 -> x0, blocking collectives: 30.9 us -> none  [the longest x1 15.6 us: local(): lax.all_gather(key_projection, 'req', axis=0, tiled=True)]
    reshape x0 -> x10, local copies, waits for them, and re-layouts: none -> 11.4 us  [the longest x3 4.44 us: local(): out_rows = small[:, q_end:].reshape(req_count, out_rows_each, w_out.shape...]
    dot_general x0 -> x1, local copies, waits for them, and re-layouts: none -> 6.93 us  [local(): query_sum = jnp.dot(normed_perm, q_full, preferred_element_type=jnp.float32)]
    all_to_all x2, starting transfers between devices: 12.2 us -> 9.03 us  [routed_whole(): lax.all_to_all(reshaped_rows, 'exp', split_axis=0, concat_axis=0, tiled=T...]
    unnamed x53 -> x64, local copies, waits for them, and re-layouts: 10.8 us -> 13.9 us
    dot_general x3 -> x2, matrix products: 6.75 us -> 4.33 us  [the longest x1 3.75 us: local(): query_sum = jnp.dot(normed_perm, q_full, preferred_element_type=jnp.float32)]
  transfers between devices with their start and end apart: 6 -> 7, of which waited for: 5 -> 7; matrix products, arithmetic and copies ran while one was open for 37% -> 36% of each run, Pallas kernels for 0% -> 0%
where the time goes in v6:
time: 316 us; the launch traced here: 315 us
  waiting for transfers between devices  146 us (46%)
  matrix products  64.3 us (20%)
  local copies, waits for them, and re-layouts  61.3 us (19%)
  starting transfers between devices  18 us (6%)
  between operations  14.4 us (5%)
  other arithmetic  11.5 us (4%)
    all_gather x1, waiting for transfers between devices, local(): q_full = lax.all_gather(q_rows, 'exp', axis=0, tiled=True)  45.9 us
    all_to_all x2, waiting for transfers between devices, routed_whole(): lax.all_to_all(reshaped_rows, 'exp', split_axis=0, concat_axis=0, tiled=T...  36.4 us
    all_to_all x2, waiting for transfers between devices, routed_whole(): lax.all_to_all(produced, 'exp', split_axis=0, concat_axis=0, tiled=True)  34.3 us
    all_gather x1, waiting for transfers between devices, local(): lax.all_gather(jnp.concatenate([kv_shard.reshape(-1), q_slice.reshape(-1)...  28.2 us
    dot_general x2, matrix products, expert_products(): jnp.einsum('pekf,efd->pekd', hidden, w_down, preferred_element_type=jnp.f...  20.9 us
    unnamed x64, local copies, waits for them, and re-layouts  13.9 us
    dot_general x2, matrix products, expert_products(): jnp.einsum('pekd,edf->pekf', received, w_up, preferred_element_type=jnp.f...  13.1 us
    all_to_all x2, starting transfers between devices, routed_whole(): lax.all_to_all(reshaped_rows, 'exp', split_axis=0, concat_axis=0, tiled=T...  9.03 us
  transfers between devices with their start and end apart: 7, of which 7 were waited for; matrix products, arithmetic and copies ran while one was open for 36% of the time, Pallas kernels for 0%

profile of v6, /device:TPU:0, one launch (start us, length us, event | category | flops | bytes accessed | tf_op | source)
XLA Modules:
  0.0 315.1 jit_solution(15250829266262404830)
XLA Ops:
  11.4 28.2 %all-gather.9.cloned.1.call-done = bf16[1081344]{0:T(1024)(128)(2,1)} async-done(((bf16[135168]{0:T(1024)(128)(2,1)}), bf16[1081344]{0:T(1024)(128)(2,1)}) %all-gather.9.cloned.1.call-update) | async-done | bytes 2162704 | tf_op jit(solution)/shard_map/all_gather | solution.py:199
  52.2 45.9 %all-gather.5.cloned.1.call-done = bf16[1536,1536]{1,0:T(8,128)(2,1)} async-done(((bf16[96,1536]{1,0:T(8,128)(2,1)}), bf16[1536,1536]{1,0:T(8,128)(2,1)}) %all-gather.5.cloned.1.call-update) | async-done | bytes 4718608 | tf_op jit(solution)/shard_map/all_gather | solution.py:215
  106.6 4.6 %fusion.134 = (bf16[4,1024,256]{2,1,0:T(8,128)(2,1)}, bf16[4,1024,256]{2,1,0:T(8,128)(2,1)}) fusion(bf16[4,1024,512]{2,1,0:T(8,128)(2,1)} %param.28), kind=kLoop, calls=%fused_computation.170 | loop fusion | bytes 8388608 | tf_op jit(solution)/shard_map/vmap()/slice | solution.py:62
  111.3 4.0 %copy.184 = bf16[4,1024,256]{1,2,0:T(8,128)(2,1)} copy(bf16[4,1024,256]{2,1,0:T(8,128)(2,1)} %get-tuple-element.9) | data formatting | bytes 4194304
  115.2 4.0 %copy.187 = bf16[4,1024,256]{1,2,0:T(8,128)(2,1)} copy(bf16[4,1024,256]{2,1,0:T(8,128)(2,1)} %get-tuple-element.8) | data formatting | bytes 4194304
  126.4 6.9 %copy.136 = bf16[1536,1536]{1,0:T(8,128)(2,1)} copy(bf16[1536,1536]{0,1:T(8,128)(2,1)} %bitcast.134) | data formatting | bytes 9437184 | tf_op jit(solution)/shard_map/dot_general | solution.py:222
  133.3 3.8 %fusion.74 = f32[256,12,128]{0,2,1:T(8,128)S(1)} fusion(bf16[12,128,1536]{2,1,0:T(8,128)(2,1)} %bitcast.135, bf16[256,1536]{0,1:T(8,128)(2,1)S(1)} %copy-done.15), kind=kOutput, calls=%fused_computation.71 | convolution fusion | flops 1207959552 | bytes 7077888 | tf_op jit(solution)/shard_map/dot_general | solution.py:222
  148.1 4.2 %fusion.40 = bf16[4,64,2,6,128]{4,1,3,2,0:T(8,128)(2,1)S(1)} fusion(f32[4,2,128,6,64]{2,4,3,1,0:T(8,128)S(1)} %fusion.76, bf16[4,1024,2,128,1]{1,3,4,2,0:T(8,128)(2,1)S(1)} %bitcast.137, f32[4,2,64,6,1024]{4,2,3,1,0:T(8,128)S(1)} %get-tuple-element.31, f32[4,2,6,64]{3,2,1,0:T(8,128)S(1)} %add.121, f32[4,2,6,64]{3,2,1,0:T(8,128)S(1)} %max.25, ...), kind=kOutput, calls=%fused_computation.46 | convolution fusion | flops 821821440 | bytes 17068032 | tf_op jit(solution)/shard_map/vmap(gsij,jgd->igsd)/dot_general | solution.py:92
  153.7 3.2 %multiply_reduce_fusion.1 = (f32[128]{0:T(128)S(1)}, f32[128,1536]{1,0:T(8,128)S(1)}) fusion(bf16[128,1536]{1,0:T(8,128)(2,1)S(1)} %slice.99, bf16[1536,1536]{1,0:T(8,128)(2,1)} %all-gather.7.cloned.1.call-done, bf16[256,1536]{1,0:T(8,128)(2,1)S(1)} %copy-done.4), kind=kOutput, calls=%fused_computation.76 | convolution fusion | flops 605159296 | bytes 6291968 | tf_op jit(solution)/shard_map/dot_general | solution.py:241
  160.2 5.3 %all-to-all-start = ((bf16[16,2,24,1536]{3,2,1,0:T(8,128)(2,1)}), bf16[16,2,24,1536]{3,2,1,0:T(8,128)(2,1)}, u32[]{:S(2)}, u32[]{:S(2)}) async-start(bf16[16,2,24,1536]{3,2,1,0:T(8,128)(2,1)} %bitcast.17), calls=%async_computation | async-start | bytes 4718592 | tf_op jit(solution)/shard_map/all_to_all | solution.py:160
  166.2 3.2 %multiply_reduce_fusion = (f32[128]{0:T(128)S(1)}, f32[128,1536]{1,0:T(8,128)S(1)}) fusion(bf16[128,1536]{1,0:T(8,128)(2,1)S(1)} %slice.107, bf16[1536,1536]{1,0:T(8,128)(2,1)} %all-gather.7.cloned.1.call-done, bf16[256,1536]{1,0:T(8,128)(2,1)S(1)} %copy-done.4), kind=kOutput, calls=%fused_computation.74 | convolution fusion | flops 605159296 | bytes 6291968 | tf_op jit(solution)/shard_map/dot_general | solution.py:241
  172.6 26.4 %all-to-all-done = bf16[16,2,24,1536]{3,2,1,0:T(8,128)(2,1)} async-done(((bf16[16,2,24,1536]{3,2,1,0:T(8,128)(2,1)}), bf16[16,2,24,1536]{3,2,1,0:T(8,128)(2,1)}, u32[]{:S(2)}, u32[]{:S(2)}) %all-to-all-start) | async-done | bytes 2359328 | tf_op jit(solution)/shard_map/all_to_all | solution.py:160
  198.9 3.7 %all-to-all-start.2 = ((bf16[16,2,24,1536]{3,2,1,0:T(8,128)(2,1)}), bf16[16,2,24,1536]{3,2,1,0:T(8,128)(2,1)S(1)}, u32[]{:S(2)}, u32[]{:S(2)}) async-start(bf16[16,2,24,1536]{3,2,1,0:T(8,128)(2,1)} %bitcast.27), calls=%async_computation.2 | async-start | bytes 4718592 | tf_op jit(solution)/shard_map/all_to_all | solution.py:160
  202.7 6.5 %fusion.9 = f32[2,16,24,768]{3,2,1,0:T(8,128)} fusion(bf16[2,1536,768]{2,1,0:T(8,128)(2,1)} %param.24, bf16[16,2,24,1536]{3,2,1,0:T(8,128)(2,1)} %all-to-all-done), kind=kOutput, calls=%fused_computation.14 | convolution fusion | flops 1811939328 | bytes 9437184 | tf_op jit(solution)/shard_map/pekd,edf->pekf/dot_general | solution.py:138
  209.2 10.5 %fusion.25 = bf16[16,2,24,1536]{3,2,0,1:T(8,128)(2,1)} fusion(bf16[2,768,1536]{2,1,0:T(8,128)(2,1)} %param.25, f32[2,16,24,768]{3,2,1,0:T(8,128)} %fusion.9, bf16[2,1536,768]{2,1,0:T(8,128)(2,1)} %param.23, bf16[16,2,24,1536]{3,2,1,0:T(8,128)(2,1)} %all-to-all-done), kind=kOutput, calls=%fused_computation.26 | convolution fusion | flops 3626827776 | bytes 16515072 | tf_op jit(solution)/shard_map/pekf,efd->pekd/dot_general | solution.py:140
  219.6 3.4 %copy.158 = bf16[16,2,24,1536]{3,2,1,0:T(8,128)(2,1)} copy(bf16[16,2,24,1536]{3,2,0,1:T(8,128)(2,1)} %fusion.25) | data formatting | bytes 4718592 | tf_op jit(solution)/shard_map/convert_element_type | solution.py:140
  223.0 10.1 %all-to-all-done.2 = bf16[16,2,24,1536]{3,2,1,0:T(8,128)(2,1)S(1)} async-done(((bf16[16,2,24,1536]{3,2,1,0:T(8,128)(2,1)}), bf16[16,2,24,1536]{3,2,1,0:T(8,128)(2,1)S(1)}, u32[]{:S(2)}, u32[]{:S(2)}) %all-to-all-start.2) | async-done | bytes 2359328 | tf_op jit(solution)/shard_map/all_to_all | solution.py:160
  234.6 4.5 %all-to-all-start.1 = ((bf16[16,2,24,1536]{3,2,1,0:T(8,128)(2,1)}), bf16[16,2,24,1536]{3,2,1,0:T(8,128)(2,1)S(1)}, u32[]{:S(2)}, u32[]{:S(2)}) async-start(bf16[16,2,24,1536]{3,2,1,0:T(8,128)(2,1)} %copy.158), calls=%async_computation.1 | async-start | bytes 4718592 | tf_op jit(solution)/shard_map/all_to_all | solution.py:165
  240.6 6.6 %fusion.7 = f32[2,16,24,768]{3,2,1,0:T(8,128)} fusion(bf16[2,1536,768]{2,1,0:T(8,128)(2,1)} %param.24, bf16[16,2,24,1536]{3,2,1,0:T(8,128)(2,1)} %copy-done.10), kind=kOutput, calls=%fused_computation.12 | convolution fusion | flops 1811939328 | bytes 9437184 | tf_op jit(solution)/shard_map/pekd,edf->pekf/dot_general | solution.py:138
  247.1 10.4 %fusion.22 = bf16[16,2,24,1536]{3,2,0,1:T(8,128)(2,1)} fusion(bf16[2,768,1536]{2,1,0:T(8,128)(2,1)} %param.25, f32[2,16,24,768]{3,2,1,0:T(8,128)} %fusion.7, bf16[2,1536,768]{2,1,0:T(8,128)(2,1)} %param.23, bf16[16,2,24,1536]{3,2,1,0:T(8,128)(2,1)} %copy-done.10), kind=kOutput, calls=%fused_computation.25 | convolution fusion | flops 3626827776 | bytes 16515072 | tf_op jit(solution)/shard_map/pekf,efd->pekd/dot_general | solution.py:140
  257.6 3.4 %copy.162 = bf16[16,2,24,1536]{3,2,1,0:T(8,128)(2,1)} copy(bf16[16,2,24,1536]{3,2,0,1:T(8,128)(2,1)} %fusion.22) | data formatting | bytes 4718592 | tf_op jit(solution)/shard_map/convert_element_type | solution.py:140
  261.0 8.6 %all-to-all-done.1 = bf16[16,2,24,1536]{3,2,1,0:T(8,128)(2,1)S(1)} async-done(((bf16[16,2,24,1536]{3,2,1,0:T(8,128)(2,1)}), bf16[16,2,24,1536]{3,2,1,0:T(8,128)(2,1)S(1)}, u32[]{:S(2)}, u32[]{:S(2)}) %all-to-all-start.1) | async-done | bytes 2359328 | tf_op jit(solution)/shard_map/all_to_all | solution.py:165
  269.6 4.4 %all-to-all-start.3 = ((bf16[16,2,24,1536]{3,2,1,0:T(8,128)(2,1)}), bf16[16,2,24,1536]{3,2,1,0:T(8,128)(2,1)}, u32[]{:S(2)}, u32[]{:S(2)}) async-start(bf16[16,2,24,1536]{3,2,1,0:T(8,128)(2,1)} %copy.162), calls=%async_computation.3 | async-start | bytes 4718592 | tf_op jit(solution)/shard_map/all_to_all | solution.py:165
  279.3 25.7 %all-to-all-done.3 = bf16[16,2,24,1536]{3,2,1,0:T(8,128)(2,1)} async-done(((bf16[16,2,24,1536]{3,2,1,0:T(8,128)(2,1)}), bf16[16,2,24,1536]{3,2,1,0:T(8,128)(2,1)}, u32[]{:S(2)}, u32[]{:S(2)}) %all-to-all-start.3) | async-done | bytes 2359328 | tf_op jit(solution)/shard_map/all_to_all | solution.py:165
  (154 shorter events, 63.3 us)
Async XLA Ops:
  7.2 32.4 %all-gather.9.cloned.1.call-start = ((), (), s32[]{:S(2)}) async-start(), calls=%async_computation.6 | async-start | bytes 2433024 | tf_op jit(solution)/shard_map/all_gather | solution.py:199
  11.4 32.8 %copy-start.28 = (s32[4,64]{1,0:T(4,128)S(1)}, s32[4,64]{1,0:T(4,128)}, u32[]{:S(2)}) copy-start(s32[4,64]{1,0:T(4,128)} %param.30) | copy-start | bytes 3076
  11.4 86.8 %all-gather.5.cloned.1.call-start = ((), (), s32[]{:S(2)}) async-start(), calls=%async_computation.4 | async-start | bytes 5013504 | tf_op jit(solution)/shard_map/all_gather | solution.py:215
  42.1 3.2 %copy-start.27 = (s32[4]{0:T(128)S(1)}, s32[4]{0:T(128)}, u32[]{:S(2)}) copy-start(s32[4]{0:T(128)} %param.29) | copy-start | bytes 52
  42.9 55.3 %copy-start.3 = (bf16[256,1536]{1,0:T(8,128)(2,1)S(1)}, bf16[256,1536]{1,0:T(8,128)(2,1)}, u32[]{:S(2)}) copy-start(bf16[256,1536]{1,0:T(8,128)(2,1)} %param.16) | copy-start | bytes 2359300
  44.1 109.7 %all-gather.7.cloned.1.call-start = ((), (), s32[]{:S(2)}) async-start(), calls=%async_computation.5 | async-start | bytes 5013504 | tf_op jit(solution)/shard_map/all_gather | solution.py:232
  44.1 54.3 %copy-start.25 = (f32[1536]{0:T(1024)S(1)}, f32[1536]{0:T(1024)}, u32[]{:S(2)}) copy-start(f32[1536]{0:T(1024)} %param.17) | copy-start | bytes 18436
  115.2 4.0 %copy-start.23 = (s32[256,4]{0,1:T(4,128)S(1)}, s32[256,4]{0,1:T(4,128)}, u32[]{:S(2)}) copy-start(s32[256,4]{0,1:T(4,128)} %param.26) | copy-start | bytes 12292
  126.4 13.6 %copy-start.13 = (bf16[256,2,128]{2,0,1:T(8,128)(2,1)}, bf16[256,2,128]{2,0,1:T(8,128)(2,1)S(1)}, u32[]{:S(2)}) copy-start(bf16[256,2,128]{2,0,1:T(8,128)(2,1)S(1)} %pad_maximum_fusion.3) | copy-start | bytes 393220
  126.4 6.9 %copy-start.15 = (bf16[256,1536]{0,1:T(8,128)(2,1)S(1)}, bf16[256,1536]{0,1:T(8,128)(2,1)}, u32[]{:S(2)}) copy-start(bf16[256,1536]{0,1:T(8,128)(2,1)} %reshape.326) | copy-start | bytes 2359300
  133.3 3.8 %copy-start.17 = (f32[256,64]{0,1:T(8,128)S(1)}, f32[256,64]{0,1:T(8,128)}, u32[]{:S(2)}) copy-start(f32[256,64]{0,1:T(8,128)} %copy-done.16) | copy-start | bytes 196612
  138.3 2.6 copy-start.2
  143.3 3.1 copy-start.22
  153.1 4.7 %copy-start.12 = (bf16[256,768]{1,0:T(8,128)(2,1)S(1)}, bf16[256,768]{1,0:T(8,128)(2,1)}, u32[]{:S(2)}) copy-start(bf16[256,768]{1,0:T(8,128)(2,1)} %fusion.39) | copy-start | bytes 1179652
  153.1 4.7 %copy-start.24 = (f32[1536]{0:T(1024)S(1)}, f32[1536]{0:T(1024)}, u32[]{:S(2)}) copy-start(f32[1536]{0:T(1024)} %param.22) | copy-start | bytes 18436
  160.2 38.8 %all-to-all-start = ((bf16[16,2,24,1536]{3,2,1,0:T(8,128)(2,1)}), bf16[16,2,24,1536]{3,2,1,0:T(8,128)(2,1)}, u32[]{:S(2)}, u32[]{:S(2)}) async-start(bf16[16,2,24,1536]{3,2,1,0:T(8,128)(2,1)} %bitcast.17), calls=%async_computation | async-start | bytes 4718592 | tf_op jit(solution)/shard_map/all_to_all | solution.py:160
  198.9 34.2 %all-to-all-start.2 = ((bf16[16,2,24,1536]{3,2,1,0:T(8,128)(2,1)}), bf16[16,2,24,1536]{3,2,1,0:T(8,128)(2,1)S(1)}, u32[]{:S(2)}, u32[]{:S(2)}) async-start(bf16[16,2,24,1536]{3,2,1,0:T(8,128)(2,1)} %bitcast.27), calls=%async_computation.2 | async-start | bytes 4718592 | tf_op jit(solution)/shard_map/all_to_all | solution.py:160
  223.0 16.0 %copy-start.29 = (s32[4]{0:T(128)S(1)}, s32[4]{0:T(128)}, u32[]{:S(2)}) copy-start(s32[4]{0:T(128)} %param.31) | copy-start | bytes 52
  234.6 35.0 %all-to-all-start.1 = ((bf16[16,2,24,1536]{3,2,1,0:T(8,128)(2,1)}), bf16[16,2,24,1536]{3,2,1,0:T(8,128)(2,1)S(1)}, u32[]{:S(2)}, u32[]{:S(2)}) async-start(bf16[16,2,24,1536]{3,2,1,0:T(8,128)(2,1)} %copy.158), calls=%async_computation.1 | async-start | bytes 4718592 | tf_op jit(solution)/shard_map/all_to_all | solution.py:165
  261.0 13.1 %copy-start.26 = (f32[256,4]{0,1:T(4,128)S(1)}, f32[256,4]{0,1:T(4,128)}, u32[]{:S(2)}) copy-start(f32[256,4]{0,1:T(4,128)} %param.27) | copy-start | bytes 12292
  269.6 35.4 %all-to-all-start.3 = ((bf16[16,2,24,1536]{3,2,1,0:T(8,128)(2,1)}), bf16[16,2,24,1536]{3,2,1,0:T(8,128)(2,1)}, u32[]{:S(2)}, u32[]{:S(2)}) async-start(bf16[16,2,24,1536]{3,2,1,0:T(8,128)(2,1)} %copy.162), calls=%async_computation.3 | async-start | bytes 4718592 | tf_op jit(solution)/shard_map/all_to_all | solution.py:165
  275.6 3.6 %copy-start.6 = (f32[128,1536]{1,0:T(8,128)S(1)}, f32[128,1536]{1,0:T(8,128)}, u32[]{:S(2)}) copy-start(f32[128,1536]{1,0:T(8,128)} %copy-done.5) | copy-start | bytes 2359300
  279.3 28.2 %copy-start.8 = (f32[128,1536]{1,0:T(8,128)S(1)}, f32[128,1536]{1,0:T(8,128)}, u32[]{:S(2)}) copy-start(f32[128,1536]{1,0:T(8,128)} %copy-done.7) | copy-start | bytes 2359300
  305.0 3.6 %copy-start.1 = (bf16[1536,192]{0,1:T(8,128)(2,1)S(1)}, bf16[1536,192]{0,1:T(8,128)(2,1)}, u32[]{:S(2)}) copy-start(bf16[1536,192]{0,1:T(8,128)(2,1)} %param.21) | copy-start | bytes 1769476
  (13 other events, 18.1 us)
Sparse Core Ops, SparseCore 0:
  11.5 28.0 all-gather.8
  44.2 53.8 all-gather.4
  100.3 53.3 all-gather.6

commit v7 on v4

--- a/solution.py
+++ b/solution.py
@@ -47,8 +47,12 @@
     node_index = jnp.arange(node_count, dtype=jnp.int32)
     parent_step = (parents[..., :, None] == node_index[None, None, :]).astype(jnp.float32)
     closure = jnp.maximum(parent_step, jnp.eye(node_count, dtype=jnp.float32)[None])
-    for squaring in range(max(1, (node_count - 1).bit_length())):
-        closure = jnp.minimum(jnp.einsum("rij,rjk->rik", closure, closure), 1.0)
+    closure = lax.fori_loop(
+        0,
+        max(1, (node_count - 1).bit_length()),
+        lambda step, held: jnp.minimum(jnp.einsum("rij,rjk->rik", held, held), 1.0),
+        closure,
+    )
     tree_depth = jnp.sum(closure, axis=-1).astype(jnp.int32) - 1
     return (closure, tree_depth)
 
@@ -151,11 +155,11 @@
     return mixed[:rows] + mixed[rows:]
 
 
-def routed_whole(moe_in, place, weight_hi, weight_lo, w_gate, w_up, w_down):
-    capacity = place.shape[1] // EXPERTS
-    buffer = pack_slots(moe_in, place)
+def routed_whole(buffer, weight_hi, weight_lo, w_gate, w_up, w_down):
+    capacity = buffer.shape[0] // EXPERTS
+    width = buffer.shape[1]
     peer_count = lax.axis_size("exp")
-    reshaped_rows = buffer.reshape(peer_count, w_gate.shape[0], capacity, moe_in.shape[1])
+    reshaped_rows = buffer.reshape(peer_count, w_gate.shape[0], capacity, width)
     produced = expert_products(
         lax.all_to_all(reshaped_rows, "exp", split_axis=0, concat_axis=0, tiled=True),
         w_gate,
@@ -204,8 +208,9 @@
         lax.all_gather(value_projection, "req", axis=0, tiled=True),
         preferred_element_type=jnp.float32,
     )
-    query_rows = rotate(query_sum, positions).astype(jnp.bfloat16)
-    tree_key_value = jnp.concatenate([rotate(key_sum, positions), value_sum], axis=1).astype(
+    turned = rotate(jnp.concatenate([query_sum, key_sum], axis=1), positions)
+    query_rows = turned[:, : query_sum.shape[1]].astype(jnp.bfloat16)
+    tree_key_value = jnp.concatenate([turned[:, query_sum.shape[1] :], value_sum], axis=1).astype(
         jnp.bfloat16
     )
     query_req = query_rows.reshape(local_reqs, DRAFT_TOKENS, query_rows.shape[1])
@@ -216,17 +221,21 @@
         query_req, key_value_request, kv_cache, lengths, closure
     ).reshape(rows_here, -1)
     place, weight_hi, weight_lo = slot_tables(routes, gate_weights, CAP)
+    attn_out = jnp.dot(context_all, w_out_full, preferred_element_type=jnp.float32)
+    residual = (tokens.astype(jnp.float32) + attn_out).astype(jnp.bfloat16)
+    moe_in = rms_scale(residual, moe_gain)
+    buffers = jnp.einsum(
+        "hts,htd->hsd",
+        place.reshape(chunk_count, BLOCK_ROWS, -1),
+        moe_in.reshape(chunk_count, BLOCK_ROWS, -1),
+        preferred_element_type=jnp.bfloat16,
+    )
     outs = []
     for chunk in range(chunk_count):
         rw = slice(chunk * BLOCK_ROWS, (chunk + 1) * BLOCK_ROWS)
-        attn_out = jnp.dot(context_all[rw], w_out_full, preferred_element_type=jnp.float32)
-        residual = (tokens[rw].astype(jnp.float32) + attn_out).astype(jnp.bfloat16)
-        moe_in = rms_scale(residual, moe_gain)
-        mixed = routed_whole(
-            moe_in, place[rw], weight_hi[rw], weight_lo[rw], w_gate, w_up, w_down
-        )
-        outs.append((residual.astype(jnp.float32) + mixed).astype(jnp.bfloat16))
-    layer_out = jnp.concatenate(outs, axis=0)
+        mixed = routed_whole(buffers[chunk], weight_hi[rw], weight_lo[rw], w_gate, w_up, w_down)
+        outs.append(residual[rw].astype(jnp.float32) + mixed)
+    layer_out = jnp.concatenate(outs, axis=0).astype(jnp.bfloat16)
     new_entries = compact(key_value_request, closure, tree_depth, accepted)
     return (layer_out, new_entries)
 

time: 251 us -> 251 us (level)
  blocking collectives: 30.9 us -> 69.2 us
  waiting for transfers between devices: 77 us -> 47.4 us
  starting transfers between devices: 21 us -> 12.4 us
  matrix products: 67 us -> 61.4 us
  local copies, waits for them, and re-layouts: 30.2 us -> 33.8 us
    all_to_all x0 -> x1, blocking collectives: none -> 38.6 us  [routed_whole(): lax.all_to_all(reshaped_rows, 'exp', split_axis=0, concat_axis=0, tiled=T...]
    all_to_all x2 -> x1, waiting for transfers between devices: 37.7 us -> 12.2 us  [routed_whole(): lax.all_to_all(reshaped_rows, 'exp', split_axis=0, concat_axis=0, tiled=T...]
    all_to_all x2 -> x1, starting transfers between devices: 12.2 us -> 3.95 us  [routed_whole(): lax.all_to_all(reshaped_rows, 'exp', split_axis=0, concat_axis=0, tiled=T...]
    dot_general x7 -> x8, matrix products: 14.6 us -> 6.43 us  [the longest x1 4.12 us: local(): jnp.dot(context_all, w_out_full, preferred_element_type=jnp.float32)]
    another operation x0 -> x2, local copies, waits for them, and re-layouts: none -> 4.26 us  [attend(): query_rows.reshape(tree_drafts, KEY_VALUE_HEADS, queries_per_group, HEAD_...]
    all_to_all x2, waiting for transfers between devices: 36.3 us -> 33.7 us  [routed_whole(): lax.all_to_all(produced, 'exp', split_axis=0, concat_axis=0, tiled=True)]
    unnamed x53 -> x35, local copies, waits for them, and re-layouts: 10.8 us -> 9.63 us
  transfers between devices with their start and end apart: 6 -> 5, of which waited for: 5 -> 3; matrix products, arithmetic and copies ran while one was open for 37% -> 37% of each run, Pallas kernels for 0% -> 0%
where the time goes in v7:
time: 251 us; the launch traced here: 250 us
  blocking collectives  69.2 us (28%)
  matrix products  61.4 us (24%)
  waiting for transfers between devices  47.4 us (19%)
  local copies, waits for them, and re-layouts  33.8 us (13%)
  between operations  14.5 us (6%)
  starting transfers between devices  12.4 us (5%)
  other arithmetic  11.6 us (5%)
    all_to_all x1, blocking collectives, routed_whole(): lax.all_to_all(reshaped_rows, 'exp', split_axis=0, concat_axis=0, tiled=T...  38.6 us
    all_to_all x2, waiting for transfers between devices, routed_whole(): lax.all_to_all(produced, 'exp', split_axis=0, concat_axis=0, tiled=True)  33.7 us
    dot_general x2, matrix products, expert_products(): jnp.einsum('pekf,efd->pekd', hidden, w_down, preferred_element_type=jnp.f...  20.8 us
    all_gather x1, blocking collectives, local(): lax.all_gather(value_projection, 'req', axis=0, tiled=True)  16.9 us
    all_gather x1, blocking collectives, local(): lax.all_gather(key_projection, 'req', axis=0, tiled=True)  13.7 us
    dot_general x2, matrix products, expert_products(): jnp.einsum('pekd,edf->pekf', received, w_up, preferred_element_type=jnp.f...  13 us
    all_to_all x1, waiting for transfers between devices, routed_whole(): lax.all_to_all(reshaped_rows, 'exp', split_axis=0, concat_axis=0, tiled=T...  12.2 us
    unnamed x35, local copies, waits for them, and re-layouts  9.63 us
  transfers between devices with their start and end apart: 5, of which 3 were waited for; matrix products, arithmetic and copies ran while one was open for 37% of the time, Pallas kernels for 0%

profile of v7, /device:TPU:0, one launch (start us, length us, event | category | flops | bytes accessed | tf_op | source)
XLA Modules:
  0.0 250.4 jit_solution(7681561555885589700)
XLA Ops:
  10.7 4.6 %fusion.113 = (bf16[4,1024,256]{2,1,0:T(8,128)(2,1)}, bf16[4,1024,256]{2,1,0:T(8,128)(2,1)}) fusion(bf16[4,1024,512]{2,1,0:T(8,128)(2,1)} %param.30), kind=kLoop, calls=%fused_computation.135 | loop fusion | bytes 8388608 | tf_op jit(solution)/shard_map/vmap()/slice | solution.py:66
  15.3 16.9 %all_gather.14 = bf16[1536,256]{1,0:T(8,128)(2,1)} all-gather(bf16[192,256]{1,0:T(8,128)(2,1)S(1)} %copy-done.8), channel_id=1, replica_groups=mesh['req'=8,'exp'=16] {'req'}, dimensions={0}, use_global_device_ids=true | all-gather | bytes 884736 | tf_op jit(solution)/shard_map/all_gather | solution.py:208
  32.7 3.0 %copy.146 = bf16[4,1024,256]{1,2,0:T(8,128)(2,1)S(1)} copy(bf16[4,1024,256]{2,1,0:T(8,128)(2,1)} %get-tuple-element.24) | data formatting | bytes 4194304
  38.0 4.1 %copy.147 = bf16[4,1024,256]{1,2,0:T(8,128)(2,1)} copy(bf16[4,1024,256]{2,1,0:T(8,128)(2,1)} %get-tuple-element.23) | data formatting | bytes 4194304
  44.0 13.7 %all_gather.13 = bf16[1536,256]{1,0:T(8,128)(2,1)S(1)} all-gather(bf16[192,256]{1,0:T(8,128)(2,1)S(1)} %copy-done.9), channel_id=1, replica_groups=mesh['req'=8,'exp'=16] {'req'}, dimensions={0}, use_global_device_ids=true | all-gather | bytes 884736 | tf_op jit(solution)/shard_map/all_gather | solution.py:203
  58.1 4.1 %fusion.110 = f32[256,1536]{1,0:T(8,128)S(1)} fusion(bf16[1536,1536]{1,0:T(8,128)(2,1)} %all-gather.3.cloned.1.call-done, bf16[256,1536]{1,0:T(8,128)(2,1)S(1)} %copy-done.5, f32[1536]{0:T(1024)S(1)} %copy-done.14, f32[256]{0:T(256)S(1)} %add_rsqrt_fusion.1), kind=kOutput, calls=%fused_computation.133 | convolution fusion | flops 1209532416 | bytes 7085056 | tf_op jit(solution)/shard_map/dot_general | solution.py:196
  63.6 2.8 %copy.102 = f32[256,1792]{0,1:T(8,128)} copy(f32[256,1792]{1,0:T(8,128)} %pad_maximum_fusion) | data formatting | bytes 3670016 | tf_op jit(solution)/shard_map/concatenate | solution.py:211
  76.0 3.1 %fusion.1 = f32[4,2,6,64]{3,2,1,0:T(8,128)S(1)} fusion(f32[4,2,64,6,1024]{4,2,3,1,0:T(8,128)S(1)} %get-tuple-element.38, f32[4,2,6,64]{3,2,1,0:T(8,128)S(1)} %max.25, pred[4,1024]{1,0:T(4,128)(4,1)S(1)} %iota_compare_fusion.6), kind=kLoop, calls=%fused_computation.7 | loop fusion | flops 12579840 | bytes 12611584 | tf_op jit(solution)/shard_map/vmap()/reduce_sum | solution.py:91
  80.8 3.9 %fusion.40 = bf16[4,64,2,6,128]{4,1,3,2,0:T(8,128)(2,1)S(1)} fusion(f32[4,2,128,6,64]{2,4,3,1,0:T(8,128)S(1)} %fusion.74, bf16[4,1024,2,128,1]{1,3,4,2,0:T(8,128)(2,1)S(1)} %bitcast.131, f32[4,2,64,6,1024]{4,2,3,1,0:T(8,128)S(1)} %get-tuple-element.38, f32[4,2,6,64]{3,2,1,0:T(8,128)S(1)} %add.97, f32[4,2,6,64]{3,2,1,0:T(8,128)S(1)} %max.25, ...), kind=kOutput, calls=%fused_computation.50 | convolution fusion | flops 821821440 | bytes 17068032 | tf_op jit(solution)/shard_map/vmap(gsij,jgd->igsd)/dot_general | solution.py:96
  86.2 4.1 %fusion.33 = (f32[256]{0:T(256)S(1)}, bf16[256,1536]{1,0:T(8,128)(2,1)S(1)}) fusion(bf16[256,1536]{1,0:T(8,128)(2,1)S(1)} %convert_element_type.137, bf16[1536,1536]{0,1:T(8,128)(2,1)} %all-gather.5.cloned.1.call-done, bf16[256,1536]{1,0:T(8,128)(2,1)} %param.18), kind=kOutput, calls=%fused_computation.42 | convolution fusion | flops 1210318592 | bytes 7078912 | tf_op jit(solution)/shard_map/dot_general | solution.py:224
  93.7 38.6 %all_to_all.20 = bf16[16,2,24,1536]{3,2,1,0:T(8,128)(2,1)} all-to-all(bf16[16,2,24,1536]{3,2,1,0:T(8,128)(2,1)S(1)} %bitcast.125), channel_id=1, replica_groups=mesh['req'=8,'exp'=16] {'exp'}, dimensions={0} | all-to-all | bytes 4718592 | tf_op jit(solution)/shard_map/all_to_all | solution.py:164
  132.4 3.9 %all-to-all-start = ((bf16[16,2,24,1536]{3,2,1,0:T(8,128)(2,1)}), bf16[16,2,24,1536]{3,2,1,0:T(8,128)(2,1)S(1)}, u32[]{:S(2)}, u32[]{:S(2)}) async-start(bf16[16,2,24,1536]{3,2,1,0:T(8,128)(2,1)} %bitcast.14), calls=%async_computation | async-start | bytes 4718592 | tf_op jit(solution)/shard_map/all_to_all | solution.py:164
  136.3 6.5 %fusion.7 = f32[2,16,24,768]{3,2,1,0:T(8,128)} fusion(bf16[2,1536,768]{2,1,0:T(8,128)(2,1)} %param.26, bf16[16,2,24,1536]{3,2,1,0:T(8,128)(2,1)} %all_to_all.20), kind=kOutput, calls=%fused_computation.13 | convolution fusion | flops 1811939328 | bytes 9437184 | tf_op jit(solution)/shard_map/pekd,edf->pekf/dot_general | solution.py:142
  142.8 10.4 %fusion.22 = bf16[16,2,24,1536]{3,2,0,1:T(8,128)(2,1)} fusion(bf16[2,768,1536]{2,1,0:T(8,128)(2,1)} %param.27, f32[2,16,24,768]{3,2,1,0:T(8,128)} %fusion.7, bf16[2,1536,768]{2,1,0:T(8,128)(2,1)} %param.25, bf16[16,2,24,1536]{3,2,1,0:T(8,128)(2,1)} %all_to_all.20), kind=kOutput, calls=%fused_computation.26 | convolution fusion | flops 3626827776 | bytes 16515072 | tf_op jit(solution)/shard_map/pekf,efd->pekd/dot_general | solution.py:144
  153.2 3.4 %copy.122 = bf16[16,2,24,1536]{3,2,1,0:T(8,128)(2,1)} copy(bf16[16,2,24,1536]{3,2,0,1:T(8,128)(2,1)} %fusion.22) | data formatting | bytes 4718592 | tf_op jit(solution)/shard_map/convert_element_type | solution.py:144
  156.6 12.2 %all-to-all-done = bf16[16,2,24,1536]{3,2,1,0:T(8,128)(2,1)S(1)} async-done(((bf16[16,2,24,1536]{3,2,1,0:T(8,128)(2,1)}), bf16[16,2,24,1536]{3,2,1,0:T(8,128)(2,1)S(1)}, u32[]{:S(2)}, u32[]{:S(2)}) %all-to-all-start) | async-done | bytes 2359328 | tf_op jit(solution)/shard_map/all_to_all | solution.py:164
  170.2 3.9 %all-to-all-start.3 = ((bf16[16,2,24,1536]{3,2,1,0:T(8,128)(2,1)}), bf16[16,2,24,1536]{3,2,1,0:T(8,128)(2,1)S(1)}, u32[]{:S(2)}, u32[]{:S(2)}) async-start(bf16[16,2,24,1536]{3,2,1,0:T(8,128)(2,1)} %copy.122), calls=%async_computation.3 | async-start | bytes 4718592 | tf_op jit(solution)/shard_map/all_to_all | solution.py:169
  174.1 6.5 %fusion.9 = f32[2,16,24,768]{3,2,1,0:T(8,128)} fusion(bf16[2,1536,768]{2,1,0:T(8,128)(2,1)} %param.26, bf16[16,2,24,1536]{3,2,1,0:T(8,128)(2,1)} %copy-done.1), kind=kOutput, calls=%fused_computation.15 | convolution fusion | flops 1811939328 | bytes 9437184 | tf_op jit(solution)/shard_map/pekd,edf->pekf/dot_general | solution.py:142
  180.6 10.4 %fusion.25 = bf16[16,2,24,1536]{3,2,0,1:T(8,128)(2,1)} fusion(bf16[2,768,1536]{2,1,0:T(8,128)(2,1)} %param.27, f32[2,16,24,768]{3,2,1,0:T(8,128)} %fusion.9, bf16[2,1536,768]{2,1,0:T(8,128)(2,1)} %param.25, bf16[16,2,24,1536]{3,2,1,0:T(8,128)(2,1)} %copy-done.1), kind=kOutput, calls=%fused_computation.27 | convolution fusion | flops 3626827776 | bytes 16515072 | tf_op jit(solution)/shard_map/pekf,efd->pekd/dot_general | solution.py:144
  191.0 3.4 %copy.119 = bf16[16,2,24,1536]{3,2,1,0:T(8,128)(2,1)} copy(bf16[16,2,24,1536]{3,2,0,1:T(8,128)(2,1)} %fusion.25) | data formatting | bytes 4718592 | tf_op jit(solution)/shard_map/convert_element_type | solution.py:144
  194.4 10.1 %all-to-all-done.3 = bf16[16,2,24,1536]{3,2,1,0:T(8,128)(2,1)S(1)} async-done(((bf16[16,2,24,1536]{3,2,1,0:T(8,128)(2,1)}), bf16[16,2,24,1536]{3,2,1,0:T(8,128)(2,1)S(1)}, u32[]{:S(2)}, u32[]{:S(2)}) %all-to-all-start.3) | async-done | bytes 2359328 | tf_op jit(solution)/shard_map/all_to_all | solution.py:169
  204.5 4.6 %all-to-all-start.1 = ((bf16[16,2,24,1536]{3,2,1,0:T(8,128)(2,1)}), bf16[16,2,24,1536]{3,2,1,0:T(8,128)(2,1)}, u32[]{:S(2)}, u32[]{:S(2)}) async-start(bf16[16,2,24,1536]{3,2,1,0:T(8,128)(2,1)} %copy.119), calls=%async_computation.1 | async-start | bytes 4718592 | tf_op jit(solution)/shard_map/all_to_all | solution.py:169
  213.1 3.0 %fusion.79 = f32[256,1536]{1,0:T(8,128)} fusion(bf16[768,1536]{1,0:T(8,128)(2,1)S(1)} %bitcast.124, bf16[128,768]{1,0:T(8,128)(2,1)} %get-tuple-element.43, bf16[128,768]{1,0:T(8,128)(2,1)} %get-tuple-element.30), kind=kOutput, calls=%fused_computation.77 | convolution fusion | flops 604766208 | bytes 4325376 | tf_op jit(solution)/shard_map/dot_general | solution.py:154
  216.1 23.6 %all-to-all-done.1 = bf16[16,2,24,1536]{3,2,1,0:T(8,128)(2,1)} async-done(((bf16[16,2,24,1536]{3,2,1,0:T(8,128)(2,1)}), bf16[16,2,24,1536]{3,2,1,0:T(8,128)(2,1)}, u32[]{:S(2)}, u32[]{:S(2)}) %all-to-all-start.1) | async-done | bytes 2359328 | tf_op jit(solution)/shard_map/all_to_all | solution.py:169
  (107 shorter events, 36.2 us)
Async XLA Ops:
  7.2 51.0 %all-gather.3.cloned.1.call-start = ((), (), s32[]{:S(2)}) async-start(), calls=%async_computation.4 | async-start | bytes 5308416 | tf_op jit(solution)/shard_map/all_gather | solution.py:198
  7.9 78.3 %all-gather.5.cloned.1.call-start = ((), (), s32[]{:S(2)}) async-start(), calls=%async_computation.5 | async-start | bytes 5308416 | tf_op jit(solution)/shard_map/all_gather | solution.py:218
  10.7 4.6 %copy-start.8 = (bf16[192,256]{1,0:T(8,128)(2,1)S(1)}, bf16[192,256]{1,0:T(8,128)(2,1)}, u32[]{:S(2)}) copy-start(bf16[192,256]{1,0:T(8,128)(2,1)} %param.22) | copy-start | bytes 294916
  10.7 21.5 %copy-start.13 = (s32[4]{0:T(128)S(1)}, s32[4]{0:T(128)}, u32[]{:S(2)}) copy-start(s32[4]{0:T(128)} %param.31) | copy-start | bytes 52
  10.7 21.6 %copy-start.5 = (bf16[256,1536]{1,0:T(8,128)(2,1)S(1)}, bf16[256,1536]{1,0:T(8,128)(2,1)}, u32[]{:S(2)}) copy-start(bf16[256,1536]{1,0:T(8,128)(2,1)} %param.18) | copy-start | bytes 2359300
  32.2 3.5 %copy-start.14 = (f32[1536]{0:T(1024)S(1)}, f32[1536]{0:T(1024)}, u32[]{:S(2)}) copy-start(f32[1536]{0:T(1024)} %param.19) | copy-start | bytes 18436
  37.3 5.1 %copy-start.6 = (bf16[256,256]{1,0:T(8,128)(2,1)}, bf16[256,256]{1,0:T(8,128)(2,1)S(1)}, u32[]{:S(2)}) copy-start(bf16[256,256]{1,0:T(8,128)(2,1)S(1)} %convolution_convert_fusion.1) | copy-start | bytes 393220
  37.3 4.8 %copy-start.10 = (s32[256,4]{0,1:T(4,128)S(1)}, s32[256,4]{0,1:T(4,128)}, u32[]{:S(2)}) copy-start(s32[256,4]{0,1:T(4,128)} %param.28) | copy-start | bytes 12292
  38.0 6.0 %copy-start.9 = (bf16[192,256]{1,0:T(8,128)(2,1)S(1)}, bf16[192,256]{1,0:T(8,128)(2,1)}, u32[]{:S(2)}) copy-start(bf16[192,256]{1,0:T(8,128)(2,1)} %param.21) | copy-start | bytes 294916
  76.0 3.1 %copy-start.7 = (bf16[4,64,2,128]{3,2,1,0:T(2,128)(2,1)S(1)}, bf16[4,64,2,128]{3,2,1,0:T(2,128)(2,1)}, u32[]{:S(2)}) copy-start(bf16[4,64,2,128]{3,2,1,0:T(2,128)(2,1)} %reshape.286) | copy-start | bytes 393220
  79.2 1.6 copy-start.2
  86.1 4.2 %copy-start.11 = (f32[1536]{0:T(1024)S(1)}, f32[1536]{0:T(1024)}, u32[]{:S(2)}) copy-start(f32[1536]{0:T(1024)} %param.24) | copy-start | bytes 18436
  86.2 4.4 %copy-start.3 = (bf16[256,768]{1,0:T(8,128)(2,1)S(1)}, bf16[256,768]{1,0:T(8,128)(2,1)}, u32[]{:S(2)}) copy-start(bf16[256,768]{1,0:T(8,128)(2,1)} %fusion.39) | copy-start | bytes 1179652
  132.4 36.5 %all-to-all-start = ((bf16[16,2,24,1536]{3,2,1,0:T(8,128)(2,1)}), bf16[16,2,24,1536]{3,2,1,0:T(8,128)(2,1)S(1)}, u32[]{:S(2)}, u32[]{:S(2)}) async-start(bf16[16,2,24,1536]{3,2,1,0:T(8,128)(2,1)} %bitcast.14), calls=%async_computation | async-start | bytes 4718592 | tf_op jit(solution)/shard_map/all_to_all | solution.py:164
  168.8 1.4 copy-start.1
  170.2 34.3 %all-to-all-start.3 = ((bf16[16,2,24,1536]{3,2,1,0:T(8,128)(2,1)}), bf16[16,2,24,1536]{3,2,1,0:T(8,128)(2,1)S(1)}, u32[]{:S(2)}, u32[]{:S(2)}) async-start(bf16[16,2,24,1536]{3,2,1,0:T(8,128)(2,1)} %copy.122), calls=%async_computation.3 | async-start | bytes 4718592 | tf_op jit(solution)/shard_map/all_to_all | solution.py:169
  194.4 14.7 %copy-start.15 = (s32[4]{0:T(128)S(1)}, s32[4]{0:T(128)}, u32[]{:S(2)}) copy-start(s32[4]{0:T(128)} %param.33) | copy-start | bytes 52
  194.4 15.3 %copy-start.12 = (f32[256,4]{0,1:T(4,128)S(1)}, f32[256,4]{0,1:T(4,128)}, u32[]{:S(2)}) copy-start(f32[256,4]{0,1:T(4,128)} %param.29) | copy-start | bytes 12292
  204.5 35.2 %all-to-all-start.1 = ((bf16[16,2,24,1536]{3,2,1,0:T(8,128)(2,1)}), bf16[16,2,24,1536]{3,2,1,0:T(8,128)(2,1)}, u32[]{:S(2)}, u32[]{:S(2)}) async-start(bf16[16,2,24,1536]{3,2,1,0:T(8,128)(2,1)} %copy.119), calls=%async_computation.1 | async-start | bytes 4718592 | tf_op jit(solution)/shard_map/all_to_all | solution.py:169
  211.2 28.5 %copy-start.4 = (bf16[128,768]{1,0:T(8,128)(2,1)S(1)}, bf16[128,768]{1,0:T(8,128)(2,1)}, u32[]{:S(2)}) copy-start(bf16[128,768]{1,0:T(8,128)(2,1)} %get-tuple-element.29) | copy-start | bytes 589828
  216.1 26.2 %copy-start = (f32[256,1536]{1,0:T(8,128)S(1)}, f32[256,1536]{1,0:T(8,128)}, u32[]{:S(2)}) copy-start(f32[256,1536]{1,0:T(8,128)} %fusion.79) | copy-start | bytes 4718596
Sparse Core Ops, SparseCore 0:
  9.7 38.5 all-gather.2
  49.9 34.2 all-gather.4

commit v8 on v4

--- a/solution.py
+++ b/solution.py
@@ -47,8 +47,12 @@
     node_index = jnp.arange(node_count, dtype=jnp.int32)
     parent_step = (parents[..., :, None] == node_index[None, None, :]).astype(jnp.float32)
     closure = jnp.maximum(parent_step, jnp.eye(node_count, dtype=jnp.float32)[None])
-    for squaring in range(max(1, (node_count - 1).bit_length())):
-        closure = jnp.minimum(jnp.einsum("rij,rjk->rik", closure, closure), 1.0)
+    closure = lax.fori_loop(
+        0,
+        max(1, (node_count - 1).bit_length()),
+        lambda step, held: jnp.minimum(jnp.einsum("rij,rjk->rik", held, held), 1.0),
+        closure,
+    )
     tree_depth = jnp.sum(closure, axis=-1).astype(jnp.int32) - 1
     return (closure, tree_depth)
 
@@ -204,8 +208,9 @@
         lax.all_gather(value_projection, "req", axis=0, tiled=True),
         preferred_element_type=jnp.float32,
     )
-    query_rows = rotate(query_sum, positions).astype(jnp.bfloat16)
-    tree_key_value = jnp.concatenate([rotate(key_sum, positions), value_sum], axis=1).astype(
+    turned = rotate(jnp.concatenate([query_sum, key_sum], axis=1), positions)
+    query_rows = turned[:, : query_sum.shape[1]].astype(jnp.bfloat16)
+    tree_key_value = jnp.concatenate([turned[:, query_sum.shape[1] :], value_sum], axis=1).astype(
         jnp.bfloat16
     )
     query_req = query_rows.reshape(local_reqs, DRAFT_TOKENS, query_rows.shape[1])

time: 251 us -> 255 us (1.016)
  other arithmetic: 9.53 us -> 12.4 us
    all_to_all x2, waiting for transfers between devices: 37.7 us -> 42 us  [routed_whole(): lax.all_to_all(reshaped_rows, 'exp', split_axis=0, concat_axis=0, tiled=T...]
    another operation x0 -> x2, local copies, waits for them, and re-layouts: none -> 4.26 us  [attend(): query_rows.reshape(tree_drafts, KEY_VALUE_HEADS, queries_per_group, HEAD_...]
    unnamed x53 -> x43, local copies, waits for them, and re-layouts: 10.8 us -> 8.29 us
  transfers between devices with their start and end apart: 6 -> 6, of which waited for: 5 -> 4; matrix products, arithmetic and copies ran while one was open for 37% -> 38% of each run, Pallas kernels for 0% -> 0%
where the time goes in v8:
time: 255 us; the launch traced here: 254 us
  waiting for transfers between devices  79 us (31%)
  matrix products  65 us (25%)
  blocking collectives  31.3 us (12%)
  local copies, waits for them, and re-layouts  30 us (12%)
  starting transfers between devices  21.5 us (8%)
  between operations  14.6 us (6%)
  other arithmetic  12.4 us (5%)
    all_to_all x2, waiting for transfers between devices, routed_whole(): lax.all_to_all(reshaped_rows, 'exp', split_axis=0, concat_axis=0, tiled=T...  42 us
    all_to_all x2, waiting for transfers between devices, routed_whole(): lax.all_to_all(produced, 'exp', split_axis=0, concat_axis=0, tiled=True)  35.6 us
    dot_general x2, matrix products, expert_products(): jnp.einsum('pekf,efd->pekd', hidden, w_down, preferred_element_type=jnp.f...  19.4 us
    all_gather x1, blocking collectives, local(): lax.all_gather(value_projection, 'req', axis=0, tiled=True)  17.5 us
    all_gather x1, blocking collectives, local(): lax.all_gather(key_projection, 'req', axis=0, tiled=True)  13.9 us
    dot_general x2, matrix products, expert_products(): jnp.einsum('pekd,edf->pekf', received, w_up, preferred_element_type=jnp.f...  13 us
    all_to_all x2, starting transfers between devices, routed_whole(): lax.all_to_all(reshaped_rows, 'exp', split_axis=0, concat_axis=0, tiled=T...  12.9 us
    all_to_all x2, starting transfers between devices, routed_whole(): lax.all_to_all(produced, 'exp', split_axis=0, concat_axis=0, tiled=True)  8.57 us
  transfers between devices with their start and end apart: 6, of which 4 were waited for; matrix products, arithmetic and copies ran while one was open for 38% of the time, Pallas kernels for 0%

profile of v8, /device:TPU:0, one launch (start us, length us, event | category | flops | bytes accessed | tf_op | source)
XLA Modules:
  0.0 254.0 jit_solution(11154082486473080834)
XLA Ops:
  12.1 4.6 %fusion.120 = (bf16[4,1024,256]{2,1,0:T(8,128)(2,1)}, bf16[4,1024,256]{2,1,0:T(8,128)(2,1)}) fusion(bf16[4,1024,512]{2,1,0:T(8,128)(2,1)} %param.30), kind=kLoop, calls=%fused_computation.146 | loop fusion | bytes 8388608 | tf_op jit(solution)/shard_map/vmap()/slice | solution.py:66
  16.6 17.5 %all_gather.14 = bf16[1536,256]{1,0:T(8,128)(2,1)} all-gather(bf16[192,256]{1,0:T(8,128)(2,1)S(1)} %copy-done.12), channel_id=1, replica_groups=mesh['req'=8,'exp'=16] {'req'}, dimensions={0}, use_global_device_ids=true | all-gather | bytes 884736 | tf_op jit(solution)/shard_map/all_gather | solution.py:208
  34.4 3.0 %copy.145 = bf16[4,1024,256]{1,2,0:T(8,128)(2,1)S(1)} copy(bf16[4,1024,256]{2,1,0:T(8,128)(2,1)} %get-tuple-element.22) | data formatting | bytes 4194304
  39.7 4.1 %copy.146 = bf16[4,1024,256]{1,2,0:T(8,128)(2,1)} copy(bf16[4,1024,256]{2,1,0:T(8,128)(2,1)} %get-tuple-element.21) | data formatting | bytes 4194304
  45.8 13.9 %all_gather.13 = bf16[1536,256]{1,0:T(8,128)(2,1)S(1)} all-gather(bf16[192,256]{1,0:T(8,128)(2,1)S(1)} %copy-done.13), channel_id=1, replica_groups=mesh['req'=8,'exp'=16] {'req'}, dimensions={0}, use_global_device_ids=true | all-gather | bytes 884736 | tf_op jit(solution)/shard_map/all_gather | solution.py:203
  60.1 4.2 %fusion.118 = f32[256,1536]{1,0:T(8,128)S(1)} fusion(bf16[1536,1536]{1,0:T(8,128)(2,1)} %all-gather.3.cloned.1.call-done, bf16[256,1536]{1,0:T(8,128)(2,1)S(1)} %copy-done.2, f32[1536]{0:T(1024)S(1)} %copy-done.18, f32[256]{0:T(256)S(1)} %add_rsqrt_fusion), kind=kOutput, calls=%fused_computation.145 | convolution fusion | flops 1209532416 | bytes 7085056 | tf_op jit(solution)/shard_map/dot_general | solution.py:196
  65.6 2.8 %copy.102 = f32[256,1792]{0,1:T(8,128)} copy(f32[256,1792]{1,0:T(8,128)} %pad_maximum_fusion) | data formatting | bytes 3670016 | tf_op jit(solution)/shard_map/concatenate | solution.py:211
  78.1 3.1 %fusion.1 = f32[4,2,6,64]{3,2,1,0:T(8,128)S(1)} fusion(f32[4,2,64,6,1024]{4,2,3,1,0:T(8,128)S(1)} %get-tuple-element.36, f32[4,2,6,64]{3,2,1,0:T(8,128)S(1)} %max.25, pred[4,1024]{1,0:T(4,128)(4,1)S(1)} %iota_compare_fusion.6), kind=kLoop, calls=%fused_computation.7 | loop fusion | flops 12579840 | bytes 12611584 | tf_op jit(solution)/shard_map/vmap()/reduce_sum | solution.py:91
  82.9 3.9 %fusion.40 = bf16[4,64,2,6,128]{4,1,3,2,0:T(8,128)(2,1)S(1)} fusion(f32[4,2,128,6,64]{2,4,3,1,0:T(8,128)S(1)} %fusion.74, bf16[4,1024,2,128,1]{1,3,4,2,0:T(8,128)(2,1)S(1)} %bitcast.127, f32[4,2,64,6,1024]{4,2,3,1,0:T(8,128)S(1)} %get-tuple-element.36, f32[4,2,6,64]{3,2,1,0:T(8,128)S(1)} %add.112, f32[4,2,6,64]{3,2,1,0:T(8,128)S(1)} %max.25, ...), kind=kOutput, calls=%fused_computation.49 | convolution fusion | flops 821821440 | bytes 17068032 | tf_op jit(solution)/shard_map/vmap(gsij,jgd->igsd)/dot_general | solution.py:96
  88.4 4.1 %multiply_reduce_fusion.1 = (f32[128]{0:T(128)S(1)}, f32[128,1536]{1,0:T(8,128)S(1)}) fusion(bf16[128,1536]{1,0:T(8,128)(2,1)S(1)} %slice.80, bf16[1536,1536]{0,1:T(8,128)(2,1)} %all-gather.5.cloned.1.call-done, bf16[256,1536]{1,0:T(8,128)(2,1)S(1)} %copy-done.3), kind=kOutput, calls=%fused_computation.73 | convolution fusion | flops 605159296 | bytes 6291968 | tf_op jit(solution)/shard_map/dot_general | solution.py:227
  94.9 7.2 %all-to-all-start = ((bf16[16,2,24,1536]{3,2,1,0:T(8,128)(2,1)}), bf16[16,2,24,1536]{3,2,1,0:T(8,128)(2,1)}, u32[]{:S(2)}, u32[]{:S(2)}) async-start(bf16[16,2,24,1536]{3,2,1,0:T(8,128)(2,1)} %bitcast.12), calls=%async_computation | async-start | bytes 4718592 | tf_op jit(solution)/shard_map/all_to_all | solution.py:164
  102.8 4.1 %multiply_reduce_fusion = (f32[128]{0:T(128)S(1)}, f32[128,1536]{1,0:T(8,128)S(1)}) fusion(bf16[128,1536]{1,0:T(8,128)(2,1)S(1)} %slice.88, bf16[1536,1536]{0,1:T(8,128)(2,1)} %all-gather.5.cloned.1.call-done, bf16[256,1536]{1,0:T(8,128)(2,1)S(1)} %copy-done.3), kind=kOutput, calls=%fused_computation.71 | convolution fusion | flops 605159296 | bytes 6291968 | tf_op jit(solution)/shard_map/dot_general | solution.py:227
  109.2 26.6 %all-to-all-done = bf16[16,2,24,1536]{3,2,1,0:T(8,128)(2,1)} async-done(((bf16[16,2,24,1536]{3,2,1,0:T(8,128)(2,1)}), bf16[16,2,24,1536]{3,2,1,0:T(8,128)(2,1)}, u32[]{:S(2)}, u32[]{:S(2)}) %all-to-all-start) | async-done | bytes 2359328 | tf_op jit(solution)/shard_map/all_to_all | solution.py:164
  135.7 5.7 %all-to-all-start.2 = ((bf16[16,2,24,1536]{3,2,1,0:T(8,128)(2,1)}), bf16[16,2,24,1536]{3,2,1,0:T(8,128)(2,1)}, u32[]{:S(2)}, u32[]{:S(2)}) async-start(bf16[16,2,24,1536]{3,2,1,0:T(8,128)(2,1)} %bitcast.22), calls=%async_computation.2 | async-start | bytes 4718592 | tf_op jit(solution)/shard_map/all_to_all | solution.py:164
  141.5 6.5 %fusion.9 = f32[2,16,24,768]{3,2,1,0:T(8,128)} fusion(bf16[2,1536,768]{2,1,0:T(8,128)(2,1)} %param.26, bf16[16,2,24,1536]{3,2,1,0:T(8,128)(2,1)} %all-to-all-done), kind=kOutput, calls=%fused_computation.15 | convolution fusion | flops 1811939328 | bytes 9437184 | tf_op jit(solution)/shard_map/pekd,edf->pekf/dot_general | solution.py:142
  148.0 9.0 %fusion.25 = bf16[16,2,24,1536]{3,2,0,1:T(8,128)(2,1)S(1)} fusion(bf16[2,768,1536]{2,1,0:T(8,128)(2,1)} %param.27, f32[2,16,24,768]{3,2,1,0:T(8,128)} %fusion.9, bf16[2,1536,768]{2,1,0:T(8,128)(2,1)} %param.25, bf16[16,2,24,1536]{3,2,1,0:T(8,128)(2,1)} %all-to-all-done), kind=kOutput, calls=%fused_computation.27 | convolution fusion | flops 3626827776 | bytes 16515072 | tf_op jit(solution)/shard_map/pekf,efd->pekd/dot_general | solution.py:144
  158.7 15.4 %all-to-all-done.2 = bf16[16,2,24,1536]{3,2,1,0:T(8,128)(2,1)} async-done(((bf16[16,2,24,1536]{3,2,1,0:T(8,128)(2,1)}), bf16[16,2,24,1536]{3,2,1,0:T(8,128)(2,1)}, u32[]{:S(2)}, u32[]{:S(2)}) %all-to-all-start.2) | async-done | bytes 2359328 | tf_op jit(solution)/shard_map/all_to_all | solution.py:164
  174.1 4.0 %all-to-all-start.1 = ((bf16[16,2,24,1536]{3,2,1,0:T(8,128)(2,1)}), bf16[16,2,24,1536]{3,2,1,0:T(8,128)(2,1)S(1)}, u32[]{:S(2)}, u32[]{:S(2)}) async-start(bf16[16,2,24,1536]{3,2,1,0:T(8,128)(2,1)} %copy.118), calls=%async_computation.1 | async-start | bytes 4718592 | tf_op jit(solution)/shard_map/all_to_all | solution.py:169
  178.8 6.5 %fusion.7 = f32[2,16,24,768]{3,2,1,0:T(8,128)} fusion(bf16[2,1536,768]{2,1,0:T(8,128)(2,1)} %param.26, bf16[16,2,24,1536]{3,2,1,0:T(8,128)(2,1)} %all-to-all-done.2), kind=kOutput, calls=%fused_computation.13 | convolution fusion | flops 1811939328 | bytes 9437184 | tf_op jit(solution)/shard_map/pekd,edf->pekf/dot_general | solution.py:142
  185.2 10.4 %fusion.22 = bf16[16,2,24,1536]{3,2,0,1:T(8,128)(2,1)} fusion(bf16[2,768,1536]{2,1,0:T(8,128)(2,1)} %param.27, f32[2,16,24,768]{3,2,1,0:T(8,128)} %fusion.7, bf16[2,1536,768]{2,1,0:T(8,128)(2,1)} %param.25, bf16[16,2,24,1536]{3,2,1,0:T(8,128)(2,1)} %all-to-all-done.2), kind=kOutput, calls=%fused_computation.26 | convolution fusion | flops 3626827776 | bytes 16515072 | tf_op jit(solution)/shard_map/pekf,efd->pekd/dot_general | solution.py:144
  195.7 3.4 %copy.122 = bf16[16,2,24,1536]{3,2,1,0:T(8,128)(2,1)} copy(bf16[16,2,24,1536]{3,2,0,1:T(8,128)(2,1)} %fusion.22) | data formatting | bytes 4718592 | tf_op jit(solution)/shard_map/convert_element_type | solution.py:144
  199.0 9.4 %all-to-all-done.1 = bf16[16,2,24,1536]{3,2,1,0:T(8,128)(2,1)S(1)} async-done(((bf16[16,2,24,1536]{3,2,1,0:T(8,128)(2,1)}), bf16[16,2,24,1536]{3,2,1,0:T(8,128)(2,1)S(1)}, u32[]{:S(2)}, u32[]{:S(2)}) %all-to-all-start.1) | async-done | bytes 2359328 | tf_op jit(solution)/shard_map/all_to_all | solution.py:169
  208.5 4.5 %all-to-all-start.3 = ((bf16[16,2,24,1536]{3,2,1,0:T(8,128)(2,1)}), bf16[16,2,24,1536]{3,2,1,0:T(8,128)(2,1)}, u32[]{:S(2)}, u32[]{:S(2)}) async-start(bf16[16,2,24,1536]{3,2,1,0:T(8,128)(2,1)} %copy.122), calls=%async_computation.3 | async-start | bytes 4718592 | tf_op jit(solution)/shard_map/all_to_all | solution.py:169
  217.5 26.2 %all-to-all-done.3 = bf16[16,2,24,1536]{3,2,1,0:T(8,128)(2,1)} async-done(((bf16[16,2,24,1536]{3,2,1,0:T(8,128)(2,1)}), bf16[16,2,24,1536]{3,2,1,0:T(8,128)(2,1)}, u32[]{:S(2)}, u32[]{:S(2)}) %all-to-all-start.3) | async-done | bytes 2359328 | tf_op jit(solution)/shard_map/all_to_all | solution.py:169
  (121 shorter events, 40.4 us)
Async XLA Ops:
  7.2 52.9 %all-gather.3.cloned.1.call-start = ((), (), s32[]{:S(2)}) async-start(), calls=%async_computation.4 | async-start | bytes 5308416 | tf_op jit(solution)/shard_map/all_gather | solution.py:198
  7.9 80.5 %all-gather.5.cloned.1.call-start = ((), (), s32[]{:S(2)}) async-start(), calls=%async_computation.5 | async-start | bytes 5308416 | tf_op jit(solution)/shard_map/all_gather | solution.py:218
  12.0 4.6 %copy-start.12 = (bf16[192,256]{1,0:T(8,128)(2,1)S(1)}, bf16[192,256]{1,0:T(8,128)(2,1)}, u32[]{:S(2)}) copy-start(bf16[192,256]{1,0:T(8,128)(2,1)} %param.22) | copy-start | bytes 294916
  12.0 22.1 %copy-start.17 = (s32[4]{0:T(128)S(1)}, s32[4]{0:T(128)}, u32[]{:S(2)}) copy-start(s32[4]{0:T(128)} %param.31) | copy-start | bytes 52
  16.6 20.8 %copy-start.2 = (bf16[256,1536]{1,0:T(8,128)(2,1)S(1)}, bf16[256,1536]{1,0:T(8,128)(2,1)}, u32[]{:S(2)}) copy-start(bf16[256,1536]{1,0:T(8,128)(2,1)} %param.18) | copy-start | bytes 2359300
  16.6 20.8 %copy-start.18 = (f32[1536]{0:T(1024)S(1)}, f32[1536]{0:T(1024)}, u32[]{:S(2)}) copy-start(f32[1536]{0:T(1024)} %param.19) | copy-start | bytes 18436
  39.0 5.2 %copy-start.9 = (bf16[256,256]{1,0:T(8,128)(2,1)}, bf16[256,256]{1,0:T(8,128)(2,1)S(1)}, u32[]{:S(2)}) copy-start(bf16[256,256]{1,0:T(8,128)(2,1)S(1)} %convolution_convert_fusion.1) | copy-start | bytes 393220
  39.0 4.8 %copy-start.14 = (s32[256,4]{0,1:T(4,128)S(1)}, s32[256,4]{0,1:T(4,128)}, u32[]{:S(2)}) copy-start(s32[256,4]{0,1:T(4,128)} %param.28) | copy-start | bytes 12292
  39.7 6.0 %copy-start.13 = (bf16[192,256]{1,0:T(8,128)(2,1)S(1)}, bf16[192,256]{1,0:T(8,128)(2,1)}, u32[]{:S(2)}) copy-start(bf16[192,256]{1,0:T(8,128)(2,1)} %param.21) | copy-start | bytes 294916
  78.1 3.1 %copy-start.11 = (bf16[4,64,2,128]{3,2,1,0:T(2,128)(2,1)S(1)}, bf16[4,64,2,128]{3,2,1,0:T(2,128)(2,1)}, u32[]{:S(2)}) copy-start(bf16[4,64,2,128]{3,2,1,0:T(2,128)(2,1)} %reshape.299) | copy-start | bytes 393220
  86.8 1.6 copy-start.3
  88.4 4.2 %copy-start.5 = (bf16[256,768]{1,0:T(8,128)(2,1)S(1)}, bf16[256,768]{1,0:T(8,128)(2,1)}, u32[]{:S(2)}) copy-start(bf16[256,768]{1,0:T(8,128)(2,1)} %fusion.39) | copy-start | bytes 1179652
  88.4 4.2 %copy-start.15 = (f32[1536]{0:T(1024)S(1)}, f32[1536]{0:T(1024)}, u32[]{:S(2)}) copy-start(f32[1536]{0:T(1024)} %param.24) | copy-start | bytes 18436
  94.9 7.2 %copy-start.6 = (bf16[2,64,2,6,128]{4,1,3,2,0:T(8,128)(2,1)S(1)}, bf16[2,64,2,6,128]{4,1,3,2,0:T(8,128)(2,1)}, u32[]{:S(2)}) copy-start(bf16[2,64,2,6,128]{4,1,3,2,0:T(8,128)(2,1)} %get-tuple-element.26) | copy-start | bytes 1179652
  94.9 40.8 %all-to-all-start = ((bf16[16,2,24,1536]{3,2,1,0:T(8,128)(2,1)}), bf16[16,2,24,1536]{3,2,1,0:T(8,128)(2,1)}, u32[]{:S(2)}, u32[]{:S(2)}) async-start(bf16[16,2,24,1536]{3,2,1,0:T(8,128)(2,1)} %bitcast.12), calls=%async_computation | async-start | bytes 4718592 | tf_op jit(solution)/shard_map/all_to_all | solution.py:164
  106.9 28.8 %copy-start = (f32[128,1536]{1,0:T(8,128)}, f32[128,1536]{1,0:T(8,128)S(1)}, u32[]{:S(2)}) copy-start(f32[128,1536]{1,0:T(8,128)S(1)} %get-tuple-element.40) | copy-start | bytes 2359300
  135.7 38.4 %all-to-all-start.2 = ((bf16[16,2,24,1536]{3,2,1,0:T(8,128)(2,1)}), bf16[16,2,24,1536]{3,2,1,0:T(8,128)(2,1)}, u32[]{:S(2)}, u32[]{:S(2)}) async-start(bf16[16,2,24,1536]{3,2,1,0:T(8,128)(2,1)} %bitcast.22), calls=%async_computation.2 | async-start | bytes 4718592 | tf_op jit(solution)/shard_map/all_to_all | solution.py:164
  158.7 19.4 %copy-start.19 = (s32[4]{0:T(128)S(1)}, s32[4]{0:T(128)}, u32[]{:S(2)}) copy-start(s32[4]{0:T(128)} %param.33) | copy-start | bytes 52
  174.1 34.4 %all-to-all-start.1 = ((bf16[16,2,24,1536]{3,2,1,0:T(8,128)(2,1)}), bf16[16,2,24,1536]{3,2,1,0:T(8,128)(2,1)S(1)}, u32[]{:S(2)}, u32[]{:S(2)}) async-start(bf16[16,2,24,1536]{3,2,1,0:T(8,128)(2,1)} %copy.118), calls=%async_computation.1 | async-start | bytes 4718592 | tf_op jit(solution)/shard_map/all_to_all | solution.py:169
  199.0 14.0 %copy-start.16 = (f32[256,4]{0,1:T(4,128)S(1)}, f32[256,4]{0,1:T(4,128)}, u32[]{:S(2)}) copy-start(f32[256,4]{0,1:T(4,128)} %param.29) | copy-start | bytes 12292
  208.5 35.2 %all-to-all-start.3 = ((bf16[16,2,24,1536]{3,2,1,0:T(8,128)(2,1)}), bf16[16,2,24,1536]{3,2,1,0:T(8,128)(2,1)}, u32[]{:S(2)}, u32[]{:S(2)}) async-start(bf16[16,2,24,1536]{3,2,1,0:T(8,128)(2,1)} %copy.122), calls=%async_computation.3 | async-start | bytes 4718592 | tf_op jit(solution)/shard_map/all_to_all | solution.py:169
  217.3 26.4 %copy-start.7 = (bf16[128,768]{1,0:T(8,128)(2,1)S(1)}, bf16[128,768]{1,0:T(8,128)(2,1)}, u32[]{:S(2)}) copy-start(bf16[128,768]{1,0:T(8,128)(2,1)} %get-tuple-element.28) | copy-start | bytes 589828
  217.3 26.4 %copy-start.8 = (bf16[128,768]{1,0:T(8,128)(2,1)S(1)}, bf16[128,768]{1,0:T(8,128)(2,1)}, u32[]{:S(2)}) copy-start(bf16[128,768]{1,0:T(8,128)(2,1)} %get-tuple-element.43) | copy-start | bytes 589828
  217.5 28.7 %copy-start.1 = (f32[128,1536]{1,0:T(8,128)S(1)}, f32[128,1536]{1,0:T(8,128)}, u32[]{:S(2)}) copy-start(f32[128,1536]{1,0:T(8,128)} %copy-done) | copy-start | bytes 2359300
  (2 other events, 3.2 us)
Sparse Core Ops, SparseCore 0:
  9.7 39.0 all-gather.2
  50.4 34.2 all-gather.4

commit v9 on v7

--- a/solution.py
+++ b/solution.py
@@ -224,16 +224,11 @@
     attn_out = jnp.dot(context_all, w_out_full, preferred_element_type=jnp.float32)
     residual = (tokens.astype(jnp.float32) + attn_out).astype(jnp.bfloat16)
     moe_in = rms_scale(residual, moe_gain)
-    buffers = jnp.einsum(
-        "hts,htd->hsd",
-        place.reshape(chunk_count, BLOCK_ROWS, -1),
-        moe_in.reshape(chunk_count, BLOCK_ROWS, -1),
-        preferred_element_type=jnp.bfloat16,
-    )
     outs = []
     for chunk in range(chunk_count):
         rw = slice(chunk * BLOCK_ROWS, (chunk + 1) * BLOCK_ROWS)
-        mixed = routed_whole(buffers[chunk], weight_hi[rw], weight_lo[rw], w_gate, w_up, w_down)
+        buffer = pack_slots(moe_in[rw], place[rw])
+        mixed = routed_whole(buffer, weight_hi[rw], weight_lo[rw], w_gate, w_up, w_down)
         outs.append(residual[rw].astype(jnp.float32) + mixed)
     layer_out = jnp.concatenate(outs, axis=0).astype(jnp.bfloat16)
     new_entries = compact(key_value_request, closure, tree_depth, accepted)

time: 251 us -> 255 us (1.016)
  blocking collectives: 69.2 us -> 30.6 us
  waiting for transfers between devices: 47.4 us -> 79.2 us
  starting transfers between devices: 12.4 us -> 21.5 us
  matrix products: 61.4 us -> 64.4 us
    all_to_all x1 -> x0, blocking collectives: 38.6 us -> none  [routed_whole(): lax.all_to_all(reshaped_rows, 'exp', split_axis=0, concat_axis=0, tiled=T...]
    all_to_all x1 -> x2, waiting for transfers between devices: 12.2 us -> 44 us  [routed_whole(): lax.all_to_all(reshaped_rows, 'exp', split_axis=0, concat_axis=0, tiled=T...]
    all_to_all x1 -> x2, starting transfers between devices: 3.95 us -> 13 us  [routed_whole(): lax.all_to_all(reshaped_rows, 'exp', split_axis=0, concat_axis=0, tiled=T...]
    dot_general x1 -> x2, matrix products: 1.43 us -> 4.46 us  [pack_slots(): jnp.einsum('ts,td->sd', place, token_rows, preferred_element_type=jnp.bfl...]
  transfers between devices with their start and end apart: 5 -> 6, of which waited for: 3 -> 4; matrix products, arithmetic and copies ran while one was open for 37% -> 37% of each run, Pallas kernels for 0% -> 0%
where the time goes in v9:
time: 255 us; the launch traced here: 254 us
  waiting for transfers between devices  79.2 us (31%)
  matrix products  64.4 us (25%)
  local copies, waits for them, and re-layouts  32.1 us (13%)
  blocking collectives  30.6 us (12%)
  starting transfers between devices  21.5 us (8%)
  between operations  14.5 us (6%)
  other arithmetic  11.6 us (5%)
    all_to_all x2, waiting for transfers between devices, routed_whole(): lax.all_to_all(reshaped_rows, 'exp', split_axis=0, concat_axis=0, tiled=T...  44 us
    all_to_all x2, waiting for transfers between devices, routed_whole(): lax.all_to_all(produced, 'exp', split_axis=0, concat_axis=0, tiled=True)  33.8 us
    dot_general x2, matrix products, expert_products(): jnp.einsum('pekf,efd->pekd', hidden, w_down, preferred_element_type=jnp.f...  20.8 us
    all_gather x1, blocking collectives, local(): lax.all_gather(value_projection, 'req', axis=0, tiled=True)  16.9 us
    all_gather x1, blocking collectives, local(): lax.all_gather(key_projection, 'req', axis=0, tiled=True)  13.6 us
    dot_general x2, matrix products, expert_products(): jnp.einsum('pekd,edf->pekf', received, w_up, preferred_element_type=jnp.f...  13.1 us
    all_to_all x2, starting transfers between devices, routed_whole(): lax.all_to_all(reshaped_rows, 'exp', split_axis=0, concat_axis=0, tiled=T...  13 us
    unnamed x35, local copies, waits for them, and re-layouts  9.64 us
  transfers between devices with their start and end apart: 6, of which 4 were waited for; matrix products, arithmetic and copies ran while one was open for 37% of the time, Pallas kernels for 0%

profile of v9, /device:TPU:0, one launch (start us, length us, event | category | flops | bytes accessed | tf_op | source)
XLA Modules:
  0.0 254.1 jit_solution(12402007342184642751)
XLA Ops:
  10.7 4.6 %fusion.118 = (bf16[4,1024,256]{2,1,0:T(8,128)(2,1)}, bf16[4,1024,256]{2,1,0:T(8,128)(2,1)}) fusion(bf16[4,1024,512]{2,1,0:T(8,128)(2,1)} %param.30), kind=kLoop, calls=%fused_computation.140 | loop fusion | bytes 8388608 | tf_op jit(solution)/shard_map/vmap()/slice | solution.py:66
  15.3 16.9 %all_gather.14 = bf16[1536,256]{1,0:T(8,128)(2,1)} all-gather(bf16[192,256]{1,0:T(8,128)(2,1)S(1)} %copy-done.8), channel_id=1, replica_groups=mesh['req'=8,'exp'=16] {'req'}, dimensions={0}, use_global_device_ids=true | all-gather | bytes 884736 | tf_op jit(solution)/shard_map/all_gather | solution.py:208
  32.7 3.0 %copy.141 = bf16[4,1024,256]{1,2,0:T(8,128)(2,1)S(1)} copy(bf16[4,1024,256]{2,1,0:T(8,128)(2,1)} %get-tuple-element.22) | data formatting | bytes 4194304
  38.1 4.1 %copy.142 = bf16[4,1024,256]{1,2,0:T(8,128)(2,1)} copy(bf16[4,1024,256]{2,1,0:T(8,128)(2,1)} %get-tuple-element.21) | data formatting | bytes 4194304
  44.0 13.6 %all_gather.13 = bf16[1536,256]{1,0:T(8,128)(2,1)S(1)} all-gather(bf16[192,256]{1,0:T(8,128)(2,1)S(1)} %copy-done.9), channel_id=1, replica_groups=mesh['req'=8,'exp'=16] {'req'}, dimensions={0}, use_global_device_ids=true | all-gather | bytes 884736 | tf_op jit(solution)/shard_map/all_gather | solution.py:203
  58.2 4.1 %fusion.116 = f32[256,1536]{1,0:T(8,128)S(1)} fusion(bf16[1536,1536]{1,0:T(8,128)(2,1)} %all-gather.3.cloned.1.call-done, bf16[256,1536]{1,0:T(8,128)(2,1)S(1)} %copy-done.5, f32[1536]{0:T(1024)S(1)} %copy-done.14, f32[256]{0:T(256)S(1)} %add_rsqrt_fusion.1), kind=kOutput, calls=%fused_computation.139 | convolution fusion | flops 1209532416 | bytes 7085056 | tf_op jit(solution)/shard_map/dot_general | solution.py:196
  76.1 3.1 %fusion.1 = f32[4,2,6,64]{3,2,1,0:T(8,128)S(1)} fusion(f32[4,2,64,6,1024]{4,2,3,1,0:T(8,128)S(1)} %get-tuple-element.36, f32[4,2,6,64]{3,2,1,0:T(8,128)S(1)} %max.25, pred[4,1024]{1,0:T(4,128)(4,1)S(1)} %iota_compare_fusion.6), kind=kLoop, calls=%fused_computation.7 | loop fusion | flops 12579840 | bytes 12611584 | tf_op jit(solution)/shard_map/vmap()/reduce_sum | solution.py:91
  80.8 3.9 %fusion.40 = bf16[4,64,2,6,128]{4,1,3,2,0:T(8,128)(2,1)S(1)} fusion(f32[4,2,128,6,64]{2,4,3,1,0:T(8,128)S(1)} %fusion.74, bf16[4,1024,2,128,1]{1,3,4,2,0:T(8,128)(2,1)S(1)} %bitcast.125, f32[4,2,64,6,1024]{4,2,3,1,0:T(8,128)S(1)} %get-tuple-element.36, f32[4,2,6,64]{3,2,1,0:T(8,128)S(1)} %add.97, f32[4,2,6,64]{3,2,1,0:T(8,128)S(1)} %max.25, ...), kind=kOutput, calls=%fused_computation.50 | convolution fusion | flops 821821440 | bytes 17068032 | tf_op jit(solution)/shard_map/vmap(gsij,jgd->igsd)/dot_general | solution.py:96
  86.2 4.1 %fusion.33 = (f32[256]{0:T(256)S(1)}, bf16[256,1536]{1,0:T(8,128)(2,1)S(1)}) fusion(bf16[256,1536]{1,0:T(8,128)(2,1)S(1)} %convert_element_type.137, bf16[1536,1536]{0,1:T(8,128)(2,1)} %all-gather.5.cloned.1.call-done, bf16[256,1536]{1,0:T(8,128)(2,1)} %param.18), kind=kOutput, calls=%fused_computation.42 | convolution fusion | flops 1210318592 | bytes 7078912 | tf_op jit(solution)/shard_map/dot_general | solution.py:224
  92.9 7.2 %all-to-all-start.2 = ((bf16[16,2,24,1536]{3,2,1,0:T(8,128)(2,1)}), bf16[16,2,24,1536]{3,2,1,0:T(8,128)(2,1)}, u32[]{:S(2)}, u32[]{:S(2)}) async-start(bf16[16,2,24,1536]{3,2,1,0:T(8,128)(2,1)} %bitcast.22), calls=%async_computation.2 | async-start | bytes 4718592 | tf_op jit(solution)/shard_map/all_to_all | solution.py:164
  102.2 31.5 %all-to-all-done.2 = bf16[16,2,24,1536]{3,2,1,0:T(8,128)(2,1)} async-done(((bf16[16,2,24,1536]{3,2,1,0:T(8,128)(2,1)}), bf16[16,2,24,1536]{3,2,1,0:T(8,128)(2,1)}, u32[]{:S(2)}, u32[]{:S(2)}) %all-to-all-start.2) | async-done | bytes 2359328 | tf_op jit(solution)/shard_map/all_to_all | solution.py:164
  133.7 5.9 %all-to-all-start = ((bf16[16,2,24,1536]{3,2,1,0:T(8,128)(2,1)}), bf16[16,2,24,1536]{3,2,1,0:T(8,128)(2,1)S(1)}, u32[]{:S(2)}, u32[]{:S(2)}) async-start(bf16[16,2,24,1536]{3,2,1,0:T(8,128)(2,1)} %bitcast.12), calls=%async_computation | async-start | bytes 4718592 | tf_op jit(solution)/shard_map/all_to_all | solution.py:164
  139.6 6.5 %fusion.7 = f32[2,16,24,768]{3,2,1,0:T(8,128)} fusion(bf16[2,1536,768]{2,1,0:T(8,128)(2,1)} %param.26, bf16[16,2,24,1536]{3,2,1,0:T(8,128)(2,1)} %all-to-all-done.2), kind=kOutput, calls=%fused_computation.13 | convolution fusion | flops 1811939328 | bytes 9437184 | tf_op jit(solution)/shard_map/pekd,edf->pekf/dot_general | solution.py:142
  146.2 10.4 %fusion.22 = bf16[16,2,24,1536]{3,2,0,1:T(8,128)(2,1)} fusion(bf16[2,768,1536]{2,1,0:T(8,128)(2,1)} %param.27, f32[2,16,24,768]{3,2,1,0:T(8,128)} %fusion.7, bf16[2,1536,768]{2,1,0:T(8,128)(2,1)} %param.25, bf16[16,2,24,1536]{3,2,1,0:T(8,128)(2,1)} %all-to-all-done.2), kind=kOutput, calls=%fused_computation.26 | convolution fusion | flops 3626827776 | bytes 16515072 | tf_op jit(solution)/shard_map/pekf,efd->pekd/dot_general | solution.py:144
  156.6 3.4 %copy.118 = bf16[16,2,24,1536]{3,2,1,0:T(8,128)(2,1)} copy(bf16[16,2,24,1536]{3,2,0,1:T(8,128)(2,1)} %fusion.22) | data formatting | bytes 4718592 | tf_op jit(solution)/shard_map/convert_element_type | solution.py:144
  159.9 12.5 %all-to-all-done = bf16[16,2,24,1536]{3,2,1,0:T(8,128)(2,1)S(1)} async-done(((bf16[16,2,24,1536]{3,2,1,0:T(8,128)(2,1)}), bf16[16,2,24,1536]{3,2,1,0:T(8,128)(2,1)S(1)}, u32[]{:S(2)}, u32[]{:S(2)}) %all-to-all-start) | async-done | bytes 2359328 | tf_op jit(solution)/shard_map/all_to_all | solution.py:164
  173.9 3.8 %all-to-all-start.3 = ((bf16[16,2,24,1536]{3,2,1,0:T(8,128)(2,1)}), bf16[16,2,24,1536]{3,2,1,0:T(8,128)(2,1)S(1)}, u32[]{:S(2)}, u32[]{:S(2)}) async-start(bf16[16,2,24,1536]{3,2,1,0:T(8,128)(2,1)} %copy.118), calls=%async_computation.3 | async-start | bytes 4718592 | tf_op jit(solution)/shard_map/all_to_all | solution.py:169
  177.8 6.5 %fusion.9 = f32[2,16,24,768]{3,2,1,0:T(8,128)} fusion(bf16[2,1536,768]{2,1,0:T(8,128)(2,1)} %param.26, bf16[16,2,24,1536]{3,2,1,0:T(8,128)(2,1)} %copy-done.1), kind=kOutput, calls=%fused_computation.15 | convolution fusion | flops 1811939328 | bytes 9437184 | tf_op jit(solution)/shard_map/pekd,edf->pekf/dot_general | solution.py:142
  184.3 10.4 %fusion.25 = bf16[16,2,24,1536]{3,2,0,1:T(8,128)(2,1)} fusion(bf16[2,768,1536]{2,1,0:T(8,128)(2,1)} %param.27, f32[2,16,24,768]{3,2,1,0:T(8,128)} %fusion.9, bf16[2,1536,768]{2,1,0:T(8,128)(2,1)} %param.25, bf16[16,2,24,1536]{3,2,1,0:T(8,128)(2,1)} %copy-done.1), kind=kOutput, calls=%fused_computation.27 | convolution fusion | flops 3626827776 | bytes 16515072 | tf_op jit(solution)/shard_map/pekf,efd->pekd/dot_general | solution.py:144
  194.7 3.4 %copy.115 = bf16[16,2,24,1536]{3,2,1,0:T(8,128)(2,1)} copy(bf16[16,2,24,1536]{3,2,0,1:T(8,128)(2,1)} %fusion.25) | data formatting | bytes 4718592 | tf_op jit(solution)/shard_map/convert_element_type | solution.py:144
  198.1 10.1 %all-to-all-done.3 = bf16[16,2,24,1536]{3,2,1,0:T(8,128)(2,1)S(1)} async-done(((bf16[16,2,24,1536]{3,2,1,0:T(8,128)(2,1)}), bf16[16,2,24,1536]{3,2,1,0:T(8,128)(2,1)S(1)}, u32[]{:S(2)}, u32[]{:S(2)}) %all-to-all-start.3) | async-done | bytes 2359328 | tf_op jit(solution)/shard_map/all_to_all | solution.py:169
  208.2 4.5 %all-to-all-start.1 = ((bf16[16,2,24,1536]{3,2,1,0:T(8,128)(2,1)}), bf16[16,2,24,1536]{3,2,1,0:T(8,128)(2,1)}, u32[]{:S(2)}, u32[]{:S(2)}) async-start(bf16[16,2,24,1536]{3,2,1,0:T(8,128)(2,1)} %copy.115), calls=%async_computation.1 | async-start | bytes 4718592 | tf_op jit(solution)/shard_map/all_to_all | solution.py:169
  216.8 3.0 %fusion.83 = f32[256,1536]{1,0:T(8,128)} fusion(bf16[768,1536]{1,0:T(8,128)(2,1)S(1)} %bitcast.120, bf16[128,768]{1,0:T(8,128)(2,1)} %get-tuple-element.41, bf16[128,768]{1,0:T(8,128)(2,1)} %get-tuple-element.28), kind=kOutput, calls=%fused_computation.81 | convolution fusion | flops 604766208 | bytes 4325376 | tf_op jit(solution)/shard_map/dot_general | solution.py:154
  219.7 23.6 %all-to-all-done.1 = bf16[16,2,24,1536]{3,2,1,0:T(8,128)(2,1)} async-done(((bf16[16,2,24,1536]{3,2,1,0:T(8,128)(2,1)}), bf16[16,2,24,1536]{3,2,1,0:T(8,128)(2,1)}, u32[]{:S(2)}, u32[]{:S(2)}) %all-to-all-start.1) | async-done | bytes 2359328 | tf_op jit(solution)/shard_map/all_to_all | solution.py:169
  (108 shorter events, 40.3 us)
Async XLA Ops:
  7.2 51.0 %all-gather.3.cloned.1.call-start = ((), (), s32[]{:S(2)}) async-start(), calls=%async_computation.4 | async-start | bytes 5308416 | tf_op jit(solution)/shard_map/all_gather | solution.py:198
  7.9 78.3 %all-gather.5.cloned.1.call-start = ((), (), s32[]{:S(2)}) async-start(), calls=%async_computation.5 | async-start | bytes 5308416 | tf_op jit(solution)/shard_map/all_gather | solution.py:218
  10.7 4.6 %copy-start.8 = (bf16[192,256]{1,0:T(8,128)(2,1)S(1)}, bf16[192,256]{1,0:T(8,128)(2,1)}, u32[]{:S(2)}) copy-start(bf16[192,256]{1,0:T(8,128)(2,1)} %param.22) | copy-start | bytes 294916
  10.7 21.5 %copy-start.13 = (s32[4]{0:T(128)S(1)}, s32[4]{0:T(128)}, u32[]{:S(2)}) copy-start(s32[4]{0:T(128)} %param.31) | copy-start | bytes 52
  10.7 21.6 %copy-start.5 = (bf16[256,1536]{1,0:T(8,128)(2,1)S(1)}, bf16[256,1536]{1,0:T(8,128)(2,1)}, u32[]{:S(2)}) copy-start(bf16[256,1536]{1,0:T(8,128)(2,1)} %param.18) | copy-start | bytes 2359300
  32.3 3.5 %copy-start.14 = (f32[1536]{0:T(1024)S(1)}, f32[1536]{0:T(1024)}, u32[]{:S(2)}) copy-start(f32[1536]{0:T(1024)} %param.19) | copy-start | bytes 18436
  37.3 5.1 %copy-start.6 = (bf16[256,256]{1,0:T(8,128)(2,1)}, bf16[256,256]{1,0:T(8,128)(2,1)S(1)}, u32[]{:S(2)}) copy-start(bf16[256,256]{1,0:T(8,128)(2,1)S(1)} %convolution_convert_fusion.1) | copy-start | bytes 393220
  37.3 4.8 %copy-start.10 = (s32[256,4]{0,1:T(4,128)S(1)}, s32[256,4]{0,1:T(4,128)}, u32[]{:S(2)}) copy-start(s32[256,4]{0,1:T(4,128)} %param.28) | copy-start | bytes 12292
  38.1 6.0 %copy-start.9 = (bf16[192,256]{1,0:T(8,128)(2,1)S(1)}, bf16[192,256]{1,0:T(8,128)(2,1)}, u32[]{:S(2)}) copy-start(bf16[192,256]{1,0:T(8,128)(2,1)} %param.21) | copy-start | bytes 294916
  76.1 3.1 %copy-start.7 = (bf16[4,64,2,128]{3,2,1,0:T(2,128)(2,1)S(1)}, bf16[4,64,2,128]{3,2,1,0:T(2,128)(2,1)}, u32[]{:S(2)}) copy-start(bf16[4,64,2,128]{3,2,1,0:T(2,128)(2,1)} %reshape.286) | copy-start | bytes 393220
  79.2 1.6 copy-start.2
  86.2 4.2 %copy-start.11 = (f32[1536]{0:T(1024)S(1)}, f32[1536]{0:T(1024)}, u32[]{:S(2)}) copy-start(f32[1536]{0:T(1024)} %param.24) | copy-start | bytes 18436
  86.2 4.4 %copy-start.3 = (bf16[256,768]{1,0:T(8,128)(2,1)S(1)}, bf16[256,768]{1,0:T(8,128)(2,1)}, u32[]{:S(2)}) copy-start(bf16[256,768]{1,0:T(8,128)(2,1)} %fusion.39) | copy-start | bytes 1179652
  92.9 40.9 %all-to-all-start.2 = ((bf16[16,2,24,1536]{3,2,1,0:T(8,128)(2,1)}), bf16[16,2,24,1536]{3,2,1,0:T(8,128)(2,1)}, u32[]{:S(2)}, u32[]{:S(2)}) async-start(bf16[16,2,24,1536]{3,2,1,0:T(8,128)(2,1)} %bitcast.22), calls=%async_computation.2 | async-start | bytes 4718592 | tf_op jit(solution)/shard_map/all_to_all | solution.py:164
  133.7 38.8 %all-to-all-start = ((bf16[16,2,24,1536]{3,2,1,0:T(8,128)(2,1)}), bf16[16,2,24,1536]{3,2,1,0:T(8,128)(2,1)S(1)}, u32[]{:S(2)}, u32[]{:S(2)}) async-start(bf16[16,2,24,1536]{3,2,1,0:T(8,128)(2,1)} %bitcast.12), calls=%async_computation | async-start | bytes 4718592 | tf_op jit(solution)/shard_map/all_to_all | solution.py:164
  172.5 1.4 copy-start.1
  173.9 34.3 %all-to-all-start.3 = ((bf16[16,2,24,1536]{3,2,1,0:T(8,128)(2,1)}), bf16[16,2,24,1536]{3,2,1,0:T(8,128)(2,1)S(1)}, u32[]{:S(2)}, u32[]{:S(2)}) async-start(bf16[16,2,24,1536]{3,2,1,0:T(8,128)(2,1)} %copy.118), calls=%async_computation.3 | async-start | bytes 4718592 | tf_op jit(solution)/shard_map/all_to_all | solution.py:169
  198.1 14.7 %copy-start.15 = (s32[4]{0:T(128)S(1)}, s32[4]{0:T(128)}, u32[]{:S(2)}) copy-start(s32[4]{0:T(128)} %param.33) | copy-start | bytes 52
  198.1 15.3 %copy-start.12 = (f32[256,4]{0,1:T(4,128)S(1)}, f32[256,4]{0,1:T(4,128)}, u32[]{:S(2)}) copy-start(f32[256,4]{0,1:T(4,128)} %param.29) | copy-start | bytes 12292
  208.2 35.2 %all-to-all-start.1 = ((bf16[16,2,24,1536]{3,2,1,0:T(8,128)(2,1)}), bf16[16,2,24,1536]{3,2,1,0:T(8,128)(2,1)}, u32[]{:S(2)}, u32[]{:S(2)}) async-start(bf16[16,2,24,1536]{3,2,1,0:T(8,128)(2,1)} %copy.115), calls=%async_computation.1 | async-start | bytes 4718592 | tf_op jit(solution)/shard_map/all_to_all | solution.py:169
  214.9 28.5 %copy-start.4 = (bf16[128,768]{1,0:T(8,128)(2,1)S(1)}, bf16[128,768]{1,0:T(8,128)(2,1)}, u32[]{:S(2)}) copy-start(bf16[128,768]{1,0:T(8,128)(2,1)} %get-tuple-element.27) | copy-start | bytes 589828
  219.7 26.2 %copy-start = (f32[256,1536]{1,0:T(8,128)S(1)}, f32[256,1536]{1,0:T(8,128)}, u32[]{:S(2)}) copy-start(f32[256,1536]{1,0:T(8,128)} %fusion.83) | copy-start | bytes 4718596
Sparse Core Ops, SparseCore 0:
  9.7 38.5 all-gather.2
  49.9 34.2 all-gather.4
